TPU v7x, 128 devices: a whole 4x4x4 slice. The times are simulated.
128 devices in a mesh: rep: 4 (over z), shard: 32 (over x, y, core).
Axes of the slice: x: 4, y: 4, z: 4, core: 2. Of those that a mesh axis runs over, the one named last changes fastest.
Arguments:
- trained_sq: float32 [4, 4, 768, 768], P('rep', None, 'shard'), may hold values from -6 to 6
- trained_up: float32 [4, 768, 3072], P('rep', 'shard'), may hold values from -6 to 6
- trained_down: float32 [4, 3072, 768], P('rep', 'shard'), may hold values from -6 to 6
- trained_ln: float32 [4, 4, 768], P('rep', None, 'shard'), may hold values from -6 to 6
- start_sq: float32 [4, 768, 768], P(None, 'shard'), may hold values from -6 to 6
- start_up: float32 [768, 3072], P('shard'), may hold values from -6 to 6
- start_down: float32 [3072, 768], P('shard'), may hold values from -6 to 6
- start_ln: float32 [4, 768], P(None, 'shard'), may hold values from -6 to 6
- resid_sq: float32 [4, 4, 768, 768], P('rep', None, 'shard'), may hold values from -4 to 4
- resid_up: float32 [4, 768, 3072], P('rep', 'shard'), may hold values from -4 to 4
- resid_down: float32 [4, 3072, 768], P('rep', 'shard'), may hold values from -4 to 4
- mom_sq: float32 [4, 768, 768], P(None, 'shard'), may hold values from -3 to 3
- mom_up: float32 [768, 3072], P('shard'), may hold values from -3 to 3
- mom_down: float32 [3072, 768], P('shard'), may hold values from -3 to 3
- mom_ln: float32 [4, 768], P(None, 'shard'), may hold values from -3 to 3
- basis_sq: float32 [4, 768, 64], replicated, may hold values from -0.21875 to 0.21875
- basis_up: float32 [3072, 64], replicated, may hold values from -0.109375 to 0.109375
- basis_down: float32 [768, 64], replicated, may hold values from -0.21875 to 0.21875
Outputs:
- new_resid_sq: float32 [4, 4, 768, 768], P('rep', None, 'shard')
- new_resid_up: float32 [4, 768, 3072], P('rep', 'shard')
- new_resid_down: float32 [4, 3072, 768], P('rep', 'shard')
- new_mom_sq: float32 [4, 768, 768], P(None, 'shard')
- new_mom_up: float32 [768, 3072], P('shard')
- new_mom_down: float32 [3072, 768], P('shard')
- new_mom_ln: float32 [4, 768], P(None, 'shard')
- weights_sq: bfloat16 [4, 768, 768], replicated
- weights_up: bfloat16 [768, 3072], replicated
- weights_down: bfloat16 [3072, 768], replicated
- weights_ln: bfloat16 [4, 768], replicated
All inputs are finite; a program needn't handle non-finite values.
Results may differ from a plain program's by a relative error of at most 0.001.
Values may be sent and summed in bfloat16 or wider, within the bound.
No kernel may reach another device: no remote copies, remote signals or barrier semaphores. Data moves between devices by JAX's collectives and lax.ppermute only.
A program may use at most 128 MiB of HBM per device.

v0:
```python
import jax
import jax.numpy as jnp
from jax import lax
from jax.sharding import PartitionSpec as P

moment_coef = 0.9
outer_rate = 0.7


def advance(start, moment, outer):
    new_moment = moment_coef * moment + outer
    weights = (start - outer_rate * (outer + moment_coef * new_moment)).astype(jnp.bfloat16)
    return (new_moment, weights)


def on_device(
    trained_sq,
    trained_up,
    trained_down,
    trained_ln,
    start_sq,
    start_up,
    start_down,
    start_ln,
    resid_sq,
    resid_up,
    resid_down,
    mom_sq,
    mom_up,
    mom_down,
    mom_ln,
    basis_sq,
    basis_up,
    basis_down,
):
    highest = lax.Precision.HIGHEST
    groups = lax.axis_size("rep")
    delta_sq = start_sq - trained_sq[0] + resid_sq[0]
    factor_sq = jnp.einsum("mrd,mdk->mrk", delta_sq, basis_sq, precision=highest)
    new_resid_sq = delta_sq - jnp.einsum("mrk,mdk->mrd", factor_sq, basis_sq, precision=highest)
    delta_up = start_up - trained_up[0] + resid_up[0]
    factor_up = jnp.dot(delta_up, basis_up, precision=highest, preferred_element_type=jnp.float32)
    new_resid_up = delta_up - jnp.einsum("rk,fk->rf", factor_up, basis_up, precision=highest)
    delta_down = start_down - trained_down[0] + resid_down[0]
    factor_down = jnp.dot(
        delta_down, basis_down, precision=highest, preferred_element_type=jnp.float32
    )
    new_resid_down = delta_down - jnp.einsum(
        "rk,dk->rd", factor_down, basis_down, precision=highest
    )
    norm_delta = start_ln - trained_ln[0]
    summed = lax.psum((factor_sq, factor_up, factor_down, norm_delta), "rep")
    mean_sq = summed[0] / groups
    mean_up = summed[1] / groups
    mean_down = summed[2] / groups
    mean_ln = summed[3] / groups
    new_mom_ln, norm_weights = advance(start_ln, mom_ln, mean_ln)
    outer_sq = jnp.einsum("mrk,mdk->mrd", mean_sq, basis_sq, precision=highest)
    outer_up = jnp.einsum("rk,fk->rf", mean_up, basis_up, precision=highest)
    outer_down = jnp.einsum("rk,dk->rd", mean_down, basis_down, precision=highest)
    new_mom_sq, owned_sq = advance(start_sq, mom_sq, outer_sq)
    new_mom_up, owned_up = advance(start_up, mom_up, outer_up)
    new_mom_down, owned_down = advance(start_down, mom_down, outer_down)
    weights_sq, weights_up, weights_down, weights_ln = (
        lax.all_gather(owned_sq, "shard", axis=1, tiled=True),
        lax.all_gather(owned_up, "shard", axis=0, tiled=True),
        lax.all_gather(owned_down, "shard", axis=0, tiled=True),
        lax.all_gather(norm_weights, "shard", axis=1, tiled=True),
    )
    return (
        new_resid_sq[None],
        new_resid_up[None],
        new_resid_down[None],
        new_mom_sq,
        new_mom_up,
        new_mom_down,
        new_mom_ln,
        weights_sq,
        weights_up,
        weights_down,
        weights_ln,
    )


def solution(mesh):
    placed = (
        P("rep", None, "shard", None),
        P("rep", "shard", None),
        P("rep", "shard", None),
        P("rep", None, "shard"),
        P(None, "shard", None),
        P("shard", None),
        P("shard", None),
        P(None, "shard"),
        P("rep", None, "shard", None),
        P("rep", "shard", None),
        P("rep", "shard", None),
        P(None, "shard", None),
        P("shard", None),
        P("shard", None),
        P(None, "shard"),
        P(),
        P(),
        P(),
    )
    return jax.shard_map(
        on_device,
        mesh=mesh,
        in_specs=placed,
        out_specs=(
            P("rep", None, "shard", None),
            P("rep", "shard", None),
            P("rep", "shard", None),
            P(None, "shard", None),
            P("shard", None),
            P("shard", None),
            P(None, "shard"),
            P(),
            P(),
            P(),
            P(),
        ),
        check_vma=False,
    )
```

profile of v0, /device:TPU:1, one launch (start us, length us, event | category | flops | bytes accessed | tf_op | source)
XLA Modules:
  0.0 201.4 jit_solution(2891028444277751555)
XLA Ops:
  7.2 0.0 copy-start
  7.2 0.0 copy-start.5
  7.2 0.0 copy-start.4
  7.2 0.0 copy-start.6
  7.2 0.0 copy-start.3
  7.2 0.0 copy-start.1
  7.3 0.0 all-gather.5.cloned.1.call-start
  7.3 0.9 bitcast_subtract_fusion.3
  8.2 0.5 copy-done
  8.7 0.0 copy-start.9
  8.7 2.6 %fusion.16 = f32[4,24,64]{2,1,0:T(8,128)} fusion(f32[4,768,64]{1,2,0:T(8,128)S(1)} %copy-done, f32[1,4,24,768]{3,2,1,0:T(8,128)} %param.26, f32[4,24,768]{2,1,0:T(8,128)} %param.22, f32[1,4,24,768]{3,2,1,0:T(8,128)} %param.18), kind=kOutput, calls=%fused_computation.34 | convolution fusion | flops 56770560 | bytes 1695744 | tf_op jit(solution)/shard_map/mrd,mdk->mrk/dot_general | solution.py:39
  11.2 0.0 copy-start.7
  11.2 2.3 %fusion.18 = f32[96,64]{0,1:T(8,128)} fusion(f32[768,64]{0,1:T(8,128)} %param.35, f32[1,96,768]{2,1,0:T(8,128)} %param.28, f32[96,768]{1,0:T(8,128)} %param.24, f32[1,96,768]{2,1,0:T(8,128)} %param.20), kind=kOutput, calls=%fused_computation.36 | convolution fusion | flops 56770560 | bytes 1105920 | tf_op jit(solution)/shard_map/dot_general | solution.py:45
  13.5 2.1 %fusion.17 = f32[24,64]{1,0:T(8,128)S(1)} fusion(f32[3072,64]{0,1:T(8,128)} %param.34, f32[1,24,3072]{2,1,0:T(8,128)} %param.27, f32[24,3072]{1,0:T(8,128)} %param.23, f32[1,24,3072]{2,1,0:T(8,128)} %param.19), kind=kOutput, calls=%fused_computation.35 | convolution fusion | flops 56770560 | bytes 1677312 | tf_op jit(solution)/shard_map/dot_general | solution.py:42
  15.6 17.3 %all-reduce = (f32[4,24,64]{2,1,0:T(8,128)}, f32[24,64]{1,0:T(8,128)}, f32[96,64]{0,1:T(8,128)}, f32[4,24]{1,0:T(4,128)}) all-reduce(f32[4,24,64]{2,1,0:T(8,128)} %fusion.16, f32[24,64]{1,0:T(8,128)S(1)} %fusion.17, f32[96,64]{0,1:T(8,128)} %fusion.18, f32[4,24]{1,0:T(4,128)S(1)} %bitcast_subtract_fusion.3), channel_id=1, replica_groups=mesh['rep'=4,'shard'=32] {'rep'}, use_global_device_ids=true, to_apply=%region_0.0 | all-reduce | flops 13920 | bytes 111360 | tf_op jit(solution)/shard_map/psum | solution.py:52
  33.0 0.0 copy-done.5
  33.0 2.3 %subtract_convert_fusion.2 = (bf16[4,24,768]{2,1,0:T(8,128)(2,1)}, f32[4,24,768]{2,1,0:T(8,128)}) fusion(f32[4,24,768]{2,1,0:T(8,128)S(1)} %copy-done.5, f32[4,24,768]{2,1,0:T(8,128)} %param.29, f32[4,768,64]{1,2,0:T(8,128)S(1)} %copy-done, f32[4,24,64]{2,1,0:T(8,128)} %get-tuple-element.11), kind=kOutput, calls=%fused_computation.14 | convolution fusion | flops 57145344 | bytes 1843200 | tf_op jit(solution)/shard_map/mrk,mdk->mrd/dot_general | solution.py:58
  35.3 0.0 all-gather.5.cloned.1.call-update
  35.3 0.0 all-gather.7.cloned.1.call-start
  35.3 0.0 copy-done.3
  35.3 0.0 copy-done.1
  35.4 2.3 %subtract_convert_fusion.1 = (bf16[24,3072]{1,0:T(8,128)(2,1)}, f32[24,3072]{1,0:T(8,128)}) fusion(f32[24,3072]{1,0:T(8,128)S(1)} %copy-done.3, f32[24,3072]{1,0:T(8,128)} %param.30, f32[3072,64]{0,1:T(8,128)S(1)} %copy-done.1, f32[24,64]{1,0:T(8,128)} %get-tuple-element.12), kind=kOutput, calls=%fused_computation.13 | convolution fusion | flops 57140736 | bytes 1824768 | tf_op jit(solution)/shard_map/rk,fk->rf/dot_general | solution.py:59
  37.6 0.0 all-gather.7.cloned.1.call-update
  37.6 0.0 all-gather.9.cloned.1.call-start
  37.7 0.0 copy-done.4
  37.7 0.0 copy-done.6
  37.7 2.2 %subtract_convert_fusion = (bf16[96,768]{1,0:T(8,128)(2,1)}, f32[96,768]{1,0:T(8,128)}) fusion(f32[96,768]{1,0:T(8,128)S(1)} %copy-done.4, f32[96,768]{1,0:T(8,128)} %param.31, f32[768,64]{0,1:T(8,128)S(1)} %copy-done.6, f32[96,64]{0,1:T(8,128)} %get-tuple-element.13), kind=kOutput, calls=%fused_computation.12 | convolution fusion | flops 57145344 | bytes 1253376 | tf_op jit(solution)/shard_map/rk,dk->rd/dot_general | solution.py:60
  39.9 0.0 all-gather.9.cloned.1.call-update
  40.0 0.0 copy-done.10
  40.0 1.3 fusion.12
  41.3 28.7 %all-gather = bf16[32,24,4]{1,2,0:T(4,128)(2,1)S(1)} all-gather(bf16[1,24,4]{1,2,0:T(4,128)(2,1)S(1)} %get-tuple-element.15), channel_id=1, replica_groups=mesh['rep'=4,'shard'=32] {'shard'}, dimensions={0}, use_global_device_ids=true | all-gather | bytes 6336 | tf_op jit(solution)/shard_map/all_gather | solution.py:68
  69.9 0.6 copy.30
  70.6 1.5 reshape.23
  72.0 0.0 copy-done.9
  72.0 2.1 %fusion.1 = f32[1,96,768]{2,1,0:T(8,128)} fusion(f32[96,64]{0,1:T(8,128)} %fusion.18, f32[768,64]{0,1:T(8,128)S(1)} %copy-done.6, f32[1,96,768]{2,1,0:T(8,128)S(1)} %copy-done.9, f32[96,768]{1,0:T(8,128)S(1)} %copy-done.4, f32[1,96,768]{2,1,0:T(8,128)} %param.20), kind=kOutput, calls=%fused_computation.3 | convolution fusion | flops 56844288 | bytes 1400832 | tf_op jit(solution)/shard_map/rk,dk->rd/dot_general | solution.py:48
  74.2 0.0 copy-done.7
  74.2 0.0 copy-done.8
  74.2 1.2 fusion
  75.4 2.3 %fusion.2 = f32[1,4,24,768]{3,2,1,0:T(8,128)} fusion(f32[4,24,64]{2,1,0:T(8,128)} %fusion.16, f32[4,768,64]{1,2,0:T(8,128)S(1)} %copy-done, f32[1,4,24,768]{3,2,1,0:T(8,128)} %param.26, f32[4,24,768]{2,1,0:T(8,128)S(1)} %copy-done.5, f32[1,4,24,768]{3,2,1,0:T(8,128)} %param.18), kind=kOutput, calls=%fused_computation.5 | convolution fusion | flops 56844288 | bytes 1990656 | tf_op jit(solution)/shard_map/mrk,mdk->mrd/dot_general | solution.py:40
  77.7 8.5 %all-gather.5.cloned.1.call-done = bf16[4,768,768]{2,1,0:T(8,128)(2,1)} async-done(((bf16[4,24,768]{2,1,0:T(8,128)(2,1)}), bf16[4,768,768]{2,1,0:T(8,128)(2,1)}) %all-gather.5.cloned.1.call-update) | async-done | bytes 4718608 | tf_op jit(solution)/shard_map/all_gather | solution.py:65
  86.2 49.0 %all-gather.7.cloned.1.call-done = bf16[768,3072]{1,0:T(8,128)(2,1)} async-done(((bf16[24,3072]{1,0:T(8,128)(2,1)}), bf16[768,3072]{1,0:T(8,128)(2,1)}) %all-gather.7.cloned.1.call-update) | async-done | bytes 4718608 | tf_op jit(solution)/shard_map/all_gather | solution.py:66
  135.1 49.0 %all-gather.9.cloned.1.call-done = bf16[3072,768]{1,0:T(8,128)(2,1)} async-done(((bf16[96,768]{1,0:T(8,128)(2,1)}), bf16[3072,768]{1,0:T(8,128)(2,1)}) %all-gather.9.cloned.1.call-update) | async-done | bytes 4718608 | tf_op jit(solution)/shard_map/all_gather | solution.py:67
  184.1 5.2 %copy.34 = bf16[4,768,768]{2,1,0:T(8,128)(2,1)} copy(bf16[4,768,768]{2,1,0:T(8,128)(2,1)} %all-gather.5.cloned.1.call-done) | data formatting | bytes 9437184
  189.3 0.0 copy-done.2
  189.3 2.4 %copy.35 = bf16[768,3072]{1,0:T(8,128)(2,1)} copy(bf16[768,3072]{1,0:T(8,128)(2,1)S(1)} %copy-done.2) | data formatting | bytes 9437184
  191.7 0.5 slice-done
  192.2 0.5 slice-done.1
  192.7 2.2 %copy.36 = bf16[3072,768]{1,0:T(8,128)(2,1)} copy(bf16[3072,768]{1,0:T(8,128)(2,1)S(1)} %bitcast.64) | data formatting | bytes 9437184
  (6 shorter events, 0.0 us)
Async XLA Ops:
  7.2 1.5 copy-start
  7.2 25.8 %copy-start.5 = (f32[4,24,768]{2,1,0:T(8,128)S(1)}, f32[4,24,768]{2,1,0:T(8,128)}, u32[]{:S(2)}) copy-start(f32[4,24,768]{2,1,0:T(8,128)} %param.22) | copy-start | bytes 884740
  7.2 30.5 %copy-start.4 = (f32[96,768]{1,0:T(8,128)S(1)}, f32[96,768]{1,0:T(8,128)}, u32[]{:S(2)}) copy-start(f32[96,768]{1,0:T(8,128)} %param.24) | copy-start | bytes 884740
  7.2 30.5 %copy-start.6 = (f32[768,64]{0,1:T(8,128)S(1)}, f32[768,64]{0,1:T(8,128)}, u32[]{:S(2)}) copy-start(f32[768,64]{0,1:T(8,128)} %param.35) | copy-start | bytes 589828
  7.2 28.1 %copy-start.3 = (f32[24,3072]{1,0:T(8,128)S(1)}, f32[24,3072]{1,0:T(8,128)}, u32[]{:S(2)}) copy-start(f32[24,3072]{1,0:T(8,128)} %param.23) | copy-start | bytes 884740
  7.2 28.1 %copy-start.1 = (f32[3072,64]{0,1:T(8,128)S(1)}, f32[3072,64]{0,1:T(8,128)}, u32[]{:S(2)}) copy-start(f32[3072,64]{0,1:T(8,128)} %param.34) | copy-start | bytes 2359300
  7.3 78.9 %all-gather.5.cloned.1.call-start = ((), (), s32[]{:S(2)}) async-start(), calls=%async_computation | async-start | bytes 4866048 | tf_op jit(solution)/shard_map/all_gather | solution.py:65
  8.7 63.3 %copy-start.9 = (f32[1,96,768]{2,1,0:T(8,128)S(1)}, f32[1,96,768]{2,1,0:T(8,128)}, u32[]{:S(2)}) copy-start(f32[1,96,768]{2,1,0:T(8,128)} %param.28) | copy-start | bytes 884740
  11.2 62.9 %copy-start.7 = (f32[1,24,3072]{2,1,0:T(8,128)S(1)}, f32[1,24,3072]{2,1,0:T(8,128)}, u32[]{:S(2)}) copy-start(f32[1,24,3072]{2,1,0:T(8,128)} %param.27) | copy-start | bytes 884740
  11.2 62.9 %copy-start.8 = (f32[1,24,3072]{2,1,0:T(8,128)S(1)}, f32[1,24,3072]{2,1,0:T(8,128)}, u32[]{:S(2)}) copy-start(f32[1,24,3072]{2,1,0:T(8,128)} %param.19) | copy-start | bytes 884740
  33.0 7.0 %copy-start.10 = (f32[4,24]{1,0:T(4,128)S(1)}, f32[4,24]{1,0:T(4,128)}, u32[]{:S(2)}) copy-start(f32[4,24]{1,0:T(4,128)} %get-tuple-element.14) | copy-start | bytes 1156
  35.3 99.8 %all-gather.7.cloned.1.call-start = ((), (), s32[]{:S(2)}) async-start(), calls=%async_computation.1 | async-start | bytes 4866048 | tf_op jit(solution)/shard_map/all_gather | solution.py:66
  37.6 146.5 %all-gather.9.cloned.1.call-start = ((), (), s32[]{:S(2)}) async-start(), calls=%async_computation.2 | async-start | bytes 4866048 | tf_op jit(solution)/shard_map/all_gather | solution.py:67
  184.1 5.2 %copy-start.2 = (bf16[768,3072]{1,0:T(8,128)(2,1)S(1)}, bf16[768,3072]{1,0:T(8,128)(2,1)}, u32[]{:S(2)}) copy-start(bf16[768,3072]{1,0:T(8,128)(2,1)} %all-gather.7.cloned.1.call-done) | copy-start | bytes 14155780
  184.1 8.0 %slice-start = ((s8[4718592]{0:T(1024)(128)(4,1)}), s8[4194304]{0:T(1024)(128)(4,1)S(1)}, s32[]{:S(2)}) async-start(s8[4718592]{0:T(1024)(128)(4,1)} %bitcast.63), calls=%async_computation.3 | async-start | bytes 8388608
  189.3 3.4 %slice-start.1 = ((s8[4718592]{0:T(1024)(128)(4,1)}), s8[524288]{0:T(1024)(128)(4,1)S(1)}, s32[]{:S(2)}) async-start(s8[4718592]{0:T(1024)(128)(4,1)} %bitcast.63), calls=%async_computation.4 | async-start | bytes 1048576
Sparse Core Ops, SparseCore 0:
  35.4 50.7 all-gather.4
  89.0 46.0 all-gather.6
  137.9 46.1 all-gather.8
where the time goes:
time: 202 us; the launch traced here: 201 us
  waiting for transfers between devices  106 us (52%)
  blocking collectives  46 us (23%)
  matrix products  19.4 us (10%)
  between operations  13.9 us (7%)
  local copies, waits for them, and re-layouts  13.4 us (7%)
  other arithmetic  2.13 us (1%)
    all_gather x1, waiting for transfers between devices, on_device(): lax.all_gather(owned_down, 'shard', axis=0, tiled=True)  49 us
    all_gather x1, waiting for transfers between devices, on_device(): lax.all_gather(owned_up, 'shard', axis=0, tiled=True)  49 us
    all_gather x1, blocking collectives, on_device(): lax.all_gather(norm_weights, 'shard', axis=1, tiled=True)  28.7 us
    psum x1, blocking collectives, on_device(): summed = lax.psum((factor_sq, factor_up, factor_down, norm_delta), 'rep')  17.3 us
    unnamed x30, local copies, waits for them, and re-layouts  12.8 us
    all_gather x1, waiting for transfers between devices, on_device(): lax.all_gather(owned_sq, 'shard', axis=1, tiled=True)  8.47 us
  transfers between devices with their start and end apart: 3, of which 3 were waited for; matrix products, arithmetic and copies ran while one was open for 7% of the time, Pallas kernels for 0%

commit v1 on v0

--- a/solution.py
+++ b/solution.py
@@ -11,6 +11,14 @@
     new_moment = moment_coef * moment + outer
     weights = (start - outer_rate * (outer + moment_coef * new_moment)).astype(jnp.bfloat16)
     return (new_moment, weights)
+
+
+def split_cols(a, width):
+    return a.reshape(a.shape[0], -1, width).transpose(1, 0, 2)
+
+
+def join_cols(a):
+    return a.transpose(1, 0, 2).reshape(a.shape[1], -1)
 
 
 def on_device(
@@ -35,6 +43,8 @@
 ):
     highest = lax.Precision.HIGHEST
     groups = lax.axis_size("rep")
+    square, rows, width = start_sq.shape
+    rank = basis_sq.shape[-1]
     delta_sq = start_sq - trained_sq[0] + resid_sq[0]
     factor_sq = jnp.einsum("mrd,mdk->mrk", delta_sq, basis_sq, precision=highest)
     new_resid_sq = delta_sq - jnp.einsum("mrk,mdk->mrd", factor_sq, basis_sq, precision=highest)
@@ -55,18 +65,40 @@
     mean_down = summed[2] / groups
     mean_ln = summed[3] / groups
     new_mom_ln, norm_weights = advance(start_ln, mom_ln, mean_ln)
-    outer_sq = jnp.einsum("mrk,mdk->mrd", mean_sq, basis_sq, precision=highest)
-    outer_up = jnp.einsum("rk,fk->rf", mean_up, basis_up, precision=highest)
-    outer_down = jnp.einsum("rk,dk->rd", mean_down, basis_down, precision=highest)
-    new_mom_sq, owned_sq = advance(start_sq, mom_sq, outer_sq)
-    new_mom_up, owned_up = advance(start_up, mom_up, outer_up)
-    new_mom_down, owned_down = advance(start_down, mom_down, outer_down)
-    weights_sq, weights_up, weights_down, weights_ln = (
-        lax.all_gather(owned_sq, "shard", axis=1, tiled=True),
-        lax.all_gather(owned_up, "shard", axis=0, tiled=True),
-        lax.all_gather(owned_down, "shard", axis=0, tiled=True),
-        lax.all_gather(norm_weights, "shard", axis=1, tiled=True),
+    blocks_up = start_up.shape[1] // width
+    blocks_down = start_down.shape[0] // rows
+    start_all = jnp.concatenate(
+        [start_sq, split_cols(start_up, width), start_down.reshape(blocks_down, rows, width)]
     )
+    mom_all = jnp.concatenate(
+        [mom_sq, split_cols(mom_up, width), mom_down.reshape(blocks_down, rows, width)]
+    )
+    mean_all = jnp.concatenate(
+        [
+            mean_sq,
+            jnp.broadcast_to(mean_up[None], (blocks_up, rows, rank)),
+            mean_down.reshape(blocks_down, rows, rank),
+        ]
+    )
+    basis_all = jnp.concatenate(
+        [
+            basis_sq,
+            basis_up.reshape(blocks_up, width, rank),
+            jnp.broadcast_to(basis_down[None], (blocks_down, width, rank)),
+        ]
+    )
+    outer_all = jnp.einsum("brk,bdk->brd", mean_all, basis_all, precision=highest)
+    new_mom_all, owned_all = advance(start_all, mom_all, outer_all)
+    new_mom_sq = new_mom_all[:square]
+    new_mom_up = join_cols(new_mom_all[square : square + blocks_up])
+    new_mom_down = new_mom_all[square + blocks_up :].reshape(-1, width)
+    gathered = lax.all_gather(owned_all, "shard", axis=1, tiled=True)
+    shards = lax.axis_size("shard")
+    weights_sq = gathered[:square]
+    weights_up = join_cols(gathered[square : square + blocks_up])
+    down = gathered[square + blocks_up :].reshape(blocks_down, shards, rows, width)
+    weights_down = down.transpose(1, 0, 2, 3).reshape(-1, width)
+    weights_ln = lax.all_gather(norm_weights, "shard", axis=1, tiled=True)
     return (
         new_resid_sq[None],
         new_resid_up[None],

time: 202 us -> 143 us (0.71)
  waiting for transfers between devices: 106 us -> 30.3 us
  local copies, waits for them, and re-layouts: 13.4 us -> 35.2 us
  matrix products: 19.4 us -> 15.1 us
    all_gather x3 -> x1, waiting for transfers between devices: 106 us -> 30.2 us  [on_device(): gathered = lax.all_gather(owned_all, 'shard', axis=1, tiled=True)]
    slice x0 -> x2, local copies, waits for them, and re-layouts: none -> 13 us  [the longest x1 11 us: on_device(): gathered[square + blocks_up:].reshape(blocks_down, shards, rows, width)]
    transpose x0 -> x3, local copies, waits for them, and re-layouts: none -> 11.8 us  [the longest x1 6.68 us: join_cols(): return a.transpose(1, 0, 2).reshape(a.shape[1], -1)]
    unnamed x30 -> x28, local copies, waits for them, and re-layouts: 12.8 us -> 8.15 us
    dot_general x3 -> x1, matrix products: 6.78 us -> 3.68 us  [on_device(): jnp.einsum('brk,bdk->brd', mean_all, basis_all, precision=highest)]
  transfers between devices with their start and end apart: 3 -> 1, of which waited for: 3 -> 1; matrix products, arithmetic and copies ran while one was open for 7% -> 8% of each run, Pallas kernels for 0% -> 0%
where the time goes in v1:
time: 143 us; the launch traced here: 142 us
  blocking collectives  45.5 us (32%)
  local copies, waits for them, and re-layouts  35.2 us (25%)
  waiting for transfers between devices  30.3 us (21%)
  matrix products  15.1 us (11%)
  between operations  14.3 us (10%)
  other arithmetic  2.14 us (1%)
    all_gather x1, waiting for transfers between devices, on_device(): gathered = lax.all_gather(owned_all, 'shard', axis=1, tiled=True)  30.2 us
    all_gather x1, blocking collectives, on_device(): weights_ln = lax.all_gather(norm_weights, 'shard', axis=1, tiled=True)  28.7 us
    psum x1, blocking collectives, on_device(): summed = lax.psum((factor_sq, factor_up, factor_down, norm_delta), 'rep')  16.8 us
    slice x1, local copies, waits for them, and re-layouts, on_device(): gathered[square + blocks_up:].reshape(blocks_down, shards, rows, width)  11 us
    unnamed x28, local copies, waits for them, and re-layouts  8.15 us
    transpose x1, local copies, waits for them, and re-layouts, join_cols(): return a.transpose(1, 0, 2).reshape(a.shape[1], -1)  6.68 us
    transpose x1, local copies, waits for them, and re-layouts, on_device(): weights_down = down.transpose(1, 0, 2, 3).reshape(-1, width)  5.12 us
    dot_general x1, matrix products, on_device(): jnp.einsum('brk,bdk->brd', mean_all, basis_all, precision=highest)  3.68 us
  transfers between devices with their start and end apart: 1, of which 1 were waited for; matrix products, arithmetic and copies ran while one was open for 8% of the time, Pallas kernels for 0%

profile of v1, /device:TPU:1, one launch (start us, length us, event | category | flops | bytes accessed | tf_op | source)
XLA Modules:
  0.0 142.5 jit_solution(3235308567669390856)
XLA Ops:
  7.2 0.0 copy-start.1
  7.2 0.0 copy-start.7
  7.2 0.0 copy-start.3
  7.2 0.0 copy-start.2
  7.2 0.0 copy-start
  7.2 0.0 copy-start.11
  7.2 0.0 all-gather.3.cloned.1.call-start
  7.3 0.9 bitcast_subtract_fusion.3
  8.1 2.2 %fusion.18 = f32[4,24,64]{2,1,0:T(8,128)S(1)} fusion(f32[4,768,64]{1,2,0:T(8,128)} %param.33, f32[1,4,24,768]{3,2,1,0:T(8,128)} %param.26, f32[4,24,768]{2,1,0:T(8,128)} %param.22, f32[1,4,24,768]{3,2,1,0:T(8,128)} %param.18), kind=kOutput, calls=%fused_computation.40 | convolution fusion | flops 56770560 | bytes 1695744 | tf_op jit(solution)/shard_map/mrd,mdk->mrk/dot_general | solution.py:49
  10.3 0.0 copy-start.9
  10.3 1.6 %fusion.20 = f32[96,64]{0,1:T(8,128)S(1)} fusion(f32[768,64]{0,1:T(8,128)} %param.35, f32[1,96,768]{2,1,0:T(8,128)} %param.28, f32[96,768]{1,0:T(8,128)} %param.24, f32[1,96,768]{2,1,0:T(8,128)} %param.20), kind=kOutput, calls=%fused_computation.42 | convolution fusion | flops 56770560 | bytes 1105920 | tf_op jit(solution)/shard_map/dot_general | solution.py:55
  11.9 0.0 copy-start.10
  11.9 2.1 %fusion.19 = f32[24,64]{1,0:T(8,128)S(1)} fusion(f32[3072,64]{0,1:T(8,128)} %param.34, f32[1,24,3072]{2,1,0:T(8,128)} %param.27, f32[24,3072]{1,0:T(8,128)} %param.23, f32[1,24,3072]{2,1,0:T(8,128)} %param.19), kind=kOutput, calls=%fused_computation.41 | convolution fusion | flops 56770560 | bytes 1677312 | tf_op jit(solution)/shard_map/dot_general | solution.py:52
  14.1 16.8 %all-reduce = (f32[96,64]{0,1:T(8,128)S(1)}, f32[24,64]{1,0:T(8,128)S(1)}, f32[4,24,64]{2,1,0:T(8,128)S(1)}, f32[4,24]{1,0:T(4,128)}) all-reduce(f32[96,64]{0,1:T(8,128)S(1)} %fusion.20, f32[24,64]{1,0:T(8,128)S(1)} %fusion.19, f32[4,24,64]{2,1,0:T(8,128)S(1)} %fusion.18, ...), channel_id=1, replica_groups=mesh['rep'=4,'shard'=32] {'rep'}, use_global_device_ids=true, to_apply=%region_2.0 | all-reduce | flops 13920 | bytes 111360 | tf_op jit(solution)/shard_map/psum | solution.py:62
  30.9 0.7 copy.41
  31.6 0.0 copy-done
  31.6 0.1 copy.56
  31.7 0.0 copy-done.2
  31.7 0.0 copy-done.11
  31.8 0.0 copy-done.3
  31.8 0.1 broadcast_in_dim.25
  31.9 0.0 copy-start.12
  31.9 0.0 copy-start.6
  31.9 0.0 copy-start.8
  31.9 0.0 copy-done.9
  31.9 0.0 copy-done.10
  31.9 0.0 copy-done.1
  31.9 0.0 copy-done.7
  31.9 0.0 copy-start.4
  31.9 0.0 copy-start.5
  32.0 3.7 %fusion.10 = (bf16[12,24,768]{2,1,0:T(8,128)(2,1)}, f32[12,24,768]{2,1,0:T(8,128)}) fusion(f32[4,24,768]{2,1,0:T(8,128)S(1)} %bitcast.94, f32[4,24,768]{2,1,0:T(8,128)S(1)} %get-tuple-element.47, f32[4,24,768]{2,1,0:T(8,128)} %param.22, f32[4,24,768]{2,1,0:T(8,128)} %bitcast.101, f32[4,24,768]{2,1,0:T(8,128)S(1)} %get-tuple-element.48, ...), kind=kOutput, calls=%fused_computation.16 | convolution fusion | flops 173518848 | bytes 5529600 | tf_op jit(solution)/shard_map/brk,bdk->brd/dot_general | solution.py:90
  35.6 0.0 all-gather.3.cloned.1.call-update
  35.7 2.0 %fusion.22 = (f32[4,24,768]{2,1,0:T(8,128)}, f32[4,3,8,768]{3,2,1,0:T(8,128)S(1)}, f32[4,24,768]{2,1,0:T(8,128)}) fusion(f32[12,24,768]{2,1,0:T(8,128)} %get-tuple-element.43), kind=kLoop, calls=%fused_computation.44 | loop fusion | bytes 1769472 | tf_op jit(solution)/shard_map/slice | solution.py:94
  37.7 0.7 copy.52
  38.4 1.3 fusion.16
  39.7 28.7 %all-gather = bf16[32,24,4]{1,2,0:T(4,128)(2,1)S(1)} all-gather(bf16[1,24,4]{1,2,0:T(4,128)(2,1)S(1)} %get-tuple-element.37), channel_id=1, replica_groups=mesh['rep'=4,'shard'=32] {'shard'}, dimensions={0}, use_global_device_ids=true | all-gather | bytes 6336 | tf_op jit(solution)/shard_map/all_gather | solution.py:101
  68.4 0.6 copy.47
  69.0 1.5 %reshape.69 = bf16[768,4]{0,1:T(4,128)(2,1)} reshape(bf16[32,24,4]{1,0,2:T(8,128)(2,1)} %copy.47) | data formatting | bytes 12288
  70.5 0.0 copy-done.6
  70.5 1.9 %fusion.7 = f32[1,96,768]{2,1,0:T(8,128)} fusion(f32[96,64]{0,1:T(8,128)} %copy-done.10, f32[768,64]{0,1:T(8,128)S(1)} %copy-done.3, f32[1,96,768]{2,1,0:T(8,128)S(1)} %copy-done.6, f32[96,768]{1,0:T(8,128)S(1)} %copy-done.7, f32[1,96,768]{2,1,0:T(8,128)S(1)} %copy-done.8), kind=kOutput, calls=%fused_computation.10 | convolution fusion | flops 56844288 | bytes 1400832 | tf_op jit(solution)/shard_map/rk,dk->rd/dot_general | solution.py:58
  72.4 0.0 copy-done.5
  72.4 1.2 fusion
  73.6 2.4 %fusion.8 = f32[1,4,24,768]{3,2,1,0:T(8,128)} fusion(f32[4,24,64]{2,1,0:T(8,128)} %copy-done.9, f32[4,768,64]{1,2,0:T(8,128)S(1)} %copy-done.1, f32[1,4,24,768]{3,2,1,0:T(8,128)} %param.26, f32[4,24,768]{2,1,0:T(8,128)} %param.22, f32[1,4,24,768]{3,2,1,0:T(8,128)} %param.18), kind=kOutput, calls=%fused_computation.12 | convolution fusion | flops 56844288 | bytes 1990656 | tf_op jit(solution)/shard_map/mrk,mdk->mrd/dot_general | solution.py:50
  76.0 30.2 %all-gather.3.cloned.1.call-done = bf16[12,768,768]{2,1,0:T(8,128)(2,1)} async-done(((bf16[12,24,768]{2,1,0:T(8,128)(2,1)}), bf16[12,768,768]{2,1,0:T(8,128)(2,1)}) %all-gather.3.cloned.1.call-update) | async-done | bytes 14155792 | tf_op jit(solution)/shard_map/all_gather | solution.py:95
  106.2 11.0 %fusion.21 = (bf16[4,768,768]{2,1,0:T(8,128)(2,1)}, bf16[768,4,768]{2,0,1:T(8,128)(2,1)}, bf16[4,768,768]{2,1,0:T(8,128)(2,1)}) fusion(bf16[12,768,768]{2,1,0:T(8,128)(2,1)} %all-gather.3.cloned.1.call-done), kind=kLoop, calls=%fused_computation.43 | loop fusion | bytes 28311552 | tf_op jit(solution)/shard_map/slice | solution.py:99
  117.2 6.7 %copy.45 = bf16[768,4,768]{0,2,1:T(8,128)(2,1)} copy(bf16[768,4,768]{2,0,1:T(8,128)(2,1)} %get-tuple-element.40) | data formatting | bytes 9437184 | tf_op jit(solution)/shard_map/transpose | solution.py:21
  123.9 6.6 %copy.48 = bf16[768,3072]{1,0:T(8,128)(2,1)} copy(bf16[768,3072]{0,1:T(8,128)(2,1)} %bitcast.90) | data formatting | bytes 9437184
  130.5 5.1 %copy.46 = bf16[32,4,24,768]{3,2,1,0:T(8,128)(2,1)} copy(bf16[32,4,24,768]{3,2,0,1:T(8,128)(2,1)} %bitcast.89) | data formatting | bytes 9437184 | tf_op jit(solution)/shard_map/transpose | solution.py:100
  (8 shorter events, 0.1 us)
Async XLA Ops:
  7.2 24.7 %copy-start.1 = (f32[4,768,64]{1,2,0:T(8,128)S(1)}, f32[4,768,64]{1,2,0:T(8,128)}, u32[]{:S(2)}) copy-start(f32[4,768,64]{1,2,0:T(8,128)} %param.33) | copy-start | bytes 2359300
  7.2 24.7 %copy-start.7 = (f32[96,768]{1,0:T(8,128)S(1)}, f32[96,768]{1,0:T(8,128)}, u32[]{:S(2)}) copy-start(f32[96,768]{1,0:T(8,128)} %param.24) | copy-start | bytes 884740
  7.2 24.6 %copy-start.3 = (f32[768,64]{0,1:T(8,128)S(1)}, f32[768,64]{0,1:T(8,128)}, u32[]{:S(2)}) copy-start(f32[768,64]{0,1:T(8,128)} %param.35) | copy-start | bytes 589828
  7.2 24.5 %copy-start.2 = (f32[24,3072]{1,0:T(8,128)S(1)}, f32[24,3072]{1,0:T(8,128)}, u32[]{:S(2)}) copy-start(f32[24,3072]{1,0:T(8,128)} %param.23) | copy-start | bytes 884740
  7.2 24.4 %copy-start = (f32[3072,64]{0,1:T(8,128)S(1)}, f32[3072,64]{0,1:T(8,128)}, u32[]{:S(2)}) copy-start(f32[3072,64]{0,1:T(8,128)} %param.34) | copy-start | bytes 2359300
  7.2 24.5 %copy-start.11 = (f32[24,3072]{1,0:T(8,128)S(1)}, f32[24,3072]{1,0:T(8,128)}, u32[]{:S(2)}) copy-start(f32[24,3072]{1,0:T(8,128)} %param.30) | copy-start | bytes 884740
  7.2 99.0 %all-gather.3.cloned.1.call-start = ((), (), s32[]{:S(2)}) async-start(), calls=%async_computation | async-start | bytes 14598144 | tf_op jit(solution)/shard_map/all_gather | solution.py:95
  10.3 21.6 %copy-start.9 = (f32[4,24,64]{2,1,0:T(8,128)}, f32[4,24,64]{2,1,0:T(8,128)S(1)}, u32[]{:S(2)}) copy-start(f32[4,24,64]{2,1,0:T(8,128)S(1)} %fusion.18) | copy-start | bytes 73732
  11.9 20.0 %copy-start.10 = (f32[96,64]{0,1:T(8,128)}, f32[96,64]{0,1:T(8,128)S(1)}, u32[]{:S(2)}) copy-start(f32[96,64]{0,1:T(8,128)S(1)} %fusion.20) | copy-start | bytes 73732
  31.9 6.6 %copy-start.12 = (f32[4,24]{1,0:T(4,128)S(1)}, f32[4,24]{1,0:T(4,128)}, u32[]{:S(2)}) copy-start(f32[4,24]{1,0:T(4,128)} %param.25) | copy-start | bytes 1156
  31.9 38.6 %copy-start.6 = (f32[1,96,768]{2,1,0:T(8,128)S(1)}, f32[1,96,768]{2,1,0:T(8,128)}, u32[]{:S(2)}) copy-start(f32[1,96,768]{2,1,0:T(8,128)} %param.28) | copy-start | bytes 884740
  31.9 38.6 %copy-start.8 = (f32[1,96,768]{2,1,0:T(8,128)S(1)}, f32[1,96,768]{2,1,0:T(8,128)}, u32[]{:S(2)}) copy-start(f32[1,96,768]{2,1,0:T(8,128)} %param.20) | copy-start | bytes 884740
  31.9 40.4 %copy-start.4 = (f32[1,24,3072]{2,1,0:T(8,128)S(1)}, f32[1,24,3072]{2,1,0:T(8,128)}, u32[]{:S(2)}) copy-start(f32[1,24,3072]{2,1,0:T(8,128)} %param.27) | copy-start | bytes 884740
  31.9 40.4 %copy-start.5 = (f32[1,24,3072]{2,1,0:T(8,128)S(1)}, f32[1,24,3072]{2,1,0:T(8,128)}, u32[]{:S(2)}) copy-start(f32[1,24,3072]{2,1,0:T(8,128)} %param.19) | copy-start | bytes 884740
Sparse Core Ops, SparseCore 0:
  35.8 70.3 all-gather.2

commit v2 on v1

--- a/solution.py
+++ b/solution.py
@@ -1,6 +1,7 @@
 import jax
 import jax.numpy as jnp
 from jax import lax
+from jax.experimental import pallas as pl
 from jax.sharding import PartitionSpec as P
 
 moment_coef = 0.9
@@ -19,6 +20,41 @@
 
 def join_cols(a):
     return a.transpose(1, 0, 2).reshape(a.shape[1], -1)
+
+
+def unpack_kernel(g_ref, sq_ref, up_ref, down_ref):
+    blocks = g_ref.shape[1]
+    rows = g_ref.shape[2] // 2
+    sq_ref[...] = g_ref[0]
+    up_ref[...] = jnp.concatenate([g_ref[1, k] for k in range(blocks)], axis=1)
+    x = g_ref[2].astype(jnp.float32)
+    pieces = [x[q, h * rows : (h + 1) * rows] for h in range(2) for q in range(blocks)]
+    down_ref[...] = jnp.concatenate(pieces, axis=0).astype(down_ref.dtype)
+
+
+def unpack(gathered, rows):
+    kinds_blocks, total, width = gathered.shape
+    blocks = kinds_blocks // 3
+    g = gathered.reshape(3, blocks, total, width)
+    step = 2 * rows
+    dt = gathered.dtype
+    nbytes = 2 * gathered.size * dt.itemsize
+    return pl.pallas_call(
+        unpack_kernel,
+        grid=(total // step,),
+        in_specs=[pl.BlockSpec((3, blocks, step, width), lambda j: (0, 0, j, 0))],
+        out_specs=[
+            pl.BlockSpec((blocks, step, width), lambda j: (0, j, 0)),
+            pl.BlockSpec((step, blocks * width), lambda j: (j, 0)),
+            pl.BlockSpec((blocks * step, width), lambda j: (j, 0)),
+        ],
+        out_shape=[
+            jax.ShapeDtypeStruct((blocks, total, width), dt),
+            jax.ShapeDtypeStruct((total, blocks * width), dt),
+            jax.ShapeDtypeStruct((blocks * total, width), dt),
+        ],
+        cost_estimate=pl.CostEstimate(flops=0, transcendentals=0, bytes_accessed=nbytes),
+    )(g)
 
 
 def on_device(
@@ -93,11 +129,7 @@
     new_mom_up = join_cols(new_mom_all[square : square + blocks_up])
     new_mom_down = new_mom_all[square + blocks_up :].reshape(-1, width)
     gathered = lax.all_gather(owned_all, "shard", axis=1, tiled=True)
-    shards = lax.axis_size("shard")
-    weights_sq = gathered[:square]
-    weights_up = join_cols(gathered[square : square + blocks_up])
-    down = gathered[square + blocks_up :].reshape(blocks_down, shards, rows, width)
-    weights_down = down.transpose(1, 0, 2, 3).reshape(-1, width)
+    weights_sq, weights_up, weights_down = unpack(gathered, rows)
     weights_ln = lax.all_gather(norm_weights, "shard", axis=1, tiled=True)
     return (
         new_resid_sq[None],

time: 143 us -> 128 us (0.90)
  local copies, waits for them, and re-layouts: 35.2 us -> 6.25 us
  Pallas kernels: 0 us -> 15.9 us
  matrix products: 15.1 us -> 11.4 us
    pallas_call x0 -> x1, Pallas kernels: none -> 15.9 us  [unpack(): pl.pallas_call(unpack_kernel, grid=(total // step,), in_specs=[pl.BlockSp...]
    transpose x2 -> x0, local copies, waits for them, and re-layouts: 11.8 us -> none  [the longest x1 6.68 us: join_cols(): return a.transpose(1, 0, 2).reshape(a.shape[1], -1)]
    slice x1 -> x0, local copies, waits for them, and re-layouts: 11 us -> none  [on_device(): gathered[square + blocks_up:].reshape(blocks_down, shards, rows, width)]
    unnamed x28 -> x39, local copies, waits for them, and re-layouts: 8.15 us -> 1.56 us
where the time goes in v2:
time: 128 us; the launch traced here: 127 us
  blocking collectives  45.6 us (36%)
  waiting for transfers between devices  31.3 us (24%)
  Pallas kernels  15.9 us (12%)
  between operations  14.3 us (11%)
  matrix products  11.4 us (9%)
  local copies, waits for them, and re-layouts  6.25 us (5%)
  other arithmetic  2.1 us (2%)
    all_gather x1, waiting for transfers between devices, on_device(): gathered = lax.all_gather(owned_all, 'shard', axis=1, tiled=True)  31.3 us
    all_gather x1, blocking collectives, on_device(): weights_ln = lax.all_gather(norm_weights, 'shard', axis=1, tiled=True)  28.7 us
    psum x1, blocking collectives, on_device(): summed = lax.psum((factor_sq, factor_up, factor_down, norm_delta), 'rep')  16.9 us
    pallas_call x1, Pallas kernels, unpack(): pl.pallas_call(unpack_kernel, grid=(total // step,), in_specs=[pl.BlockSp...  15.9 us
  transfers between devices with their start and end apart: 1, of which 1 were waited for; matrix products, arithmetic and copies ran while one was open for 8% of the time, Pallas kernels for 0%

profile of v2, /device:TPU:1, one launch (start us, length us, event | category | flops | bytes accessed | tf_op | source)
XLA Modules:
  0.0 126.9 jit_solution(14437862395761135355)
XLA Ops:
  7.2 0.0 copy-start.5
  7.2 0.0 copy-start.2
  7.2 0.0 copy-start.4
  7.2 0.0 copy-start
  7.2 0.0 all-gather.3.cloned.1.call-start
  7.3 0.8 bitcast_subtract_fusion.3
  8.1 2.2 %fusion.18 = f32[4,24,64]{2,1,0:T(8,128)S(1)} fusion(f32[4,768,64]{1,2,0:T(8,128)} %param.33, f32[1,4,24,768]{3,2,1,0:T(8,128)} %param.26, f32[4,24,768]{2,1,0:T(8,128)} %param.22, f32[1,4,24,768]{3,2,1,0:T(8,128)} %param.18), kind=kOutput, calls=%fused_computation.39 | convolution fusion | flops 56770560 | bytes 1695744 | tf_op jit(solution)/shard_map/mrd,mdk->mrk/dot_general | solution.py:85
  10.2 0.0 copy-start.13
  10.3 1.6 %fusion.20 = f32[96,64]{0,1:T(8,128)S(1)} fusion(f32[768,64]{0,1:T(8,128)} %param.35, f32[1,96,768]{2,1,0:T(8,128)} %param.28, f32[96,768]{1,0:T(8,128)} %param.24, f32[1,96,768]{2,1,0:T(8,128)} %param.20), kind=kOutput, calls=%fused_computation.41 | convolution fusion | flops 56770560 | bytes 1105920 | tf_op jit(solution)/shard_map/dot_general | solution.py:91
  11.9 0.0 copy-done.5
  11.9 0.0 copy-done.2
  11.9 0.0 copy-done.4
  11.9 0.0 copy-done
  11.9 0.0 copy-start.15
  11.9 0.0 copy-start.3
  11.9 0.7 fusion.19
  12.6 0.0 copy-start.1
  12.7 0.0 copy-start.7
  12.7 0.0 copy-start.10
  12.7 16.9 %all-reduce = (f32[96,64]{0,1:T(8,128)S(1)}, f32[24,64]{1,0:T(8,128)S(1)}, f32[4,24,64]{2,1,0:T(8,128)S(1)}, f32[4,24]{1,0:T(4,128)}) all-reduce(f32[96,64]{0,1:T(8,128)S(1)} %fusion.20, f32[24,64]{1,0:T(8,128)S(1)} %fusion.19, f32[4,24,64]{2,1,0:T(8,128)S(1)} %fusion.18, ...), channel_id=1, replica_groups=mesh['rep'=4,'shard'=32] {'rep'}, use_global_device_ids=true, to_apply=%region_2.0 | all-reduce | flops 13920 | bytes 111360 | tf_op jit(solution)/shard_map/psum | solution.py:98
  29.6 0.1 copy.37
  29.7 0.0 copy-start.17
  29.7 0.0 copy-start.18
  29.8 0.1 copy.49
  29.8 0.0 copy-done.13
  29.8 1.1 bitcast_bitcast_fusion
  30.9 0.0 copy-done.15
  30.9 0.0 copy-done.3
  30.9 0.1 broadcast_in_dim.25
  31.0 0.0 copy-done.1
  31.0 0.0 copy-done.7
  31.1 2.5 %fusion.10 = (bf16[12,24,768]{2,1,0:T(8,128)(2,1)}, f32[12,24,768]{2,1,0:T(8,128)}) fusion(f32[4,24,768]{2,1,0:T(8,128)S(1)} %bitcast.86, f32[4,24,768]{2,1,0:T(8,128)S(1)} %get-tuple-element.28, f32[4,24,768]{2,1,0:T(8,128)S(1)} %copy-done.10, f32[4,24,768]{2,1,0:T(8,128)S(1)} %bitcast.93, f32[4,24,768]{2,1,0:T(8,128)S(1)} %get-tuple-element.29, ...), kind=kOutput, calls=%fused_computation.15 | convolution fusion | flops 173518848 | bytes 5529600 | tf_op jit(solution)/shard_map/brk,bdk->brd/dot_general | solution.py:126
  33.5 0.0 all-gather.3.cloned.1.call-update
  33.5 2.1 %fusion.21 = (f32[4,24,768]{2,1,0:T(8,128)}, f32[4,3,8,768]{3,2,1,0:T(8,128)S(1)}, f32[4,24,768]{2,1,0:T(8,128)}) fusion(f32[12,24,768]{2,1,0:T(8,128)} %get-tuple-element.24), kind=kLoop, calls=%fused_computation.42 | loop fusion | bytes 1769472 | tf_op jit(solution)/shard_map/slice | solution.py:130
  35.6 0.7 copy.45
  36.4 0.0 copy-done.16
  36.4 1.3 %fusion.16 = (bf16[1,24,4]{1,2,0:T(4,128)(2,1)S(1)}, f32[4,24]{1,0:T(4,128)}) fusion(f32[4,24]{1,0:T(4,128)S(1)} %copy-done.16, f32[4,24]{1,0:T(4,128)} %get-tuple-element.20, f32[4,24]{1,0:T(4,128)} %param.32), kind=kLoop, calls=%fused_computation.37 | loop fusion | flops 768 | bytes 1728
  37.6 28.7 %all-gather = bf16[32,24,4]{1,2,0:T(4,128)(2,1)S(1)} all-gather(bf16[1,24,4]{1,2,0:T(4,128)(2,1)S(1)} %get-tuple-element.21), channel_id=1, replica_groups=mesh['rep'=4,'shard'=32] {'shard'}, dimensions={0}, use_global_device_ids=true | all-gather | bytes 6336 | tf_op jit(solution)/shard_map/all_gather | solution.py:133
  66.3 0.6 copy.41
  66.9 1.5 %reshape.61 = bf16[768,4]{0,1:T(4,128)(2,1)} reshape(bf16[32,24,4]{1,0,2:T(8,128)(2,1)} %copy.41) | data formatting | bytes 12288
  68.4 0.0 copy-start.12
  68.4 0.0 copy-start.14
  68.4 2.0 %fusion.7 = f32[1,96,768]{2,1,0:T(8,128)} fusion(f32[96,64]{0,1:T(8,128)} %copy-done.15, f32[768,64]{0,1:T(8,128)S(1)} %copy-done.3, f32[1,96,768]{2,1,0:T(8,128)S(1)} %copy-done.6, f32[96,768]{1,0:T(8,128)S(1)} %copy-done.7, f32[1,96,768]{2,1,0:T(8,128)S(1)} %copy-done.8), kind=kOutput, calls=%fused_computation.9 | convolution fusion | flops 56844288 | bytes 1400832 | tf_op jit(solution)/shard_map/rk,dk->rd/dot_general | solution.py:94
  70.4 1.2 fusion
  71.6 0.0 copy-done.9
  71.7 1.2 fusion.8
  72.9 31.3 %all-gather.3.cloned.1.call-done = bf16[12,768,768]{2,1,0:T(8,128)(2,1)} async-done(((bf16[12,24,768]{2,1,0:T(8,128)(2,1)}), bf16[12,768,768]{2,1,0:T(8,128)(2,1)}) %all-gather.3.cloned.1.call-update) | async-done | bytes 14155792 | tf_op jit(solution)/shard_map/all_gather | solution.py:131
  104.2 15.9 %shard_map.257 = (bf16[4,768,768]{2,1,0:T(8,128)(2,1)}, bf16[768,3072]{1,0:T(8,128)(2,1)}, bf16[3072,768]{1,0:T(8,128)(2,1)}) custom-call(bf16[3,4,768,768]{3,2,1,0:T(8,128)(2,1)} %bitcast.83), custom_call_target="tpu_custom_call" | custom-call | bytes 28311552 | tf_op jit(solution)/shard_map/pallas_call | solution.py:42
  (17 shorter events, 0.0 us)
Async XLA Ops:
  7.2 4.7 %copy-start.5 = (f32[1,24,3072]{2,1,0:T(8,128)S(1)}, f32[1,24,3072]{2,1,0:T(8,128)}, u32[]{:S(2)}) copy-start(f32[1,24,3072]{2,1,0:T(8,128)} %param.19) | copy-start | bytes 884740
  7.2 4.7 %copy-start.2 = (f32[24,3072]{1,0:T(8,128)S(1)}, f32[24,3072]{1,0:T(8,128)}, u32[]{:S(2)}) copy-start(f32[24,3072]{1,0:T(8,128)} %param.23) | copy-start | bytes 884740
  7.2 4.7 %copy-start.4 = (f32[1,24,3072]{2,1,0:T(8,128)S(1)}, f32[1,24,3072]{2,1,0:T(8,128)}, u32[]{:S(2)}) copy-start(f32[1,24,3072]{2,1,0:T(8,128)} %param.27) | copy-start | bytes 884740
  7.2 4.7 %copy-start = (f32[3072,64]{0,1:T(8,128)S(1)}, f32[3072,64]{0,1:T(8,128)}, u32[]{:S(2)}) copy-start(f32[3072,64]{0,1:T(8,128)} %param.34) | copy-start | bytes 2359300
  7.2 96.9 %all-gather.3.cloned.1.call-start = ((), (), s32[]{:S(2)}) async-start(), calls=%async_computation | async-start | bytes 14598144 | tf_op jit(solution)/shard_map/all_gather | solution.py:131
  10.2 19.6 %copy-start.13 = (f32[4,24,64]{2,1,0:T(8,128)}, f32[4,24,64]{2,1,0:T(8,128)S(1)}, u32[]{:S(2)}) copy-start(f32[4,24,64]{2,1,0:T(8,128)S(1)} %fusion.18) | copy-start | bytes 73732
  11.9 19.0 %copy-start.15 = (f32[96,64]{0,1:T(8,128)}, f32[96,64]{0,1:T(8,128)S(1)}, u32[]{:S(2)}) copy-start(f32[96,64]{0,1:T(8,128)S(1)} %fusion.20) | copy-start | bytes 73732
  11.9 19.0 %copy-start.3 = (f32[768,64]{0,1:T(8,128)S(1)}, f32[768,64]{0,1:T(8,128)}, u32[]{:S(2)}) copy-start(f32[768,64]{0,1:T(8,128)} %param.35) | copy-start | bytes 589828
  12.6 18.4 %copy-start.1 = (f32[4,768,64]{1,2,0:T(8,128)S(1)}, f32[4,768,64]{1,2,0:T(8,128)}, u32[]{:S(2)}) copy-start(f32[4,768,64]{1,2,0:T(8,128)} %param.33) | copy-start | bytes 2359300
  12.7 18.3 %copy-start.7 = (f32[96,768]{1,0:T(8,128)S(1)}, f32[96,768]{1,0:T(8,128)}, u32[]{:S(2)}) copy-start(f32[96,768]{1,0:T(8,128)} %param.24) | copy-start | bytes 884740
  12.7 18.3 %copy-start.10 = (f32[4,24,768]{2,1,0:T(8,128)S(1)}, f32[4,24,768]{2,1,0:T(8,128)}, u32[]{:S(2)}) copy-start(f32[4,24,768]{2,1,0:T(8,128)} %param.22) | copy-start | bytes 884740
  29.7 1.3 %copy-start.17 = (f32[96,768]{1,0:T(8,128)S(1)}, f32[96,768]{1,0:T(8,128)}, u32[]{:S(2)}) copy-start(f32[96,768]{1,0:T(8,128)} %param.31) | copy-start | bytes 884740
  29.7 1.3 %copy-start.18 = (f32[4,24,768]{2,1,0:T(8,128)S(1)}, f32[4,24,768]{2,1,0:T(8,128)}, u32[]{:S(2)}) copy-start(f32[4,24,768]{2,1,0:T(8,128)} %param.29) | copy-start | bytes 884740
  33.5 2.8 %copy-start.16 = (f32[4,24]{1,0:T(4,128)S(1)}, f32[4,24]{1,0:T(4,128)}, u32[]{:S(2)}) copy-start(f32[4,24]{1,0:T(4,128)} %param.25) | copy-start | bytes 1156
  33.5 34.9 %copy-start.6 = (f32[1,96,768]{2,1,0:T(8,128)S(1)}, f32[1,96,768]{2,1,0:T(8,128)}, u32[]{:S(2)}) copy-start(f32[1,96,768]{2,1,0:T(8,128)} %param.28) | copy-start | bytes 884740
  33.5 34.9 %copy-start.8 = (f32[1,96,768]{2,1,0:T(8,128)S(1)}, f32[1,96,768]{2,1,0:T(8,128)}, u32[]{:S(2)}) copy-start(f32[1,96,768]{2,1,0:T(8,128)} %param.20) | copy-start | bytes 884740
  68.4 3.2 %copy-start.9 = (f32[1,4,24,768]{3,2,1,0:T(8,128)S(1)}, f32[1,4,24,768]{3,2,1,0:T(8,128)}, u32[]{:S(2)}) copy-start(f32[1,4,24,768]{3,2,1,0:T(8,128)} %param.26) | copy-start | bytes 884740
  68.4 3.2 %copy-start.11 = (f32[4,24,768]{2,1,0:T(8,128)S(1)}, f32[4,24,768]{2,1,0:T(8,128)}, u32[]{:S(2)}) copy-start(f32[4,24,768]{2,1,0:T(8,128)} %param.22) | copy-start | bytes 884740
  68.4 3.2 %copy-start.12 = (f32[1,4,24,768]{3,2,1,0:T(8,128)S(1)}, f32[1,4,24,768]{3,2,1,0:T(8,128)}, u32[]{:S(2)}) copy-start(f32[1,4,24,768]{3,2,1,0:T(8,128)} %param.18) | copy-start | bytes 884740
  68.4 3.2 %copy-start.14 = (f32[4,24,64]{2,1,0:T(8,128)S(1)}, f32[4,24,64]{2,1,0:T(8,128)}, u32[]{:S(2)}) copy-start(f32[4,24,64]{2,1,0:T(8,128)} %copy-done.13) | copy-start | bytes 73732
Sparse Core Ops, SparseCore 0:
  33.7 70.4 all-gather.2

commit v3 on v2

--- a/solution.py
+++ b/solution.py
@@ -1,3 +1,5 @@
+import functools
+
 import jax
 import jax.numpy as jnp
 from jax import lax
@@ -22,13 +24,13 @@
     return a.transpose(1, 0, 2).reshape(a.shape[1], -1)
 
 
-def unpack_kernel(g_ref, sq_ref, up_ref, down_ref):
+def unpack_kernel(rows, g_ref, sq_ref, up_ref, down_ref):
     blocks = g_ref.shape[1]
-    rows = g_ref.shape[2] // 2
     sq_ref[...] = g_ref[0]
     up_ref[...] = jnp.concatenate([g_ref[1, k] for k in range(blocks)], axis=1)
     x = g_ref[2].astype(jnp.float32)
-    pieces = [x[q, h * rows : (h + 1) * rows] for h in range(2) for q in range(blocks)]
+    per_step = g_ref.shape[2] // rows
+    pieces = [x[q, h * rows : (h + 1) * rows] for h in range(per_step) for q in range(blocks)]
     down_ref[...] = jnp.concatenate(pieces, axis=0).astype(down_ref.dtype)
 
 
@@ -36,11 +38,11 @@
     kinds_blocks, total, width = gathered.shape
     blocks = kinds_blocks // 3
     g = gathered.reshape(3, blocks, total, width)
-    step = 2 * rows
+    step = 8 * rows
     dt = gathered.dtype
     nbytes = 2 * gathered.size * dt.itemsize
     return pl.pallas_call(
-        unpack_kernel,
+        functools.partial(unpack_kernel, rows),
         grid=(total // step,),
         in_specs=[pl.BlockSpec((3, blocks, step, width), lambda j: (0, 0, j, 0))],
         out_specs=[
@@ -55,6 +57,16 @@
         ],
         cost_estimate=pl.CostEstimate(flops=0, transcendentals=0, bytes_accessed=nbytes),
     )(g)
+
+
+def rep_sum(parts):
+    n = lax.axis_size("rep")
+    step = 1
+    while step < n:
+        other = lax.ppermute(parts, "rep", [(i, i ^ step) for i in range(n)])
+        parts = jax.tree.map(jnp.add, parts, other)
+        step *= 2
+    return parts
 
 
 def on_device(
@@ -95,7 +107,7 @@
         "rk,dk->rd", factor_down, basis_down, precision=highest
     )
     norm_delta = start_ln - trained_ln[0]
-    summed = lax.psum((factor_sq, factor_up, factor_down, norm_delta), "rep")
+    summed = rep_sum((factor_sq, factor_up, factor_down, norm_delta))
     mean_sq = summed[0] / groups
     mean_up = summed[1] / groups
     mean_down = summed[2] / groups

time: 128 us -> 121 us (0.945)
  blocking collectives: 45.6 us -> 28.5 us
  starting transfers between devices: 0.04 us -> 13.2 us
  Pallas kernels: 15.9 us -> 10.1 us
  other arithmetic: 2.1 us -> 4.06 us
  matrix products: 11.4 us -> 12.8 us
  waiting for transfers between devices: 31.3 us -> 30 us
    psum x1 -> x0, blocking collectives: 16.9 us -> none  [on_device(): summed = lax.psum((factor_sq, factor_up, factor_down, norm_delta), 'rep')]
    ppermute x0 -> x8, starting transfers between devices: none -> 13.1 us  [rep_sum(): other = lax.ppermute(parts, 'rep', [(i, i ^ step) for i in range(n)])]
    pallas_call x1, Pallas kernels: 15.9 us -> 10.1 us  [unpack(): pl.pallas_call(functools.partial(unpack_kernel, rows), grid=(total // ste...]
    all_gather x1, waiting for transfers between devices: 31.3 us -> 29.1 us  [on_device(): gathered = lax.all_gather(owned_all, 'shard', axis=1, tiled=True)]
    dot_general x1, matrix products: 0.72 us -> 2.28 us  [on_device(): jnp.dot(delta_up, basis_up, precision=highest, preferred_element_type=jnp...]
    dot_general x1, matrix products: 2.16 us -> 0.75 us  [on_device(): jnp.einsum('mrd,mdk->mrk', delta_sq, basis_sq, precision=highest)]
    div x1, local copies, waits for them, and re-layouts: 0.08 us -> 1.47 us  [on_device(): mean_down = summed[2] / groups]
    dot_general x1, matrix products: 2.47 us -> 3.82 us  [on_device(): jnp.einsum('brk,bdk->brd', mean_all, basis_all, precision=highest)]
  transfers between devices with their start and end apart: 1 -> 9, of which waited for: 1 -> 3; matrix products, arithmetic and copies ran while one was open for 8% -> 14% of each run, Pallas kernels for 0% -> 0%
where the time goes in v3:
time: 121 us; the launch traced here: 120 us
  waiting for transfers between devices  30 us (25%)
  blocking collectives  28.5 us (24%)
  between operations  14.2 us (12%)
  starting transfers between devices  13.2 us (11%)
  matrix products  12.8 us (11%)
  Pallas kernels  10.1 us (8%)
  local copies, waits for them, and re-layouts  7.47 us (6%)
  other arithmetic  4.06 us (3%)
    all_gather x1, waiting for transfers between devices, on_device(): gathered = lax.all_gather(owned_all, 'shard', axis=1, tiled=True)  29.1 us
    all_gather x1, blocking collectives, on_device(): weights_ln = lax.all_gather(norm_weights, 'shard', axis=1, tiled=True)  28.5 us
    ppermute x8, starting transfers between devices, rep_sum(): other = lax.ppermute(parts, 'rep', [(i, i ^ step) for i in range(n)])  13.1 us
    pallas_call x1, Pallas kernels, unpack(): pl.pallas_call(functools.partial(unpack_kernel, rows), grid=(total // ste...  10.1 us
    dot_general x1, matrix products, on_device(): jnp.einsum('brk,bdk->brd', mean_all, basis_all, precision=highest)  3.82 us
  transfers between devices with their start and end apart: 9, of which 3 were waited for; matrix products, arithmetic and copies ran while one was open for 14% of the time, Pallas kernels for 0%

profile of v3, /device:TPU:1, one launch (start us, length us, event | category | flops | bytes accessed | tf_op | source)
XLA Modules:
  0.0 120.3 jit_solution(4883578615836451835)
XLA Ops:
  7.2 0.0 all-gather.3.cloned.1.call-start
  7.3 2.3 %fusion.19 = f32[24,64]{1,0:T(8,128)S(1)} fusion(f32[3072,64]{0,1:T(8,128)} %param.34, f32[1,24,3072]{2,1,0:T(8,128)} %param.27, f32[24,3072]{1,0:T(8,128)} %param.23, f32[1,24,3072]{2,1,0:T(8,128)} %param.19), kind=kOutput, calls=%fused_computation.41 | convolution fusion | flops 56770560 | bytes 1677312 | tf_op jit(solution)/shard_map/dot_general | solution.py:100
  9.6 0.0 copy-start.2
  9.6 0.0 copy-start.16
  9.6 2.5 %collective-permute-start.2 = (f32[24,64]{1,0:T(8,128)S(1)}, f32[24,64]{1,0:T(8,128)S(1)}, u32[]{:S(2)}, u32[]{:S(2)}) collective-permute-start(f32[24,64]{1,0:T(8,128)S(1)} %fusion.19), channel_id=1, source_target_pairs={{0,32},{32,0},{64,96},{96,64},{1,33},{33,1},{65,97},{97,65},{2,34}... | collective-permute-start | bytes 18440 | tf_op jit(solution)/shard_map/ppermute | solution.py:66
  12.1 1.6 %fusion.20 = f32[96,64]{0,1:T(8,128)S(1)} fusion(f32[768,64]{0,1:T(8,128)} %param.35, f32[1,96,768]{2,1,0:T(8,128)} %param.28, f32[96,768]{1,0:T(8,128)} %param.24, f32[1,96,768]{2,1,0:T(8,128)} %param.20), kind=kOutput, calls=%fused_computation.42 | convolution fusion | flops 56770560 | bytes 1105920 | tf_op jit(solution)/shard_map/dot_general | solution.py:103
  13.7 0.2 collective-permute-start.4
  13.9 0.0 collective-permute-done.2
  13.9 3.4 %collective-permute-start.3 = (f32[24,64]{1,0:T(8,128)S(1)}, f32[24,64]{1,0:T(8,128)S(1)}, u32[]{:S(2)}, u32[]{:S(2)}) collective-permute-start(f32[24,64]{1,0:T(8,128)S(1)} %add.50), channel_id=1, source_target_pairs={{0,64},{32,96},{64,0},{96,32},{1,65},{33,97},{65,1},{97,33},{2,66}... | collective-permute-start | bytes 18440 | tf_op jit(solution)/shard_map/ppermute | solution.py:66
  17.3 0.8 fusion.18
  18.1 0.8 collective-permute-start
  18.9 0.9 copy.49
  19.9 0.7 copy.51
  20.6 0.0 collective-permute-done.4
  20.6 1.0 collective-permute-start.5
  21.6 0.0 collective-permute-done.3
  21.6 0.6 add_multiply_fusion.2
  22.2 0.0 collective-permute-done
  22.2 0.6 add.48
  22.9 2.1 %collective-permute-start.1 = (f32[4,24,64]{2,1,0:T(8,128)}, f32[4,24,64]{2,1,0:T(8,128)}, u32[]{:S(2)}, u32[]{:S(2)}) collective-permute-start(f32[4,24,64]{2,1,0:T(8,128)} %add.48), channel_id=1, source_target_pairs={{0,64},{32,96},{64,0},{96,32},{1,65},{33,97},{65,1},{97,33},{2,66}... | collective-permute-start | bytes 73736 | tf_op jit(solution)/shard_map/ppermute | solution.py:66
  24.9 0.1 collective-permute-done.5
  25.0 0.6 add_multiply_fusion.1
  25.6 1.5 %copy.37 = f32[96,64]{1,0:T(8,128)} copy(f32[96,64]{0,1:T(8,128)} %add_multiply_fusion.1) | data formatting | bytes 49152 | tf_op jit(solution)/shard_map/div | solution.py:113
  27.1 0.8 collective-permute-done.1
  27.9 0.8 add_multiply_fusion
  28.7 0.7 broadcast_in_dim.24
  29.4 0.1 broadcast_in_dim.25
  29.5 0.0 copy-start.17
  29.5 3.8 %fusion.10 = (bf16[12,24,768]{2,1,0:T(8,128)(2,1)}, f32[12,24,768]{2,1,0:T(8,128)}) fusion(f32[4,24,768]{2,1,0:T(8,128)S(1)} %bitcast.90, f32[4,24,768]{2,1,0:T(8,128)S(1)} %bitcast.94, f32[4,24,768]{2,1,0:T(8,128)S(1)} %copy-done.7, f32[4,24,768]{2,1,0:T(8,128)} %bitcast.99, f32[4,24,768]{2,1,0:T(8,128)} %bitcast.95, f32[4,24,768]{2,1,0:T(8,128)} %param.29, ...), kind=kOutput, calls=%fused_computation.15 | convolution fusion | flops 173518848 | bytes 5529600 | tf_op jit(solution)/shard_map/brk,bdk->brd/dot_general | solution.py:138
  33.3 0.0 all-gather.3.cloned.1.call-update
  33.4 0.0 copy-start.9
  33.4 0.0 copy-start.11
  33.4 0.0 copy-start.12
  33.4 0.8 bitcast_subtract_fusion.3
  34.2 0.0 collective-permute-start.6
  34.2 2.0 %fusion.8 = f32[1,4,24,768]{3,2,1,0:T(8,128)} fusion(f32[4,24,64]{2,1,0:T(8,128)} %copy-done.13, f32[4,768,64]{1,2,0:T(8,128)S(1)} %copy-done.1, f32[1,4,24,768]{3,2,1,0:T(8,128)S(1)} %copy-done.6, f32[4,24,768]{2,1,0:T(8,128)S(1)} %copy-done.7, f32[1,4,24,768]{3,2,1,0:T(8,128)S(1)} %copy-done.8), kind=kOutput, calls=%fused_computation.11 | convolution fusion | flops 56844288 | bytes 1990656 | tf_op jit(solution)/shard_map/mrk,mdk->mrd/dot_general | solution.py:98
  36.2 1.2 %fusion = f32[1,24,3072]{2,1,0:T(8,128)} fusion(f32[24,64]{1,0:T(8,128)S(1)} %fusion.19, f32[3072,64]{0,1:T(8,128)S(1)} %copy-done, f32[1,24,3072]{2,1,0:T(8,128)S(1)} %copy-done.4, f32[24,3072]{1,0:T(8,128)S(1)} %copy-done.2, f32[1,24,3072]{2,1,0:T(8,128)S(1)} %copy-done.5), kind=kOutput, calls=%fused_computation.1 | convolution fusion | flops 56844288 | bytes 1972224 | tf_op jit(solution)/shard_map/rk,fk->rf/dot_general | solution.py:101
  37.5 0.0 collective-permute-done.6
  37.5 3.1 %collective-permute-start.7 = (f32[4,24]{1,0:T(4,128)S(1)}, f32[4,24]{1,0:T(4,128)S(1)}, u32[]{:S(2)}, u32[]{:S(2)}) collective-permute-start(f32[4,24]{1,0:T(4,128)S(1)} %add.55), channel_id=1, source_target_pairs={{0,64},{32,96},{64,0},{96,32},{1,65},{33,97},{65,1},{97,33},{2,66}... | collective-permute-start | bytes 1160 | tf_op jit(solution)/shard_map/ppermute | solution.py:66
  40.6 1.2 fusion.7
  41.8 0.0 collective-permute-done.7
  41.8 0.6 fusion.16
  42.4 28.5 %all-gather = bf16[32,24,4]{1,2,0:T(4,128)(2,1)S(1)} all-gather(bf16[1,24,4]{1,2,0:T(4,128)(2,1)S(1)} %get-tuple-element.17), channel_id=1, replica_groups=mesh['rep'=4,'shard'=32] {'shard'}, dimensions={0}, use_global_device_ids=true | all-gather | bytes 6336 | tf_op jit(solution)/shard_map/all_gather | solution.py:145
  70.9 0.7 reshape.61
  71.6 2.0 %fusion.21 = (f32[4,24,768]{2,1,0:T(8,128)}, f32[4,3,8,768]{3,2,1,0:T(8,128)S(1)}, f32[4,24,768]{2,1,0:T(8,128)}) fusion(f32[12,24,768]{2,1,0:T(8,128)} %get-tuple-element.20), kind=kLoop, calls=%fused_computation.43 | loop fusion | bytes 1769472 | tf_op jit(solution)/shard_map/slice | solution.py:142
  73.6 0.7 copy.45
  74.3 29.1 %all-gather.3.cloned.1.call-done = bf16[12,768,768]{2,1,0:T(8,128)(2,1)} async-done(((bf16[12,24,768]{2,1,0:T(8,128)(2,1)}), bf16[12,768,768]{2,1,0:T(8,128)(2,1)}) %all-gather.3.cloned.1.call-update) | async-done | bytes 14155792 | tf_op jit(solution)/shard_map/all_gather | solution.py:143
  103.4 10.1 %shard_map.257 = (bf16[4,768,768]{2,1,0:T(8,128)(2,1)}, bf16[768,3072]{1,0:T(8,128)(2,1)}, bf16[3072,768]{1,0:T(8,128)(2,1)}) custom-call(bf16[3,4,768,768]{3,2,1,0:T(8,128)(2,1)} %bitcast.87), custom_call_target="tpu_custom_call" | custom-call | bytes 28311552 | tf_op jit(solution)/shard_map/pallas_call | solution.py:44
  (37 shorter events, 0.1 us)
Async XLA Ops:
  7.2 11.7 %copy-start = (f32[3072,64]{0,1:T(8,128)S(1)}, f32[3072,64]{0,1:T(8,128)}, u32[]{:S(2)}) copy-start(f32[3072,64]{0,1:T(8,128)} %param.34) | copy-start | bytes 2359300
  7.2 10.1 %copy-start.8 = (f32[1,4,24,768]{3,2,1,0:T(8,128)S(1)}, f32[1,4,24,768]{3,2,1,0:T(8,128)}, u32[]{:S(2)}) copy-start(f32[1,4,24,768]{3,2,1,0:T(8,128)} %param.18) | copy-start | bytes 884740
  7.2 10.1 %copy-start.7 = (f32[4,24,768]{2,1,0:T(8,128)S(1)}, f32[4,24,768]{2,1,0:T(8,128)}, u32[]{:S(2)}) copy-start(f32[4,24,768]{2,1,0:T(8,128)} %param.22) | copy-start | bytes 884740
  7.2 10.1 %copy-start.6 = (f32[1,4,24,768]{3,2,1,0:T(8,128)S(1)}, f32[1,4,24,768]{3,2,1,0:T(8,128)}, u32[]{:S(2)}) copy-start(f32[1,4,24,768]{3,2,1,0:T(8,128)} %param.26) | copy-start | bytes 884740
  7.2 10.1 %copy-start.1 = (f32[4,768,64]{1,2,0:T(8,128)S(1)}, f32[4,768,64]{1,2,0:T(8,128)}, u32[]{:S(2)}) copy-start(f32[4,768,64]{1,2,0:T(8,128)} %param.33) | copy-start | bytes 2359300
  7.2 96.2 %all-gather.3.cloned.1.call-start = ((), (), s32[]{:S(2)}) async-start(), calls=%async_computation | async-start | bytes 14598144 | tf_op jit(solution)/shard_map/all_gather | solution.py:143
  9.6 10.3 %copy-start.2 = (f32[24,3072]{1,0:T(8,128)S(1)}, f32[24,3072]{1,0:T(8,128)}, u32[]{:S(2)}) copy-start(f32[24,3072]{1,0:T(8,128)} %param.23) | copy-start | bytes 884740
  9.6 10.3 %copy-start.16 = (f32[24,3072]{1,0:T(8,128)S(1)}, f32[24,3072]{1,0:T(8,128)}, u32[]{:S(2)}) copy-start(f32[24,3072]{1,0:T(8,128)} %param.30) | copy-start | bytes 884740
  9.6 4.3 %collective-permute-start.2 = (f32[24,64]{1,0:T(8,128)S(1)}, f32[24,64]{1,0:T(8,128)S(1)}, u32[]{:S(2)}, u32[]{:S(2)}) collective-permute-start(f32[24,64]{1,0:T(8,128)S(1)} %fusion.19), channel_id=1, source_target_pairs={{0,32},{32,0},{64,96},{96,64},{1,33},{33,1},{65,97},{97,65},{2,34}... | collective-permute-start | bytes 18440 | tf_op jit(solution)/shard_map/ppermute | solution.py:66
  13.7 9.1 %copy-start.14 = (f32[96,64]{0,1:T(8,128)}, f32[96,64]{0,1:T(8,128)S(1)}, u32[]{:S(2)}) copy-start(f32[96,64]{0,1:T(8,128)S(1)} %fusion.20) | copy-start | bytes 73732
  13.7 6.9 %collective-permute-start.4 = (f32[96,64]{0,1:T(8,128)S(1)}, f32[96,64]{0,1:T(8,128)S(1)}, u32[]{:S(2)}, u32[]{:S(2)}) collective-permute-start(f32[96,64]{0,1:T(8,128)S(1)} %fusion.20), channel_id=1, source_target_pairs={{0,32},{32,0},{64,96},{96,64},{1,33},{33,1},{65,97},{97,65},{2,34}... | collective-permute-start | bytes 73736 | tf_op jit(solution)/shard_map/ppermute | solution.py:66
  13.9 15.5 %copy-start.3 = (f32[768,64]{0,1:T(8,128)S(1)}, f32[768,64]{0,1:T(8,128)}, u32[]{:S(2)}) copy-start(f32[768,64]{0,1:T(8,128)} %param.35) | copy-start | bytes 589828
  13.9 7.7 %collective-permute-start.3 = (f32[24,64]{1,0:T(8,128)S(1)}, f32[24,64]{1,0:T(8,128)S(1)}, u32[]{:S(2)}, u32[]{:S(2)}) collective-permute-start(f32[24,64]{1,0:T(8,128)S(1)} %add.50), channel_id=1, source_target_pairs={{0,64},{32,96},{64,0},{96,32},{1,65},{33,97},{65,1},{97,33},{2,66}... | collective-permute-start | bytes 18440 | tf_op jit(solution)/shard_map/ppermute | solution.py:66
  18.1 4.1 %copy-start.13 = (f32[4,24,64]{2,1,0:T(8,128)}, f32[4,24,64]{2,1,0:T(8,128)S(1)}, u32[]{:S(2)}) copy-start(f32[4,24,64]{2,1,0:T(8,128)S(1)} %fusion.18) | copy-start | bytes 73732
  18.1 11.4 %copy-start.10 = (f32[96,768]{1,0:T(8,128)S(1)}, f32[96,768]{1,0:T(8,128)}, u32[]{:S(2)}) copy-start(f32[96,768]{1,0:T(8,128)} %param.24) | copy-start | bytes 884740
  18.1 4.1 %collective-permute-start = (f32[4,24,64]{2,1,0:T(8,128)S(1)}, f32[4,24,64]{2,1,0:T(8,128)S(1)}, u32[]{:S(2)}, u32[]{:S(2)}) collective-permute-start(f32[4,24,64]{2,1,0:T(8,128)S(1)} %fusion.18), channel_id=1, source_target_pairs={{0,32},{32,0},{64,96},{96,64},{1,33},{33,1},{65,97},{97,65},{2,34}... | collective-permute-start | bytes 73736 | tf_op jit(solution)/shard_map/ppermute | solution.py:66
  20.6 4.3 %collective-permute-start.5 = (f32[96,64]{0,1:T(8,128)S(1)}, f32[96,64]{0,1:T(8,128)S(1)}, u32[]{:S(2)}, u32[]{:S(2)}) collective-permute-start(f32[96,64]{0,1:T(8,128)S(1)} %add.52), channel_id=1, source_target_pairs={{0,64},{32,96},{64,0},{96,32},{1,65},{33,97},{65,1},{97,33},{2,66}... | collective-permute-start | bytes 73736 | tf_op jit(solution)/shard_map/ppermute | solution.py:66
  22.9 5.0 %collective-permute-start.1 = (f32[4,24,64]{2,1,0:T(8,128)}, f32[4,24,64]{2,1,0:T(8,128)}, u32[]{:S(2)}, u32[]{:S(2)}) collective-permute-start(f32[4,24,64]{2,1,0:T(8,128)} %add.48), channel_id=1, source_target_pairs={{0,64},{32,96},{64,0},{96,32},{1,65},{33,97},{65,1},{97,33},{2,66}... | collective-permute-start | bytes 73736 | tf_op jit(solution)/shard_map/ppermute | solution.py:66
  29.5 3.9 %copy-start.17 = (f32[4,24]{1,0:T(4,128)S(1)}, f32[4,24]{1,0:T(4,128)}, u32[]{:S(2)}) copy-start(f32[4,24]{1,0:T(4,128)} %param.25) | copy-start | bytes 1156
  33.3 2.9 %copy-start.4 = (f32[1,24,3072]{2,1,0:T(8,128)S(1)}, f32[1,24,3072]{2,1,0:T(8,128)}, u32[]{:S(2)}) copy-start(f32[1,24,3072]{2,1,0:T(8,128)} %param.27) | copy-start | bytes 884740
  33.3 2.9 %copy-start.5 = (f32[1,24,3072]{2,1,0:T(8,128)S(1)}, f32[1,24,3072]{2,1,0:T(8,128)}, u32[]{:S(2)}) copy-start(f32[1,24,3072]{2,1,0:T(8,128)} %param.19) | copy-start | bytes 884740
  33.4 7.2 %copy-start.9 = (f32[1,96,768]{2,1,0:T(8,128)S(1)}, f32[1,96,768]{2,1,0:T(8,128)}, u32[]{:S(2)}) copy-start(f32[1,96,768]{2,1,0:T(8,128)} %param.28) | copy-start | bytes 884740
  33.4 7.2 %copy-start.11 = (f32[96,768]{1,0:T(8,128)S(1)}, f32[96,768]{1,0:T(8,128)}, u32[]{:S(2)}) copy-start(f32[96,768]{1,0:T(8,128)} %param.24) | copy-start | bytes 884740
  33.4 7.2 %copy-start.12 = (f32[1,96,768]{2,1,0:T(8,128)S(1)}, f32[1,96,768]{2,1,0:T(8,128)}, u32[]{:S(2)}) copy-start(f32[1,96,768]{2,1,0:T(8,128)} %param.20) | copy-start | bytes 884740
  33.4 7.2 %copy-start.15 = (f32[96,64]{0,1:T(8,128)S(1)}, f32[96,64]{0,1:T(8,128)}, u32[]{:S(2)}) copy-start(f32[96,64]{0,1:T(8,128)} %copy-done.14) | copy-start | bytes 73732
  34.2 7.6 %copy-start.18 = (f32[4,24]{1,0:T(4,128)S(1)}, f32[4,24]{1,0:T(4,128)}, u32[]{:S(2)}) copy-start(f32[4,24]{1,0:T(4,128)} %param.32) | copy-start | bytes 1156
  34.2 3.3 %collective-permute-start.6 = (f32[4,24]{1,0:T(4,128)S(1)}, f32[4,24]{1,0:T(4,128)S(1)}, u32[]{:S(2)}, u32[]{:S(2)}) collective-permute-start(f32[4,24]{1,0:T(4,128)S(1)} %bitcast_subtract_fusion.3), channel_id=1, source_target_pairs={{0,32},{32,0},{64,96},{96,64},{1,33},{33,1},{65,97},{97,65},{2,34}... | collective-permute-start | bytes 1160 | tf_op jit(solution)/shard_map/ppermute | solution.py:66
  37.5 4.3 %collective-permute-start.7 = (f32[4,24]{1,0:T(4,128)S(1)}, f32[4,24]{1,0:T(4,128)S(1)}, u32[]{:S(2)}, u32[]{:S(2)}) collective-permute-start(f32[4,24]{1,0:T(4,128)S(1)} %add.55), channel_id=1, source_target_pairs={{0,64},{32,96},{64,0},{96,32},{1,65},{33,97},{65,1},{97,33},{2,66}... | collective-permute-start | bytes 1160 | tf_op jit(solution)/shard_map/ppermute | solution.py:66
Sparse Core Ops, SparseCore 0:
  33.5 69.8 all-gather.2

commit v4 on v3

--- a/solution.py
+++ b/solution.py
@@ -107,11 +107,17 @@
         "rk,dk->rd", factor_down, basis_down, precision=highest
     )
     norm_delta = start_ln - trained_ln[0]
-    summed = rep_sum((factor_sq, factor_up, factor_down, norm_delta))
-    mean_sq = summed[0] / groups
-    mean_up = summed[1] / groups
-    mean_down = summed[2] / groups
-    mean_ln = summed[3] / groups
+    norm_flat = norm_delta.reshape(-1)
+    norm_rows = -(-norm_flat.shape[0] // rank)
+    norm_pad = jnp.pad(norm_flat, (0, norm_rows * rank - norm_flat.shape[0]))
+    parts = [factor_sq.reshape(-1, rank), factor_up, factor_down, norm_pad.reshape(norm_rows, rank)]
+    summed = rep_sum(jnp.concatenate(parts)) / groups
+    cuts = [p.shape[0] for p in parts]
+    at = [sum(cuts[:i]) for i in range(len(cuts))]
+    mean_sq = summed[at[0] : at[1]].reshape(factor_sq.shape)
+    mean_up = summed[at[1] : at[2]]
+    mean_down = summed[at[2] : at[3]]
+    mean_ln = summed[at[3] :].reshape(-1)[: norm_flat.shape[0]].reshape(norm_delta.shape)
     new_mom_ln, norm_weights = advance(start_ln, mom_ln, mean_ln)
     blocks_up = start_up.shape[1] // width
     blocks_down = start_down.shape[0] // rows
@@ -140,6 +146,7 @@
     new_mom_sq = new_mom_all[:square]
     new_mom_up = join_cols(new_mom_all[square : square + blocks_up])
     new_mom_down = new_mom_all[square + blocks_up :].reshape(-1, width)
+    owned_all, norm_weights = lax.optimization_barrier((owned_all, norm_weights))
     gathered = lax.all_gather(owned_all, "shard", axis=1, tiled=True)
     weights_sq, weights_up, weights_down = unpack(gathered, rows)
     weights_ln = lax.all_gather(norm_weights, "shard", axis=1, tiled=True)

time: 121 us -> 118 us (0.975)
  waiting for transfers between devices: 30 us -> 38.8 us
  starting transfers between devices: 13.2 us -> 6.08 us
  other arithmetic: 4.06 us -> 0.84 us
  blocking collectives: 28.5 us -> 26.4 us
    all_gather x1, waiting for transfers between devices: 29.1 us -> 37.1 us  [on_device(): gathered = lax.all_gather(owned_all, 'shard', axis=1, tiled=True)]
    ppermute x8 -> x2, starting transfers between devices: 13.1 us -> 6.04 us  [rep_sum(): other = lax.ppermute(parts, 'rep', [(i, i ^ step) for i in range(n)])]
    all_gather x1, blocking collectives: 28.5 us -> 26.4 us  [on_device(): weights_ln = lax.all_gather(norm_weights, 'shard', axis=1, tiled=True)]
    div x3 -> x1, other arithmetic: 2.06 us -> 0.01 us  [on_device(): summed = rep_sum(jnp.concatenate(parts)) / groups]
    slice x0 -> x7, local copies, waits for them, and re-layouts: none -> 1.79 us  [the longest x2 0.8 us: on_device(): mean_sq = summed[at[0]:at[1]].reshape(factor_sq.shape)]
    dot_general x1, matrix products: 0.75 us -> 2.28 us  [on_device(): jnp.einsum('mrd,mdk->mrk', delta_sq, basis_sq, precision=highest)]
    div x1 -> x0, local copies, waits for them, and re-layouts: 1.47 us -> none  [on_device(): mean_down = summed[2] / groups]
  transfers between devices with their start and end apart: 9 -> 3, of which waited for: 3 -> 2; matrix products, arithmetic and copies ran while one was open for 14% -> 8% of each run, Pallas kernels for 0% -> 0%
where the time goes in v4:
time: 118 us
  waiting for transfers between devices  38.8 us (33%)
  blocking collectives  26.4 us (22%)
  between operations  14.3 us (12%)
  matrix products  13.4 us (11%)
  Pallas kernels  10.1 us (9%)
  local copies, waits for them, and re-layouts  7.88 us (7%)
  starting transfers between devices  6.08 us (5%)
    all_gather x1, waiting for transfers between devices, on_device(): gathered = lax.all_gather(owned_all, 'shard', axis=1, tiled=True)  37.1 us
    all_gather x1, blocking collectives, on_device(): weights_ln = lax.all_gather(norm_weights, 'shard', axis=1, tiled=True)  26.4 us
    pallas_call x1, Pallas kernels, unpack(): pl.pallas_call(functools.partial(unpack_kernel, rows), grid=(total // ste...  10.1 us
    ppermute x2, starting transfers between devices, rep_sum(): other = lax.ppermute(parts, 'rep', [(i, i ^ step) for i in range(n)])  6.04 us
    dot_general x1, matrix products, on_device(): jnp.einsum('brk,bdk->brd', mean_all, basis_all, precision=highest)  4.09 us
  transfers between devices with their start and end apart: 3, of which 2 were waited for; matrix products, arithmetic and copies ran while one was open for 8% of the time, Pallas kernels for 0%

profile of v4, /device:TPU:1, one launch (start us, length us, event | category | flops | bytes accessed | tf_op | source)
XLA Modules:
  0.0 117.7 jit_solution(8781717846825657459)
XLA Ops:
  7.2 0.0 copy-start
  7.3 0.0 all-gather.3.cloned.1.call-start
  7.3 2.3 %fusion.17 = f32[4,24,64]{2,1,0:T(8,128)S(1)} fusion(f32[4,768,64]{1,2,0:T(8,128)} %param.33, f32[1,4,24,768]{3,2,1,0:T(8,128)} %param.26, f32[4,24,768]{2,1,0:T(8,128)} %param.22, f32[1,4,24,768]{3,2,1,0:T(8,128)} %param.18), kind=kOutput, calls=%fused_computation.37 | convolution fusion | flops 56770560 | bytes 1695744 | tf_op jit(solution)/shard_map/mrd,mdk->mrk/dot_general | solution.py:97
  9.6 0.0 copy-start.14
  9.6 0.6 copy-done.14
  10.2 0.1 copy.49
  10.3 0.0 copy-start.2
  10.3 0.0 copy-start.16
  10.3 2.2 %fusion.18 = f32[24,64]{1,0:T(8,128)S(1)} fusion(f32[3072,64]{0,1:T(8,128)} %param.34, f32[1,24,3072]{2,1,0:T(8,128)} %param.27, f32[24,3072]{1,0:T(8,128)} %param.23, f32[1,24,3072]{2,1,0:T(8,128)} %param.19), kind=kOutput, calls=%fused_computation.38 | convolution fusion | flops 56770560 | bytes 1677312 | tf_op jit(solution)/shard_map/dot_general | solution.py:100
  12.5 0.1 copy.50
  12.6 0.1 reshape.72
  12.7 0.1 reshape.73
  12.8 0.1 copy.51
  12.9 0.4 fusion.19
  13.3 0.0 copy-start.13
  13.3 0.1 pad_maximum_fusion
  13.5 0.0 copy-start.1
  13.5 2.5 %collective-permute-start = (f32[218,64]{0,1:T(8,128)S(1)}, f32[218,64]{0,1:T(8,128)S(1)}, u32[]{:S(2)}, u32[]{:S(2)}) collective-permute-start(f32[218,64]{0,1:T(8,128)S(1)} %pad_maximum_fusion), channel_id=1, source_target_pairs={{0,32},{32,0},{64,96},{96,64},{1,33},{33,1},{65,97},{97,65},{2,34}... | collective-permute-start | bytes 167432 | tf_op jit(solution)/shard_map/ppermute | solution.py:66
  16.0 1.7 %collective-permute-done = f32[218,64]{0,1:T(8,128)S(1)} collective-permute-done((f32[218,64]{0,1:T(8,128)S(1)}, f32[218,64]{0,1:T(8,128)S(1)}, u32[]{:S(2)}, u32[]{:S(2)}) %collective-permute-start) | collective-permute-done | bytes 55840 | tf_op jit(solution)/shard_map/ppermute | solution.py:66
  17.7 0.1 fusion.31
  17.8 3.5 %collective-permute-start.1 = (f32[218,64]{0,1:T(8,128)S(1)}, f32[218,64]{0,1:T(8,128)S(1)}, u32[]{:S(2)}, u32[]{:S(2)}) collective-permute-start(f32[218,64]{0,1:T(8,128)S(1)} %fusion.31), channel_id=1, source_target_pairs={{0,64},{32,96},{64,0},{96,32},{1,65},{33,97},{65,1},{97,33},{2,66}... | collective-permute-start | bytes 167432 | tf_op jit(solution)/shard_map/ppermute | solution.py:66
  21.3 0.9 copy.67
  22.2 0.7 copy.68
  23.0 0.7 copy.69
  23.7 0.1 fusion.21
  23.8 0.1 slice.33
  23.9 0.1 slice.38
  23.9 0.7 copy.52
  24.7 0.7 copy.54
  25.4 0.1 copy.53
  25.4 0.1 copy.57
  25.5 0.1 reshape.79
  25.6 0.1 reshape.80
  25.7 0.6 subtract_convert_fusion
  26.3 0.1 broadcast_in_dim.25
  26.4 0.0 copy-start.5
  26.4 4.1 %fusion.10 = (bf16[12,24,768]{2,1,0:T(8,128)(2,1)}, f32[12,24,768]{2,1,0:T(8,128)}) fusion(f32[4,24,768]{2,1,0:T(8,128)S(1)} %bitcast.92, f32[4,24,768]{2,1,0:T(8,128)} %bitcast.98, f32[4,24,768]{2,1,0:T(8,128)} %param.22, f32[4,24,768]{2,1,0:T(8,128)} %bitcast.105, f32[4,24,768]{2,1,0:T(8,128)} %bitcast.99, f32[4,24,768]{2,1,0:T(8,128)} %param.29, ...), kind=kOutput, calls=%fused_computation.15 | convolution fusion | flops 173518848 | bytes 5529600 | tf_op jit(solution)/shard_map/brk,bdk->brd/dot_general | solution.py:144
  30.5 0.0 all-gather.3.cloned.1.call-update
  30.5 0.0 copy-start.11
  30.6 2.0 %fusion.7 = f32[1,96,768]{2,1,0:T(8,128)} fusion(f32[96,64]{0,1:T(8,128)} %copy-done.13, f32[768,64]{0,1:T(8,128)S(1)} %copy-done.3, f32[1,96,768]{2,1,0:T(8,128)S(1)} %copy-done.6, f32[96,768]{1,0:T(8,128)S(1)} %copy-done.7, f32[1,96,768]{2,1,0:T(8,128)S(1)} %copy-done.8), kind=kOutput, calls=%fused_computation.9 | convolution fusion | flops 56844288 | bytes 1400832 | tf_op jit(solution)/shard_map/rk,dk->rd/dot_general | solution.py:106
  32.5 1.2 %fusion = f32[1,24,3072]{2,1,0:T(8,128)} fusion(f32[24,64]{1,0:T(8,128)S(1)} %fusion.18, f32[3072,64]{0,1:T(8,128)S(1)} %copy-done, f32[1,24,3072]{2,1,0:T(8,128)S(1)} %copy-done.4, f32[24,3072]{1,0:T(8,128)S(1)} %copy-done.2, f32[1,24,3072]{2,1,0:T(8,128)S(1)} %copy-done.5), kind=kOutput, calls=%fused_computation.1 | convolution fusion | flops 56844288 | bytes 1972224 | tf_op jit(solution)/shard_map/rk,fk->rf/dot_general | solution.py:101
  33.8 1.2 %fusion.8 = f32[1,4,24,768]{3,2,1,0:T(8,128)} fusion(f32[4,24,64]{2,1,0:T(8,128)S(1)} %copy-done.15, f32[4,768,64]{1,2,0:T(8,128)S(1)} %copy-done.1, f32[1,4,24,768]{3,2,1,0:T(8,128)S(1)} %copy-done.9, f32[4,24,768]{2,1,0:T(8,128)S(1)} %copy-done.10, f32[1,4,24,768]{3,2,1,0:T(8,128)S(1)} %copy-done.11), kind=kOutput, calls=%fused_computation.11 | convolution fusion | flops 56844288 | bytes 1990656 | tf_op jit(solution)/shard_map/mrk,mdk->mrd/dot_general | solution.py:98
  35.0 26.4 %all-gather = bf16[32,24,4]{1,2,0:T(4,128)(2,1)S(1)} all-gather(bf16[1,24,4]{1,2,0:T(4,128)(2,1)S(1)} %bitcast.103), channel_id=1, replica_groups=mesh['rep'=4,'shard'=32] {'shard'}, dimensions={0}, use_global_device_ids=true | all-gather | bytes 6336 | tf_op jit(solution)/shard_map/all_gather | solution.py:152
  61.4 0.7 reshape.85
  62.1 0.9 fusion.20
  63.0 0.7 copy.63
  63.7 37.1 %all-gather.3.cloned.1.call-done = bf16[12,768,768]{2,1,0:T(8,128)(2,1)} async-done(((bf16[12,24,768]{2,1,0:T(8,128)(2,1)}), bf16[12,768,768]{2,1,0:T(8,128)(2,1)}) %all-gather.3.cloned.1.call-update) | async-done | bytes 14155792 | tf_op jit(solution)/shard_map/all_gather | solution.py:150
  100.8 10.1 %shard_map.257 = (bf16[4,768,768]{2,1,0:T(8,128)(2,1)}, bf16[768,3072]{1,0:T(8,128)(2,1)}, bf16[3072,768]{1,0:T(8,128)(2,1)}) custom-call(bf16[3,4,768,768]{3,2,1,0:T(8,128)(2,1)} %bitcast.89), custom_call_target="tpu_custom_call" | custom-call | bytes 28311552 | tf_op jit(solution)/shard_map/pallas_call | solution.py:44
  (37 shorter events, 0.1 us)
Async XLA Ops:
  7.2 14.1 %copy-start = (f32[3072,64]{0,1:T(8,128)S(1)}, f32[3072,64]{0,1:T(8,128)}, u32[]{:S(2)}) copy-start(f32[3072,64]{0,1:T(8,128)} %param.34) | copy-start | bytes 2359300
  7.2 5.4 %copy-start.18 = (f32[1,4,24]{2,1,0:T(4,128)S(1)}, f32[1,4,24]{2,1,0:T(4,128)}, u32[]{:S(2)}) copy-start(f32[1,4,24]{2,1,0:T(4,128)} %param.21) | copy-start | bytes 1156
  7.2 5.4 %copy-start.17 = (f32[4,24]{1,0:T(4,128)S(1)}, f32[4,24]{1,0:T(4,128)}, u32[]{:S(2)}) copy-start(f32[4,24]{1,0:T(4,128)} %param.25) | copy-start | bytes 1156
  7.2 5.7 %copy-start.8 = (f32[1,96,768]{2,1,0:T(8,128)S(1)}, f32[1,96,768]{2,1,0:T(8,128)}, u32[]{:S(2)}) copy-start(f32[1,96,768]{2,1,0:T(8,128)} %param.20) | copy-start | bytes 884740
  7.2 5.7 %copy-start.7 = (f32[96,768]{1,0:T(8,128)S(1)}, f32[96,768]{1,0:T(8,128)}, u32[]{:S(2)}) copy-start(f32[96,768]{1,0:T(8,128)} %param.24) | copy-start | bytes 884740
  7.2 5.7 %copy-start.6 = (f32[1,96,768]{2,1,0:T(8,128)S(1)}, f32[1,96,768]{2,1,0:T(8,128)}, u32[]{:S(2)}) copy-start(f32[1,96,768]{2,1,0:T(8,128)} %param.28) | copy-start | bytes 884740
  7.2 5.7 %copy-start.3 = (f32[768,64]{0,1:T(8,128)S(1)}, f32[768,64]{0,1:T(8,128)}, u32[]{:S(2)}) copy-start(f32[768,64]{0,1:T(8,128)} %param.35) | copy-start | bytes 589828
  7.3 93.5 %all-gather.3.cloned.1.call-start = ((), (), s32[]{:S(2)}) async-start(), calls=%async_computation | async-start | bytes 14598144 | tf_op jit(solution)/shard_map/all_gather | solution.py:150
  9.6 0.6 copy-start.14
  10.3 12.0 %copy-start.2 = (f32[24,3072]{1,0:T(8,128)S(1)}, f32[24,3072]{1,0:T(8,128)}, u32[]{:S(2)}) copy-start(f32[24,3072]{1,0:T(8,128)} %param.23) | copy-start | bytes 884740
  10.3 12.7 %copy-start.16 = (f32[24,3072]{1,0:T(8,128)S(1)}, f32[24,3072]{1,0:T(8,128)}, u32[]{:S(2)}) copy-start(f32[24,3072]{1,0:T(8,128)} %param.30) | copy-start | bytes 884740
  12.9 12.8 %copy-start.19 = (f32[4,24]{1,0:T(4,128)S(1)}, f32[4,24]{1,0:T(4,128)}, u32[]{:S(2)}) copy-start(f32[4,24]{1,0:T(4,128)} %param.32) | copy-start | bytes 1156
  13.3 10.6 %copy-start.13 = (f32[96,64]{0,1:T(8,128)}, f32[96,64]{0,1:T(8,128)S(1)}, u32[]{:S(2)}) copy-start(f32[96,64]{0,1:T(8,128)S(1)} %fusion.19) | copy-start | bytes 73732
  13.5 12.9 %copy-start.1 = (f32[4,768,64]{1,2,0:T(8,128)S(1)}, f32[4,768,64]{1,2,0:T(8,128)}, u32[]{:S(2)}) copy-start(f32[4,768,64]{1,2,0:T(8,128)} %param.33) | copy-start | bytes 2359300
  13.5 4.2 %collective-permute-start = (f32[218,64]{0,1:T(8,128)S(1)}, f32[218,64]{0,1:T(8,128)S(1)}, u32[]{:S(2)}, u32[]{:S(2)}) collective-permute-start(f32[218,64]{0,1:T(8,128)S(1)} %pad_maximum_fusion), channel_id=1, source_target_pairs={{0,32},{32,0},{64,96},{96,64},{1,33},{33,1},{65,97},{97,65},{2,34}... | collective-permute-start | bytes 167432 | tf_op jit(solution)/shard_map/ppermute | solution.py:66
  17.8 5.9 %collective-permute-start.1 = (f32[218,64]{0,1:T(8,128)S(1)}, f32[218,64]{0,1:T(8,128)S(1)}, u32[]{:S(2)}, u32[]{:S(2)}) collective-permute-start(f32[218,64]{0,1:T(8,128)S(1)} %fusion.31), channel_id=1, source_target_pairs={{0,64},{32,96},{64,0},{96,32},{1,65},{33,97},{65,1},{97,33},{2,66}... | collective-permute-start | bytes 167432 | tf_op jit(solution)/shard_map/ppermute | solution.py:66
  26.4 6.2 %copy-start.4 = (f32[1,24,3072]{2,1,0:T(8,128)S(1)}, f32[1,24,3072]{2,1,0:T(8,128)}, u32[]{:S(2)}) copy-start(f32[1,24,3072]{2,1,0:T(8,128)} %param.27) | copy-start | bytes 884740
  26.4 6.2 %copy-start.5 = (f32[1,24,3072]{2,1,0:T(8,128)S(1)}, f32[1,24,3072]{2,1,0:T(8,128)}, u32[]{:S(2)}) copy-start(f32[1,24,3072]{2,1,0:T(8,128)} %param.19) | copy-start | bytes 884740
  30.5 3.3 %copy-start.9 = (f32[1,4,24,768]{3,2,1,0:T(8,128)S(1)}, f32[1,4,24,768]{3,2,1,0:T(8,128)}, u32[]{:S(2)}) copy-start(f32[1,4,24,768]{3,2,1,0:T(8,128)} %param.26) | copy-start | bytes 884740
  30.5 3.3 %copy-start.10 = (f32[4,24,768]{2,1,0:T(8,128)S(1)}, f32[4,24,768]{2,1,0:T(8,128)}, u32[]{:S(2)}) copy-start(f32[4,24,768]{2,1,0:T(8,128)} %param.22) | copy-start | bytes 884740
  30.5 3.2 %copy-start.11 = (f32[1,4,24,768]{3,2,1,0:T(8,128)S(1)}, f32[1,4,24,768]{3,2,1,0:T(8,128)}, u32[]{:S(2)}) copy-start(f32[1,4,24,768]{3,2,1,0:T(8,128)} %param.18) | copy-start | bytes 884740
  30.5 3.2 %copy-start.15 = (f32[4,24,64]{2,1,0:T(8,128)S(1)}, f32[4,24,64]{2,1,0:T(8,128)}, u32[]{:S(2)}) copy-start(f32[4,24,64]{2,1,0:T(8,128)} %copy-done.14) | copy-start | bytes 73732
  32.5 29.5 %copy-start.12 = (f32[12,24,768]{2,1,0:T(8,128)S(1)}, f32[12,24,768]{2,1,0:T(8,128)}, u32[]{:S(2)}) copy-start(f32[12,24,768]{2,1,0:T(8,128)} %get-tuple-element.24) | copy-start | bytes 2654212
Sparse Core Ops, SparseCore 0:
  30.6 70.1 all-gather.2

commit v5 on v4

--- a/solution.py
+++ b/solution.py
@@ -61,12 +61,15 @@
 
 def rep_sum(parts):
     n = lax.axis_size("rep")
-    step = 1
-    while step < n:
-        other = lax.ppermute(parts, "rep", [(i, i ^ step) for i in range(n)])
-        parts = jax.tree.map(jnp.add, parts, other)
-        step *= 2
-    return parts
+    me = lax.axis_index("rep")
+    held = [parts] + [
+        lax.ppermute(parts, "rep", [(i, (i + d) % n) for i in range(n)]) for d in range(1, n)
+    ]
+    stack = jnp.stack(held)
+    by_index = [lax.dynamic_index_in_dim(stack, (me - k) % n, keepdims=False) for k in range(n)]
+    while len(by_index) > 1:
+        by_index = [a + b for a, b in zip(by_index[::2], by_index[1::2])]
+    return by_index[0]
 
 
 def on_device(
@@ -118,7 +121,6 @@
     mean_up = summed[at[1] : at[2]]
     mean_down = summed[at[2] : at[3]]
     mean_ln = summed[at[3] :].reshape(-1)[: norm_flat.shape[0]].reshape(norm_delta.shape)
-    new_mom_ln, norm_weights = advance(start_ln, mom_ln, mean_ln)
     blocks_up = start_up.shape[1] // width
     blocks_down = start_down.shape[0] // rows
     start_all = jnp.concatenate(
@@ -146,7 +148,8 @@
     new_mom_sq = new_mom_all[:square]
     new_mom_up = join_cols(new_mom_all[square : square + blocks_up])
     new_mom_down = new_mom_all[square + blocks_up :].reshape(-1, width)
-    owned_all, norm_weights = lax.optimization_barrier((owned_all, norm_weights))
+    owned_all, mean_ln = lax.optimization_barrier((owned_all, mean_ln))
+    new_mom_ln, norm_weights = advance(start_ln, mom_ln, mean_ln)
     gathered = lax.all_gather(owned_all, "shard", axis=1, tiled=True)
     weights_sq, weights_up, weights_down = unpack(gathered, rows)
     weights_ln = lax.all_gather(norm_weights, "shard", axis=1, tiled=True)

time: 118 us -> 117 us (level)
  waiting for transfers between devices: 38.8 us -> 35.3 us
    all_gather x1, waiting for transfers between devices: 37.1 us -> 35.2 us  [on_device(): gathered = lax.all_gather(owned_all, 'shard', axis=1, tiled=True)]
    ppermute x2 -> x3, waiting for transfers between devices: 1.66 us -> 0.06 us  [rep_sum(): lax.ppermute(parts, 'rep', [(i, (i + d) % n) for i in range(n)])]
    ppermute x2 -> x3, starting transfers between devices: 6.04 us -> 6.57 us  [rep_sum(): lax.ppermute(parts, 'rep', [(i, (i + d) % n) for i in range(n)])]
  transfers between devices with their start and end apart: 3 -> 4, of which waited for: 2 -> 1; matrix products, arithmetic and copies ran while one was open for 8% -> 8% of each run, Pallas kernels for 0% -> 0%
where the time goes in v5:
time: 117 us; the launch traced here: 116 us
  waiting for transfers between devices  35.3 us (30%)
  blocking collectives  26.5 us (23%)
  between operations  14.4 us (12%)
  matrix products  13.4 us (11%)
  Pallas kernels  10.1 us (9%)
  local copies, waits for them, and re-layouts  8.49 us (7%)
  starting transfers between devices  6.6 us (6%)
  other arithmetic  1.69 us (1%)
    all_gather x1, waiting for transfers between devices, on_device(): gathered = lax.all_gather(owned_all, 'shard', axis=1, tiled=True)  35.2 us
    all_gather x1, blocking collectives, on_device(): weights_ln = lax.all_gather(norm_weights, 'shard', axis=1, tiled=True)  26.5 us
    pallas_call x1, Pallas kernels, unpack(): pl.pallas_call(functools.partial(unpack_kernel, rows), grid=(total // ste...  10.1 us
    ppermute x3, starting transfers between devices, rep_sum(): lax.ppermute(parts, 'rep', [(i, (i + d) % n) for i in range(n)])  6.57 us
    dot_general x1, matrix products, on_device(): jnp.einsum('brk,bdk->brd', mean_all, basis_all, precision=highest)  4.09 us
  transfers between devices with their start and end apart: 4, of which 1 were waited for; matrix products, arithmetic and copies ran while one was open for 8% of the time, Pallas kernels for 0%

profile of v5, /device:TPU:1, one launch (start us, length us, event | category | flops | bytes accessed | tf_op | source)
XLA Modules:
  0.0 116.4 jit_solution(14791078268970977836)
XLA Ops:
  7.2 0.0 copy-start
  7.3 0.0 all-gather.3.cloned.1.call-start
  7.3 2.3 %fusion.18 = f32[4,24,64]{2,1,0:T(8,128)S(1)} fusion(f32[4,768,64]{1,2,0:T(8,128)} %param.33, f32[1,4,24,768]{3,2,1,0:T(8,128)} %param.26, f32[4,24,768]{2,1,0:T(8,128)} %param.22, f32[1,4,24,768]{3,2,1,0:T(8,128)} %param.18), kind=kOutput, calls=%fused_computation.40 | convolution fusion | flops 56770560 | bytes 1695744 | tf_op jit(solution)/shard_map/mrd,mdk->mrk/dot_general | solution.py:100
  9.6 0.0 copy-start.14
  9.6 0.6 copy-done.14
  10.2 0.1 copy.49
  10.3 0.0 copy-start.2
  10.3 2.2 %fusion.19 = f32[24,64]{1,0:T(8,128)S(1)} fusion(f32[3072,64]{0,1:T(8,128)} %param.34, f32[1,24,3072]{2,1,0:T(8,128)} %param.27, f32[24,3072]{1,0:T(8,128)} %param.23, f32[1,24,3072]{2,1,0:T(8,128)} %param.19), kind=kOutput, calls=%fused_computation.41 | convolution fusion | flops 56770560 | bytes 1677312 | tf_op jit(solution)/shard_map/dot_general | solution.py:103
  12.5 0.0 copy-start.16
  12.5 0.1 copy.50
  12.6 0.1 reshape.84
  12.7 0.1 reshape.85
  12.8 0.1 copy.51
  12.9 0.4 fusion.20
  13.3 0.1 pad_maximum_fusion.1
  13.4 2.5 %collective-permute-start = (f32[218,64]{0,1:T(8,128)S(1)}, f32[218,64]{0,1:T(8,128)S(1)}, u32[]{:S(2)}, u32[]{:S(2)}) collective-permute-start(f32[218,64]{0,1:T(8,128)S(1)} %pad_maximum_fusion.1), channel_id=1, source_target_pairs={{0,32},{32,64},{64,96},{96,0},{1,33},{33,65},{65,97},{97,1},{2,34}... | collective-permute-start | bytes 167432 | tf_op jit(solution)/shard_map/ppermute | solution.py:66
  16.0 3.3 %collective-permute-start.1 = (f32[218,64]{0,1:T(8,128)S(1)}, f32[218,64]{0,1:T(8,128)S(1)}, u32[]{:S(2)}, u32[]{:S(2)}) collective-permute-start(f32[218,64]{0,1:T(8,128)S(1)} %pad_maximum_fusion.1), channel_id=1, source_target_pairs={{0,64},{32,96},{64,0},{96,32},{1,65},{33,97},{65,1},{97,33},{2,66}... | collective-permute-start | bytes 167432 | tf_op jit(solution)/shard_map/ppermute | solution.py:66
  19.3 0.7 collective-permute-start.2
  20.0 0.1 fusion.32
  20.2 0.0 copy-start.1
  20.2 0.9 copy.67
  21.2 0.7 copy.68
  21.9 0.7 copy.69
  22.6 0.1 collective-permute-done.2
  22.7 0.9 pad_maximum_fusion
  23.6 0.1 fusion.22
  23.6 0.1 slice_bitcast_fusion.1
  23.7 0.1 slice.45
  23.8 0.7 copy.52
  24.5 0.7 copy.54
  25.2 0.1 copy.53
  25.3 0.1 copy.58
  25.4 0.1 reshape.93
  25.4 0.7 reshape.94
  26.1 0.1 broadcast_in_dim.25
  26.2 0.0 copy-start.5
  26.2 4.1 %fusion.10 = (bf16[12,24,768]{2,1,0:T(8,128)(2,1)}, f32[12,24,768]{2,1,0:T(8,128)}) fusion(f32[4,24,768]{2,1,0:T(8,128)S(1)} %bitcast.100, f32[4,24,768]{2,1,0:T(8,128)} %bitcast.105, f32[4,24,768]{2,1,0:T(8,128)} %param.22, f32[4,24,768]{2,1,0:T(8,128)} %bitcast.114, f32[4,24,768]{2,1,0:T(8,128)} %bitcast.106, f32[4,24,768]{2,1,0:T(8,128)} %param.29, ...), kind=kOutput, calls=%fused_computation.15 | convolution fusion | flops 173518848 | bytes 5529600 | tf_op jit(solution)/shard_map/brk,bdk->brd/dot_general | solution.py:146
  30.3 0.0 all-gather.3.cloned.1.call-update
  30.4 2.0 %fusion.7 = f32[1,96,768]{2,1,0:T(8,128)} fusion(f32[96,64]{0,1:T(8,128)} %copy-done.13, f32[768,64]{0,1:T(8,128)S(1)} %copy-done.3, f32[1,96,768]{2,1,0:T(8,128)S(1)} %copy-done.6, f32[96,768]{1,0:T(8,128)S(1)} %copy-done.7, f32[1,96,768]{2,1,0:T(8,128)S(1)} %copy-done.8), kind=kOutput, calls=%fused_computation.9 | convolution fusion | flops 56844288 | bytes 1400832 | tf_op jit(solution)/shard_map/rk,dk->rd/dot_general | solution.py:109
  32.4 1.2 %fusion = f32[1,24,3072]{2,1,0:T(8,128)} fusion(f32[24,64]{1,0:T(8,128)S(1)} %fusion.19, f32[3072,64]{0,1:T(8,128)S(1)} %copy-done, f32[1,24,3072]{2,1,0:T(8,128)S(1)} %copy-done.4, f32[24,3072]{1,0:T(8,128)S(1)} %copy-done.2, f32[1,24,3072]{2,1,0:T(8,128)S(1)} %copy-done.5), kind=kOutput, calls=%fused_computation.1 | convolution fusion | flops 56844288 | bytes 1972224 | tf_op jit(solution)/shard_map/rk,fk->rf/dot_general | solution.py:104
  33.6 1.2 %fusion.8 = f32[1,4,24,768]{3,2,1,0:T(8,128)} fusion(f32[4,24,64]{2,1,0:T(8,128)S(1)} %copy-done.15, f32[4,768,64]{1,2,0:T(8,128)S(1)} %copy-done.1, f32[1,4,24,768]{3,2,1,0:T(8,128)S(1)} %copy-done.9, f32[4,24,768]{2,1,0:T(8,128)S(1)} %copy-done.10, f32[1,4,24,768]{3,2,1,0:T(8,128)S(1)} %copy-done.11), kind=kOutput, calls=%fused_computation.11 | convolution fusion | flops 56844288 | bytes 1990656 | tf_op jit(solution)/shard_map/mrk,mdk->mrd/dot_general | solution.py:101
  34.9 0.6 fusion.16
  35.5 26.5 %all-gather = bf16[32,24,4]{1,2,0:T(4,128)(2,1)S(1)} all-gather(bf16[1,24,4]{1,2,0:T(4,128)(2,1)S(1)} %get-tuple-element.21), channel_id=1, replica_groups=mesh['rep'=4,'shard'=32] {'shard'}, dimensions={0}, use_global_device_ids=true | all-gather | bytes 6336 | tf_op jit(solution)/shard_map/all_gather | solution.py:155
  61.9 0.7 reshape.97
  62.6 0.9 fusion.21
  63.5 0.7 copy.63
  64.2 35.2 %all-gather.3.cloned.1.call-done = bf16[12,768,768]{2,1,0:T(8,128)(2,1)} async-done(((bf16[12,24,768]{2,1,0:T(8,128)(2,1)}), bf16[12,768,768]{2,1,0:T(8,128)(2,1)}) %all-gather.3.cloned.1.call-update) | async-done | bytes 14155792 | tf_op jit(solution)/shard_map/all_gather | solution.py:153
  99.4 10.1 %shard_map.257 = (bf16[4,768,768]{2,1,0:T(8,128)(2,1)}, bf16[768,3072]{1,0:T(8,128)(2,1)}, bf16[3072,768]{1,0:T(8,128)(2,1)}) custom-call(bf16[3,4,768,768]{3,2,1,0:T(8,128)(2,1)} %bitcast.97), custom_call_target="tpu_custom_call" | custom-call | bytes 28311552 | tf_op jit(solution)/shard_map/pallas_call | solution.py:44
  (42 shorter events, 0.1 us)
Async XLA Ops:
  7.2 13.0 %copy-start = (f32[3072,64]{0,1:T(8,128)S(1)}, f32[3072,64]{0,1:T(8,128)}, u32[]{:S(2)}) copy-start(f32[3072,64]{0,1:T(8,128)} %param.34) | copy-start | bytes 2359300
  7.2 5.4 %copy-start.19 = (f32[1,4,24]{2,1,0:T(4,128)S(1)}, f32[1,4,24]{2,1,0:T(4,128)}, u32[]{:S(2)}) copy-start(f32[1,4,24]{2,1,0:T(4,128)} %param.21) | copy-start | bytes 1156
  7.2 5.4 %copy-start.17 = (f32[4,24]{1,0:T(4,128)S(1)}, f32[4,24]{1,0:T(4,128)}, u32[]{:S(2)}) copy-start(f32[4,24]{1,0:T(4,128)} %param.25) | copy-start | bytes 1156
  7.2 5.7 %copy-start.8 = (f32[1,96,768]{2,1,0:T(8,128)S(1)}, f32[1,96,768]{2,1,0:T(8,128)}, u32[]{:S(2)}) copy-start(f32[1,96,768]{2,1,0:T(8,128)} %param.20) | copy-start | bytes 884740
  7.2 5.7 %copy-start.7 = (f32[96,768]{1,0:T(8,128)S(1)}, f32[96,768]{1,0:T(8,128)}, u32[]{:S(2)}) copy-start(f32[96,768]{1,0:T(8,128)} %param.24) | copy-start | bytes 884740
  7.2 5.7 %copy-start.6 = (f32[1,96,768]{2,1,0:T(8,128)S(1)}, f32[1,96,768]{2,1,0:T(8,128)}, u32[]{:S(2)}) copy-start(f32[1,96,768]{2,1,0:T(8,128)} %param.28) | copy-start | bytes 884740
  7.2 5.7 %copy-start.3 = (f32[768,64]{0,1:T(8,128)S(1)}, f32[768,64]{0,1:T(8,128)}, u32[]{:S(2)}) copy-start(f32[768,64]{0,1:T(8,128)} %param.35) | copy-start | bytes 589828
  7.3 92.2 %all-gather.3.cloned.1.call-start = ((), (), s32[]{:S(2)}) async-start(), calls=%async_computation | async-start | bytes 14598144 | tf_op jit(solution)/shard_map/all_gather | solution.py:153
  9.6 0.6 copy-start.14
  10.3 10.9 %copy-start.2 = (f32[24,3072]{1,0:T(8,128)S(1)}, f32[24,3072]{1,0:T(8,128)}, u32[]{:S(2)}) copy-start(f32[24,3072]{1,0:T(8,128)} %param.23) | copy-start | bytes 884740
  12.5 9.4 %copy-start.16 = (f32[24,3072]{1,0:T(8,128)S(1)}, f32[24,3072]{1,0:T(8,128)}, u32[]{:S(2)}) copy-start(f32[24,3072]{1,0:T(8,128)} %param.30) | copy-start | bytes 884740
  13.3 6.7 %copy-start.13 = (f32[96,64]{0,1:T(8,128)}, f32[96,64]{0,1:T(8,128)S(1)}, u32[]{:S(2)}) copy-start(f32[96,64]{0,1:T(8,128)S(1)} %fusion.20) | copy-start | bytes 73732
  13.4 9.2 %collective-permute-start = (f32[218,64]{0,1:T(8,128)S(1)}, f32[218,64]{0,1:T(8,128)S(1)}, u32[]{:S(2)}, u32[]{:S(2)}) collective-permute-start(f32[218,64]{0,1:T(8,128)S(1)} %pad_maximum_fusion.1), channel_id=1, source_target_pairs={{0,32},{32,64},{64,96},{96,0},{1,33},{33,65},{65,97},{97,1},{2,34}... | collective-permute-start | bytes 167432 | tf_op jit(solution)/shard_map/ppermute | solution.py:66
  16.0 6.7 %collective-permute-start.1 = (f32[218,64]{0,1:T(8,128)S(1)}, f32[218,64]{0,1:T(8,128)S(1)}, u32[]{:S(2)}, u32[]{:S(2)}) collective-permute-start(f32[218,64]{0,1:T(8,128)S(1)} %pad_maximum_fusion.1), channel_id=1, source_target_pairs={{0,64},{32,96},{64,0},{96,32},{1,65},{33,97},{65,1},{97,33},{2,66}... | collective-permute-start | bytes 167432 | tf_op jit(solution)/shard_map/ppermute | solution.py:66
  19.3 3.4 %collective-permute-start.2 = (f32[218,64]{0,1:T(8,128)S(1)}, f32[218,64]{0,1:T(8,128)}, u32[]{:S(2)}, u32[]{:S(2)}) collective-permute-start(f32[218,64]{0,1:T(8,128)S(1)} %pad_maximum_fusion.1), channel_id=1, source_target_pairs={{0,96},{32,0},{64,32},{96,64},{1,97},{33,1},{65,33},{97,65},{2,98}... | collective-permute-start | bytes 167432 | tf_op jit(solution)/shard_map/ppermute | solution.py:66
  20.2 6.0 %copy-start.1 = (f32[4,768,64]{1,2,0:T(8,128)S(1)}, f32[4,768,64]{1,2,0:T(8,128)}, u32[]{:S(2)}) copy-start(f32[4,768,64]{1,2,0:T(8,128)} %param.33) | copy-start | bytes 2359300
  26.2 6.2 %copy-start.4 = (f32[1,24,3072]{2,1,0:T(8,128)S(1)}, f32[1,24,3072]{2,1,0:T(8,128)}, u32[]{:S(2)}) copy-start(f32[1,24,3072]{2,1,0:T(8,128)} %param.27) | copy-start | bytes 884740
  26.2 6.2 %copy-start.5 = (f32[1,24,3072]{2,1,0:T(8,128)S(1)}, f32[1,24,3072]{2,1,0:T(8,128)}, u32[]{:S(2)}) copy-start(f32[1,24,3072]{2,1,0:T(8,128)} %param.19) | copy-start | bytes 884740
  30.3 3.3 %copy-start.9 = (f32[1,4,24,768]{3,2,1,0:T(8,128)S(1)}, f32[1,4,24,768]{3,2,1,0:T(8,128)}, u32[]{:S(2)}) copy-start(f32[1,4,24,768]{3,2,1,0:T(8,128)} %param.26) | copy-start | bytes 884740
  30.4 3.3 %copy-start.10 = (f32[4,24,768]{2,1,0:T(8,128)S(1)}, f32[4,24,768]{2,1,0:T(8,128)}, u32[]{:S(2)}) copy-start(f32[4,24,768]{2,1,0:T(8,128)} %param.22) | copy-start | bytes 884740
  30.4 3.3 %copy-start.11 = (f32[1,4,24,768]{3,2,1,0:T(8,128)S(1)}, f32[1,4,24,768]{3,2,1,0:T(8,128)}, u32[]{:S(2)}) copy-start(f32[1,4,24,768]{3,2,1,0:T(8,128)} %param.18) | copy-start | bytes 884740
  30.4 3.3 %copy-start.15 = (f32[4,24,64]{2,1,0:T(8,128)S(1)}, f32[4,24,64]{2,1,0:T(8,128)}, u32[]{:S(2)}) copy-start(f32[4,24,64]{2,1,0:T(8,128)} %copy-done.14) | copy-start | bytes 73732
  30.4 4.5 %copy-start.18 = (f32[4,24]{1,0:T(4,128)S(1)}, f32[4,24]{1,0:T(4,128)}, u32[]{:S(2)}) copy-start(f32[4,24]{1,0:T(4,128)} %reshape.94) | copy-start | bytes 1156
  30.4 4.5 %copy-start.20 = (f32[4,24]{1,0:T(4,128)S(1)}, f32[4,24]{1,0:T(4,128)}, u32[]{:S(2)}) copy-start(f32[4,24]{1,0:T(4,128)} %param.32) | copy-start | bytes 1156
  32.4 30.2 %copy-start.12 = (f32[12,24,768]{2,1,0:T(8,128)S(1)}, f32[12,24,768]{2,1,0:T(8,128)}, u32[]{:S(2)}) copy-start(f32[12,24,768]{2,1,0:T(8,128)} %get-tuple-element.24) | copy-start | bytes 2654212
Sparse Core Ops, SparseCore 0:
  30.5 68.9 all-gather.2

commit v6 on v5

--- a/solution.py
+++ b/solution.py
@@ -110,31 +110,26 @@
         "rk,dk->rd", factor_down, basis_down, precision=highest
     )
     norm_delta = start_ln - trained_ln[0]
-    norm_flat = norm_delta.reshape(-1)
-    norm_rows = -(-norm_flat.shape[0] // rank)
-    norm_pad = jnp.pad(norm_flat, (0, norm_rows * rank - norm_flat.shape[0]))
-    parts = [factor_sq.reshape(-1, rank), factor_up, factor_down, norm_pad.reshape(norm_rows, rank)]
-    summed = rep_sum(jnp.concatenate(parts)) / groups
-    cuts = [p.shape[0] for p in parts]
-    at = [sum(cuts[:i]) for i in range(len(cuts))]
-    mean_sq = summed[at[0] : at[1]].reshape(factor_sq.shape)
-    mean_up = summed[at[1] : at[2]]
-    mean_down = summed[at[2] : at[3]]
-    mean_ln = summed[at[3] :].reshape(-1)[: norm_flat.shape[0]].reshape(norm_delta.shape)
     blocks_up = start_up.shape[1] // width
     blocks_down = start_down.shape[0] // rows
+    norm_cols = norm_delta.shape[0]
+    norm_block = jnp.pad(norm_delta.T, ((0, 0), (0, rank - norm_cols)))
+    stacked = jnp.concatenate(
+        [
+            factor_sq,
+            jnp.broadcast_to(factor_up[None], (blocks_up, rows, rank)),
+            factor_down.reshape(blocks_down, rows, rank),
+            norm_block[None],
+        ]
+    )
+    summed = rep_sum(stacked) / groups
+    mean_all = summed[:-1]
+    mean_ln = summed[-1, :, :norm_cols].T
     start_all = jnp.concatenate(
         [start_sq, split_cols(start_up, width), start_down.reshape(blocks_down, rows, width)]
     )
     mom_all = jnp.concatenate(
         [mom_sq, split_cols(mom_up, width), mom_down.reshape(blocks_down, rows, width)]
-    )
-    mean_all = jnp.concatenate(
-        [
-            mean_sq,
-            jnp.broadcast_to(mean_up[None], (blocks_up, rows, rank)),
-            mean_down.reshape(blocks_down, rows, rank),
-        ]
     )
     basis_all = jnp.concatenate(
         [

time: 117 us -> 117 us (level)
  waiting for transfers between devices: 35.3 us -> 39.8 us
  local copies, waits for them, and re-layouts: 8.49 us -> 4.54 us
    ppermute x3, waiting for transfers between devices: 0.06 us -> 4.61 us  [rep_sum(): lax.ppermute(parts, 'rep', [(i, (i + d) % n) for i in range(n)])]
    reshape x8 -> x0, local copies, waits for them, and re-layouts: 2.57 us -> none  [the longest x2 1.47 us: split_cols(): return a.reshape(a.shape[0], -1, width).transpose(1, 0, 2)]
    slice x7 -> x2, local copies, waits for them, and re-layouts: 1.79 us -> 0.08 us  [on_device(): mean_ln = summed[-1, :, :norm_cols].T]
    dot_general x1, matrix products: 2.28 us -> 0.75 us  [on_device(): jnp.einsum('mrd,mdk->mrk', delta_sq, basis_sq, precision=highest)]
    dot_general x1, matrix products: 0.39 us -> 1.72 us  [on_device(): jnp.dot(delta_down, basis_down, precision=highest, preferred_element_type...]
  transfers between devices with their start and end apart: 4 -> 4, of which waited for: 1 -> 3; matrix products, arithmetic and copies ran while one was open for 8% -> 8% of each run, Pallas kernels for 0% -> 0%
where the time goes in v6:
time: 117 us
  waiting for transfers between devices  39.8 us (34%)
  blocking collectives  25.8 us (22%)
  between operations  14.3 us (12%)
  matrix products  13.2 us (11%)
  Pallas kernels  10.1 us (9%)
  starting transfers between devices  6.53 us (6%)
  local copies, waits for them, and re-layouts  4.54 us (4%)
  other arithmetic  2.78 us (2%)
    all_gather x1, waiting for transfers between devices, on_device(): gathered = lax.all_gather(owned_all, 'shard', axis=1, tiled=True)  35.1 us
    all_gather x1, blocking collectives, on_device(): weights_ln = lax.all_gather(norm_weights, 'shard', axis=1, tiled=True)  25.8 us
    pallas_call x1, Pallas kernels, unpack(): pl.pallas_call(functools.partial(unpack_kernel, rows), grid=(total // ste...  10.1 us
    ppermute x3, starting transfers between devices, rep_sum(): lax.ppermute(parts, 'rep', [(i, (i + d) % n) for i in range(n)])  6.5 us
    ppermute x3, waiting for transfers between devices, rep_sum(): lax.ppermute(parts, 'rep', [(i, (i + d) % n) for i in range(n)])  4.61 us
    dot_general x1, matrix products, on_device(): jnp.einsum('brk,bdk->brd', mean_all, basis_all, precision=highest)  4.12 us
  transfers between devices with their start and end apart: 4, of which 3 were waited for; matrix products, arithmetic and copies ran while one was open for 8% of the time, Pallas kernels for 0%

profile of v6, /device:TPU:1, one launch (start us, length us, event | category | flops | bytes accessed | tf_op | source)
XLA Modules:
  0.0 117.1 jit_solution(6051645953849251477)
XLA Ops:
  7.2 0.0 copy-start.2
  7.2 0.0 copy-start.13
  7.2 0.0 copy-start.11
  7.2 0.0 copy-start.9
  7.2 0.0 all-gather.3.cloned.1.call-start
  7.3 1.7 %fusion.16 = f32[96,64]{0,1:T(8,128)S(1)} fusion(f32[768,64]{0,1:T(8,128)} %param.35, f32[1,96,768]{2,1,0:T(8,128)} %param.28, f32[96,768]{1,0:T(8,128)} %param.24, f32[1,96,768]{2,1,0:T(8,128)} %param.20), kind=kOutput, calls=%fused_computation.39 | convolution fusion | flops 56770560 | bytes 1105920 | tf_op jit(solution)/shard_map/dot_general | solution.py:106
  9.0 0.0 copy-start.18
  9.0 0.1 copy.52
  9.1 0.7 fusion.11
  9.8 0.1 copy.53
  9.9 2.2 %fusion.15 = f32[24,64]{1,0:T(8,128)S(1)} fusion(f32[3072,64]{0,1:T(8,128)} %param.34, f32[1,24,3072]{2,1,0:T(8,128)} %param.27, f32[24,3072]{1,0:T(8,128)} %param.23, f32[1,24,3072]{2,1,0:T(8,128)} %param.19), kind=kOutput, calls=%fused_computation.38 | convolution fusion | flops 56770560 | bytes 1677312 | tf_op jit(solution)/shard_map/dot_general | solution.py:103
  12.2 0.8 fusion.14
  12.9 0.7 fusion.17
  13.6 2.5 %collective-permute-start = (f32[13,24,64]{2,1,0:T(8,128)}, f32[13,24,64]{2,1,0:T(8,128)S(1)}, u32[]{:S(2)}, u32[]{:S(2)}) collective-permute-start(f32[13,24,64]{2,1,0:T(8,128)} %get-tuple-element.29), channel_id=1, source_target_pairs={{0,32},{32,64},{64,96},{96,0},{1,33},{33,65},{65,97},{97,1},{2,34}... | collective-permute-start | bytes 239624 | tf_op jit(solution)/shard_map/ppermute | solution.py:66
  16.1 3.3 %collective-permute-start.1 = (f32[13,24,64]{2,1,0:T(8,128)}, f32[13,24,64]{2,1,0:T(8,128)S(1)}, u32[]{:S(2)}, u32[]{:S(2)}) collective-permute-start(f32[13,24,64]{2,1,0:T(8,128)} %get-tuple-element.29), channel_id=1, source_target_pairs={{0,64},{32,96},{64,0},{96,32},{1,65},{33,97},{65,1},{97,33},{2,66}... | collective-permute-start | bytes 239624 | tf_op jit(solution)/shard_map/ppermute | solution.py:66
  19.4 0.7 collective-permute-start.2
  20.1 0.0 copy-done.19
  20.1 0.8 bitcast_bitcast_fusion
  21.0 0.9 copy.66
  21.9 0.3 collective-permute-done
  22.3 4.3 %collective-permute-done.1 = f32[13,24,64]{2,1,0:T(8,128)S(1)} collective-permute-done((f32[13,24,64]{2,1,0:T(8,128)}, f32[13,24,64]{2,1,0:T(8,128)S(1)}, u32[]{:S(2)}, u32[]{:S(2)}) %collective-permute-start.1) | collective-permute-done | bytes 79904 | tf_op jit(solution)/shard_map/ppermute | solution.py:66
  26.6 0.0 collective-permute-done.2
  26.6 0.7 add_multiply_fusion
  27.4 0.1 copy.57
  27.5 0.1 broadcast_in_dim.29
  27.5 0.0 copy-start.6
  27.5 0.0 copy-start.8
  27.6 0.0 copy-start.4
  27.6 0.0 copy-start.5
  27.6 4.1 %fusion.10 = (bf16[12,24,768]{2,1,0:T(8,128)(2,1)}, f32[12,24,768]{2,1,0:T(8,128)}) fusion(f32[4,24,768]{2,1,0:T(8,128)S(1)} %bitcast.107, f32[4,24,768]{2,1,0:T(8,128)} %get-tuple-element.30, f32[4,24,768]{2,1,0:T(8,128)} %param.22, f32[4,24,768]{2,1,0:T(8,128)} %bitcast.118, f32[4,24,768]{2,1,0:T(8,128)} %get-tuple-element.31, f32[4,24,768]{2,1,0:T(8,128)} %param.29, ...), kind=kOutput, calls=%fused_computation.15 | convolution fusion | flops 173481984 | bytes 5603328 | tf_op jit(solution)/shard_map/brk,bdk->brd/dot_general | solution.py:141
  31.7 0.0 all-gather.3.cloned.1.call-update
  31.8 0.0 copy-start.10
  31.8 0.0 copy-start.12
  31.8 0.0 copy-start.14
  31.8 0.0 copy-start.17
  31.8 0.0 copy-start.20
  31.8 0.0 copy-start.21
  31.8 2.0 %fusion.7 = f32[1,96,768]{2,1,0:T(8,128)} fusion(f32[96,64]{0,1:T(8,128)} %copy-done.18, f32[768,64]{0,1:T(8,128)S(1)} %copy-done.3, f32[1,96,768]{2,1,0:T(8,128)S(1)} %copy-done.6, f32[96,768]{1,0:T(8,128)S(1)} %copy-done.7, f32[1,96,768]{2,1,0:T(8,128)S(1)} %copy-done.8), kind=kOutput, calls=%fused_computation.9 | convolution fusion | flops 56844288 | bytes 1400832 | tf_op jit(solution)/shard_map/rk,dk->rd/dot_general | solution.py:109
  33.8 1.2 %fusion = f32[1,24,3072]{2,1,0:T(8,128)} fusion(f32[24,64]{1,0:T(8,128)S(1)} %fusion.15, f32[3072,64]{0,1:T(8,128)S(1)} %copy-done, f32[1,24,3072]{2,1,0:T(8,128)S(1)} %copy-done.4, f32[24,3072]{1,0:T(8,128)S(1)} %copy-done.2, f32[1,24,3072]{2,1,0:T(8,128)S(1)} %copy-done.5), kind=kOutput, calls=%fused_computation.1 | convolution fusion | flops 56844288 | bytes 1972224 | tf_op jit(solution)/shard_map/rk,fk->rf/dot_general | solution.py:104
  35.0 0.0 copy-start.15
  35.1 1.2 %fusion.8 = f32[1,4,24,768]{3,2,1,0:T(8,128)} fusion(f32[4,24,64]{2,1,0:T(8,128)S(1)} %copy-done.17, f32[4,768,64]{1,2,0:T(8,128)S(1)} %copy-done.1, f32[1,4,24,768]{3,2,1,0:T(8,128)S(1)} %copy-done.10, f32[4,24,768]{2,1,0:T(8,128)S(1)} %copy-done.12, f32[1,4,24,768]{3,2,1,0:T(8,128)S(1)} %copy-done.14), kind=kOutput, calls=%fused_computation.11 | convolution fusion | flops 56844288 | bytes 1990656 | tf_op jit(solution)/shard_map/mrk,mdk->mrd/dot_general | solution.py:101
  36.3 0.6 fusion.12
  36.9 25.8 %all-gather = bf16[32,24,4]{1,2,0:T(4,128)(2,1)S(1)} all-gather(bf16[1,24,4]{1,2,0:T(4,128)(2,1)S(1)} %get-tuple-element.21), channel_id=1, replica_groups=mesh['rep'=4,'shard'=32] {'shard'}, dimensions={0}, use_global_device_ids=true | all-gather | bytes 6336 | tf_op jit(solution)/shard_map/all_gather | solution.py:150
  62.7 0.7 reshape.67
  63.4 0.9 fusion.18
  64.3 0.7 copy.62
  65.0 35.1 %all-gather.3.cloned.1.call-done = bf16[12,768,768]{2,1,0:T(8,128)(2,1)} async-done(((bf16[12,24,768]{2,1,0:T(8,128)(2,1)}), bf16[12,768,768]{2,1,0:T(8,128)(2,1)}) %all-gather.3.cloned.1.call-update) | async-done | bytes 14155792 | tf_op jit(solution)/shard_map/all_gather | solution.py:148
  100.1 10.1 %shard_map.257 = (bf16[4,768,768]{2,1,0:T(8,128)(2,1)}, bf16[768,3072]{1,0:T(8,128)(2,1)}, bf16[3072,768]{1,0:T(8,128)(2,1)}) custom-call(bf16[3,4,768,768]{3,2,1,0:T(8,128)(2,1)} %bitcast.104), custom_call_target="tpu_custom_call" | custom-call | bytes 28311552 | tf_op jit(solution)/shard_map/pallas_call | solution.py:44
  (33 shorter events, 0.2 us)
Async XLA Ops:
  7.2 13.0 %copy-start.2 = (f32[24,3072]{1,0:T(8,128)S(1)}, f32[24,3072]{1,0:T(8,128)}, u32[]{:S(2)}) copy-start(f32[24,3072]{1,0:T(8,128)} %param.23) | copy-start | bytes 884740
  7.2 4.9 %copy-start.13 = (f32[1,4,24,768]{3,2,1,0:T(8,128)S(1)}, f32[1,4,24,768]{3,2,1,0:T(8,128)}, u32[]{:S(2)}) copy-start(f32[1,4,24,768]{3,2,1,0:T(8,128)} %param.18) | copy-start | bytes 884740
  7.2 4.9 %copy-start.11 = (f32[4,24,768]{2,1,0:T(8,128)S(1)}, f32[4,24,768]{2,1,0:T(8,128)}, u32[]{:S(2)}) copy-start(f32[4,24,768]{2,1,0:T(8,128)} %param.22) | copy-start | bytes 884740
  7.2 4.9 %copy-start.9 = (f32[1,4,24,768]{3,2,1,0:T(8,128)S(1)}, f32[1,4,24,768]{3,2,1,0:T(8,128)}, u32[]{:S(2)}) copy-start(f32[1,4,24,768]{3,2,1,0:T(8,128)} %param.26) | copy-start | bytes 884740
  7.2 4.9 %copy-start.1 = (f32[4,768,64]{1,2,0:T(8,128)S(1)}, f32[4,768,64]{1,2,0:T(8,128)}, u32[]{:S(2)}) copy-start(f32[4,768,64]{1,2,0:T(8,128)} %param.33) | copy-start | bytes 2359300
  7.2 12.9 %copy-start.19 = (f32[24,3072]{1,0:T(8,128)S(1)}, f32[24,3072]{1,0:T(8,128)}, u32[]{:S(2)}) copy-start(f32[24,3072]{1,0:T(8,128)} %param.30) | copy-start | bytes 884740
  7.2 92.9 %all-gather.3.cloned.1.call-start = ((), (), s32[]{:S(2)}) async-start(), calls=%async_computation | async-start | bytes 14598144 | tf_op jit(solution)/shard_map/all_gather | solution.py:148
  9.0 0.8 copy-start.18
  9.9 11.1 %copy-start = (f32[3072,64]{0,1:T(8,128)S(1)}, f32[3072,64]{0,1:T(8,128)}, u32[]{:S(2)}) copy-start(f32[3072,64]{0,1:T(8,128)} %param.34) | copy-start | bytes 2359300
  12.9 7.2 %copy-start.16 = (f32[4,24,64]{2,1,0:T(8,128)}, f32[4,24,64]{2,1,0:T(8,128)S(1)}, u32[]{:S(2)}) copy-start(f32[4,24,64]{2,1,0:T(8,128)S(1)} %fusion.14) | copy-start | bytes 73732
  13.6 8.6 %collective-permute-start = (f32[13,24,64]{2,1,0:T(8,128)}, f32[13,24,64]{2,1,0:T(8,128)S(1)}, u32[]{:S(2)}, u32[]{:S(2)}) collective-permute-start(f32[13,24,64]{2,1,0:T(8,128)} %get-tuple-element.29), channel_id=1, source_target_pairs={{0,32},{32,64},{64,96},{96,0},{1,33},{33,65},{65,97},{97,1},{2,34}... | collective-permute-start | bytes 239624 | tf_op jit(solution)/shard_map/ppermute | solution.py:66
  16.1 10.5 %collective-permute-start.1 = (f32[13,24,64]{2,1,0:T(8,128)}, f32[13,24,64]{2,1,0:T(8,128)S(1)}, u32[]{:S(2)}, u32[]{:S(2)}) collective-permute-start(f32[13,24,64]{2,1,0:T(8,128)} %get-tuple-element.29), channel_id=1, source_target_pairs={{0,64},{32,96},{64,0},{96,32},{1,65},{33,97},{65,1},{97,33},{2,66}... | collective-permute-start | bytes 239624 | tf_op jit(solution)/shard_map/ppermute | solution.py:66
  19.4 7.2 %collective-permute-start.2 = (f32[13,24,64]{2,1,0:T(8,128)}, f32[13,24,64]{2,1,0:T(8,128)S(1)}, u32[]{:S(2)}, u32[]{:S(2)}) collective-permute-start(f32[13,24,64]{2,1,0:T(8,128)} %get-tuple-element.29), channel_id=1, source_target_pairs={{0,96},{32,0},{64,32},{96,64},{1,97},{33,1},{65,33},{97,65},{2,98}... | collective-permute-start | bytes 239624 | tf_op jit(solution)/shard_map/ppermute | solution.py:66
  21.0 6.5 %copy-start.3 = (f32[768,64]{0,1:T(8,128)S(1)}, f32[768,64]{0,1:T(8,128)}, u32[]{:S(2)}) copy-start(f32[768,64]{0,1:T(8,128)} %param.35) | copy-start | bytes 589828
  21.0 6.5 %copy-start.7 = (f32[96,768]{1,0:T(8,128)S(1)}, f32[96,768]{1,0:T(8,128)}, u32[]{:S(2)}) copy-start(f32[96,768]{1,0:T(8,128)} %param.24) | copy-start | bytes 884740
  27.5 4.2 %copy-start.6 = (f32[1,96,768]{2,1,0:T(8,128)S(1)}, f32[1,96,768]{2,1,0:T(8,128)}, u32[]{:S(2)}) copy-start(f32[1,96,768]{2,1,0:T(8,128)} %param.28) | copy-start | bytes 884740
  27.5 4.2 %copy-start.8 = (f32[1,96,768]{2,1,0:T(8,128)S(1)}, f32[1,96,768]{2,1,0:T(8,128)}, u32[]{:S(2)}) copy-start(f32[1,96,768]{2,1,0:T(8,128)} %param.20) | copy-start | bytes 884740
  27.6 6.2 %copy-start.4 = (f32[1,24,3072]{2,1,0:T(8,128)S(1)}, f32[1,24,3072]{2,1,0:T(8,128)}, u32[]{:S(2)}) copy-start(f32[1,24,3072]{2,1,0:T(8,128)} %param.27) | copy-start | bytes 884740
  27.6 6.2 %copy-start.5 = (f32[1,24,3072]{2,1,0:T(8,128)S(1)}, f32[1,24,3072]{2,1,0:T(8,128)}, u32[]{:S(2)}) copy-start(f32[1,24,3072]{2,1,0:T(8,128)} %param.19) | copy-start | bytes 884740
  31.8 3.3 %copy-start.10 = (f32[1,4,24,768]{3,2,1,0:T(8,128)S(1)}, f32[1,4,24,768]{3,2,1,0:T(8,128)}, u32[]{:S(2)}) copy-start(f32[1,4,24,768]{3,2,1,0:T(8,128)} %param.26) | copy-start | bytes 884740
  31.8 3.3 %copy-start.12 = (f32[4,24,768]{2,1,0:T(8,128)S(1)}, f32[4,24,768]{2,1,0:T(8,128)}, u32[]{:S(2)}) copy-start(f32[4,24,768]{2,1,0:T(8,128)} %param.22) | copy-start | bytes 884740
  31.8 3.3 %copy-start.14 = (f32[1,4,24,768]{3,2,1,0:T(8,128)S(1)}, f32[1,4,24,768]{3,2,1,0:T(8,128)}, u32[]{:S(2)}) copy-start(f32[1,4,24,768]{3,2,1,0:T(8,128)} %param.18) | copy-start | bytes 884740
  31.8 3.3 %copy-start.17 = (f32[4,24,64]{2,1,0:T(8,128)S(1)}, f32[4,24,64]{2,1,0:T(8,128)}, u32[]{:S(2)}) copy-start(f32[4,24,64]{2,1,0:T(8,128)} %copy-done.16) | copy-start | bytes 73732
  31.8 4.5 %copy-start.20 = (f32[4,24]{1,0:T(4,128)S(1)}, f32[4,24]{1,0:T(4,128)}, u32[]{:S(2)}) copy-start(f32[4,24]{1,0:T(4,128)} %param.25) | copy-start | bytes 1156
  31.8 4.5 %copy-start.21 = (f32[4,24]{1,0:T(4,128)S(1)}, f32[4,24]{1,0:T(4,128)}, u32[]{:S(2)}) copy-start(f32[4,24]{1,0:T(4,128)} %param.32) | copy-start | bytes 1156
  35.0 28.4 %copy-start.15 = (f32[12,24,768]{2,1,0:T(8,128)S(1)}, f32[12,24,768]{2,1,0:T(8,128)}, u32[]{:S(2)}) copy-start(f32[12,24,768]{2,1,0:T(8,128)} %get-tuple-element.24) | copy-start | bytes 2654212
Sparse Core Ops, SparseCore 0:
  31.9 68.2 all-gather.2

commit v7 on v6

--- a/solution.py
+++ b/solution.py
@@ -92,7 +92,7 @@
     basis_up,
     basis_down,
 ):
-    highest = lax.Precision.HIGHEST
+    highest = lax.Precision.HIGH
     groups = lax.axis_size("rep")
     square, rows, width = start_sq.shape
     rank = basis_sq.shape[-1]

time: 117 us -> 116 us (level)
  matrix products: 13.2 us -> 11.5 us
  transfers between devices with their start and end apart: 4 -> 4, of which waited for: 3 -> 3; matrix products, arithmetic and copies ran while one was open for 8% -> 7% of each run, Pallas kernels for 0% -> 0%
where the time goes in v7:
time: 116 us
  waiting for transfers between devices  40.2 us (35%)
  blocking collectives  25.8 us (22%)
  between operations  14.3 us (12%)
  matrix products  11.5 us (10%)
  Pallas kernels  10.1 us (9%)
  starting transfers between devices  6.53 us (6%)
  local copies, waits for them, and re-layouts  4.53 us (4%)
  other arithmetic  2.78 us (2%)
    all_gather x1, waiting for transfers between devices, on_device(): gathered = lax.all_gather(owned_all, 'shard', axis=1, tiled=True)  35.6 us
    all_gather x1, blocking collectives, on_device(): weights_ln = lax.all_gather(norm_weights, 'shard', axis=1, tiled=True)  25.8 us
    pallas_call x1, Pallas kernels, unpack(): pl.pallas_call(functools.partial(unpack_kernel, rows), grid=(total // ste...  10.1 us
    ppermute x3, starting transfers between devices, rep_sum(): lax.ppermute(parts, 'rep', [(i, (i + d) % n) for i in range(n)])  6.5 us
    ppermute x3, waiting for transfers between devices, rep_sum(): lax.ppermute(parts, 'rep', [(i, (i + d) % n) for i in range(n)])  4.61 us
    dot_general x1, matrix products, on_device(): jnp.einsum('brk,bdk->brd', mean_all, basis_all, precision=highest)  3.63 us
  transfers between devices with their start and end apart: 4, of which 3 were waited for; matrix products, arithmetic and copies ran while one was open for 7% of the time, Pallas kernels for 0%

profile of v7, /device:TPU:1, one launch (start us, length us, event | category | flops | bytes accessed | tf_op | source)
XLA Modules:
  0.0 115.8 jit_solution(10547760653359989151)
XLA Ops:
  7.2 0.0 copy-start.2
  7.2 0.0 copy-start.13
  7.2 0.0 copy-start.11
  7.2 0.0 copy-start.9
  7.2 0.0 all-gather.3.cloned.1.call-start
  7.3 1.6 %fusion.16 = f32[96,64]{0,1:T(8,128)S(1)} fusion(f32[768,64]{0,1:T(8,128)} %param.35, f32[1,96,768]{2,1,0:T(8,128)} %param.28, f32[96,768]{1,0:T(8,128)} %param.24, f32[1,96,768]{2,1,0:T(8,128)} %param.20), kind=kOutput, calls=%fused_computation.39 | convolution fusion | flops 28459008 | bytes 1105920 | tf_op jit(solution)/shard_map/dot_general | solution.py:106
  8.9 0.0 copy-start.18
  8.9 0.1 copy.52
  9.0 0.7 fusion.11
  9.7 0.1 copy.53
  9.8 1.9 %fusion.15 = f32[24,64]{1,0:T(8,128)S(1)} fusion(f32[3072,64]{0,1:T(8,128)} %param.34, f32[1,24,3072]{2,1,0:T(8,128)} %param.27, f32[24,3072]{1,0:T(8,128)} %param.23, f32[1,24,3072]{2,1,0:T(8,128)} %param.19), kind=kOutput, calls=%fused_computation.38 | convolution fusion | flops 28459008 | bytes 1677312 | tf_op jit(solution)/shard_map/dot_general | solution.py:103
  11.7 0.0 copy-done.13
  11.8 0.4 fusion.14
  12.2 0.7 fusion.17
  12.9 2.5 %collective-permute-start = (f32[13,24,64]{2,1,0:T(8,128)}, f32[13,24,64]{2,1,0:T(8,128)S(1)}, u32[]{:S(2)}, u32[]{:S(2)}) collective-permute-start(f32[13,24,64]{2,1,0:T(8,128)} %get-tuple-element.29), channel_id=1, source_target_pairs={{0,32},{32,64},{64,96},{96,0},{1,33},{33,65},{65,97},{97,1},{2,34}... | collective-permute-start | bytes 239624 | tf_op jit(solution)/shard_map/ppermute | solution.py:66
  15.4 3.3 %collective-permute-start.1 = (f32[13,24,64]{2,1,0:T(8,128)}, f32[13,24,64]{2,1,0:T(8,128)S(1)}, u32[]{:S(2)}, u32[]{:S(2)}) collective-permute-start(f32[13,24,64]{2,1,0:T(8,128)} %get-tuple-element.29), channel_id=1, source_target_pairs={{0,64},{32,96},{64,0},{96,32},{1,65},{33,97},{65,1},{97,33},{2,66}... | collective-permute-start | bytes 239624 | tf_op jit(solution)/shard_map/ppermute | solution.py:66
  18.7 0.7 collective-permute-start.2
  19.4 0.8 bitcast_bitcast_fusion
  20.3 0.9 copy.66
  21.2 0.3 collective-permute-done
  21.5 4.3 %collective-permute-done.1 = f32[13,24,64]{2,1,0:T(8,128)S(1)} collective-permute-done((f32[13,24,64]{2,1,0:T(8,128)}, f32[13,24,64]{2,1,0:T(8,128)S(1)}, u32[]{:S(2)}, u32[]{:S(2)}) %collective-permute-start.1) | collective-permute-done | bytes 79904 | tf_op jit(solution)/shard_map/ppermute | solution.py:66
  25.8 0.0 collective-permute-done.2
  25.9 0.7 add_multiply_fusion
  26.6 0.1 copy.57
  26.7 0.1 broadcast_in_dim.29
  26.8 0.0 copy-start.6
  26.8 0.0 copy-start.8
  26.8 0.0 copy-start.4
  26.8 0.0 copy-start.5
  26.8 3.6 %fusion.10 = (bf16[12,24,768]{2,1,0:T(8,128)(2,1)}, f32[12,24,768]{2,1,0:T(8,128)}) fusion(f32[4,24,768]{2,1,0:T(8,128)S(1)} %bitcast.107, f32[4,24,768]{2,1,0:T(8,128)} %get-tuple-element.30, f32[4,24,768]{2,1,0:T(8,128)} %param.22, f32[4,24,768]{2,1,0:T(8,128)} %bitcast.118, f32[4,24,768]{2,1,0:T(8,128)} %get-tuple-element.31, f32[4,24,768]{2,1,0:T(8,128)} %param.29, ...), kind=kOutput, calls=%fused_computation.15 | convolution fusion | flops 88547328 | bytes 5603328 | tf_op jit(solution)/shard_map/brk,bdk->brd/dot_general | solution.py:141
  30.5 0.0 all-gather.3.cloned.1.call-update
  30.5 0.0 copy-start.10
  30.5 0.0 copy-start.12
  30.5 0.0 copy-start.14
  30.5 0.0 copy-start.17
  30.6 0.0 copy-start.20
  30.6 0.0 copy-start.21
  30.6 1.9 %fusion.7 = f32[1,96,768]{2,1,0:T(8,128)} fusion(f32[96,64]{0,1:T(8,128)} %copy-done.18, f32[768,64]{0,1:T(8,128)S(1)} %copy-done.3, f32[1,96,768]{2,1,0:T(8,128)S(1)} %copy-done.6, f32[96,768]{1,0:T(8,128)S(1)} %copy-done.7, f32[1,96,768]{2,1,0:T(8,128)S(1)} %copy-done.8), kind=kOutput, calls=%fused_computation.9 | convolution fusion | flops 28532736 | bytes 1400832 | tf_op jit(solution)/shard_map/rk,dk->rd/dot_general | solution.py:109
  32.5 1.0 fusion
  33.5 0.0 copy-start.15
  33.5 1.0 fusion.8
  34.6 0.6 fusion.12
  35.1 25.8 %all-gather = bf16[32,24,4]{1,2,0:T(4,128)(2,1)S(1)} all-gather(bf16[1,24,4]{1,2,0:T(4,128)(2,1)S(1)} %get-tuple-element.21), channel_id=1, replica_groups=mesh['rep'=4,'shard'=32] {'shard'}, dimensions={0}, use_global_device_ids=true | all-gather | bytes 6336 | tf_op jit(solution)/shard_map/all_gather | solution.py:150
  61.0 0.7 reshape.67
  61.7 0.9 fusion.18
  62.5 0.7 copy.62
  63.3 35.6 %all-gather.3.cloned.1.call-done = bf16[12,768,768]{2,1,0:T(8,128)(2,1)} async-done(((bf16[12,24,768]{2,1,0:T(8,128)(2,1)}), bf16[12,768,768]{2,1,0:T(8,128)(2,1)}) %all-gather.3.cloned.1.call-update) | async-done | bytes 14155792 | tf_op jit(solution)/shard_map/all_gather | solution.py:148
  98.9 10.1 %shard_map.257 = (bf16[4,768,768]{2,1,0:T(8,128)(2,1)}, bf16[768,3072]{1,0:T(8,128)(2,1)}, bf16[3072,768]{1,0:T(8,128)(2,1)}) custom-call(bf16[3,4,768,768]{3,2,1,0:T(8,128)(2,1)} %bitcast.104), custom_call_target="tpu_custom_call" | custom-call | bytes 28311552 | tf_op jit(solution)/shard_map/pallas_call | solution.py:44
  (33 shorter events, 0.2 us)
Async XLA Ops:
  7.2 12.2 %copy-start.2 = (f32[24,3072]{1,0:T(8,128)S(1)}, f32[24,3072]{1,0:T(8,128)}, u32[]{:S(2)}) copy-start(f32[24,3072]{1,0:T(8,128)} %param.23) | copy-start | bytes 884740
  7.2 4.5 %copy-start.13 = (f32[1,4,24,768]{3,2,1,0:T(8,128)S(1)}, f32[1,4,24,768]{3,2,1,0:T(8,128)}, u32[]{:S(2)}) copy-start(f32[1,4,24,768]{3,2,1,0:T(8,128)} %param.18) | copy-start | bytes 884740
  7.2 4.5 %copy-start.11 = (f32[4,24,768]{2,1,0:T(8,128)S(1)}, f32[4,24,768]{2,1,0:T(8,128)}, u32[]{:S(2)}) copy-start(f32[4,24,768]{2,1,0:T(8,128)} %param.22) | copy-start | bytes 884740
  7.2 4.5 %copy-start.9 = (f32[1,4,24,768]{3,2,1,0:T(8,128)S(1)}, f32[1,4,24,768]{3,2,1,0:T(8,128)}, u32[]{:S(2)}) copy-start(f32[1,4,24,768]{3,2,1,0:T(8,128)} %param.26) | copy-start | bytes 884740
  7.2 4.5 %copy-start.1 = (f32[4,768,64]{1,2,0:T(8,128)S(1)}, f32[4,768,64]{1,2,0:T(8,128)}, u32[]{:S(2)}) copy-start(f32[4,768,64]{1,2,0:T(8,128)} %param.33) | copy-start | bytes 2359300
  7.2 12.2 %copy-start.19 = (f32[24,3072]{1,0:T(8,128)S(1)}, f32[24,3072]{1,0:T(8,128)}, u32[]{:S(2)}) copy-start(f32[24,3072]{1,0:T(8,128)} %param.30) | copy-start | bytes 884740
  7.2 91.6 %all-gather.3.cloned.1.call-start = ((), (), s32[]{:S(2)}) async-start(), calls=%async_computation | async-start | bytes 14598144 | tf_op jit(solution)/shard_map/all_gather | solution.py:148
  8.9 0.8 copy-start.18
  9.8 10.4 %copy-start = (f32[3072,64]{0,1:T(8,128)S(1)}, f32[3072,64]{0,1:T(8,128)}, u32[]{:S(2)}) copy-start(f32[3072,64]{0,1:T(8,128)} %param.34) | copy-start | bytes 2359300
  12.2 7.2 %copy-start.16 = (f32[4,24,64]{2,1,0:T(8,128)}, f32[4,24,64]{2,1,0:T(8,128)S(1)}, u32[]{:S(2)}) copy-start(f32[4,24,64]{2,1,0:T(8,128)S(1)} %fusion.14) | copy-start | bytes 73732
  12.9 8.6 %collective-permute-start = (f32[13,24,64]{2,1,0:T(8,128)}, f32[13,24,64]{2,1,0:T(8,128)S(1)}, u32[]{:S(2)}, u32[]{:S(2)}) collective-permute-start(f32[13,24,64]{2,1,0:T(8,128)} %get-tuple-element.29), channel_id=1, source_target_pairs={{0,32},{32,64},{64,96},{96,0},{1,33},{33,65},{65,97},{97,1},{2,34}... | collective-permute-start | bytes 239624 | tf_op jit(solution)/shard_map/ppermute | solution.py:66
  15.4 10.4 %collective-permute-start.1 = (f32[13,24,64]{2,1,0:T(8,128)}, f32[13,24,64]{2,1,0:T(8,128)S(1)}, u32[]{:S(2)}, u32[]{:S(2)}) collective-permute-start(f32[13,24,64]{2,1,0:T(8,128)} %get-tuple-element.29), channel_id=1, source_target_pairs={{0,64},{32,96},{64,0},{96,32},{1,65},{33,97},{65,1},{97,33},{2,66}... | collective-permute-start | bytes 239624 | tf_op jit(solution)/shard_map/ppermute | solution.py:66
  18.7 7.1 %collective-permute-start.2 = (f32[13,24,64]{2,1,0:T(8,128)}, f32[13,24,64]{2,1,0:T(8,128)S(1)}, u32[]{:S(2)}, u32[]{:S(2)}) collective-permute-start(f32[13,24,64]{2,1,0:T(8,128)} %get-tuple-element.29), channel_id=1, source_target_pairs={{0,96},{32,0},{64,32},{96,64},{1,97},{33,1},{65,33},{97,65},{2,98}... | collective-permute-start | bytes 239624 | tf_op jit(solution)/shard_map/ppermute | solution.py:66
  20.2 6.5 %copy-start.3 = (f32[768,64]{0,1:T(8,128)S(1)}, f32[768,64]{0,1:T(8,128)}, u32[]{:S(2)}) copy-start(f32[768,64]{0,1:T(8,128)} %param.35) | copy-start | bytes 589828
  20.3 6.5 %copy-start.7 = (f32[96,768]{1,0:T(8,128)S(1)}, f32[96,768]{1,0:T(8,128)}, u32[]{:S(2)}) copy-start(f32[96,768]{1,0:T(8,128)} %param.24) | copy-start | bytes 884740
  26.8 3.7 %copy-start.6 = (f32[1,96,768]{2,1,0:T(8,128)S(1)}, f32[1,96,768]{2,1,0:T(8,128)}, u32[]{:S(2)}) copy-start(f32[1,96,768]{2,1,0:T(8,128)} %param.28) | copy-start | bytes 884740
  26.8 3.7 %copy-start.8 = (f32[1,96,768]{2,1,0:T(8,128)S(1)}, f32[1,96,768]{2,1,0:T(8,128)}, u32[]{:S(2)}) copy-start(f32[1,96,768]{2,1,0:T(8,128)} %param.20) | copy-start | bytes 884740
  26.8 5.6 %copy-start.4 = (f32[1,24,3072]{2,1,0:T(8,128)S(1)}, f32[1,24,3072]{2,1,0:T(8,128)}, u32[]{:S(2)}) copy-start(f32[1,24,3072]{2,1,0:T(8,128)} %param.27) | copy-start | bytes 884740
  26.8 5.6 %copy-start.5 = (f32[1,24,3072]{2,1,0:T(8,128)S(1)}, f32[1,24,3072]{2,1,0:T(8,128)}, u32[]{:S(2)}) copy-start(f32[1,24,3072]{2,1,0:T(8,128)} %param.19) | copy-start | bytes 884740
  30.5 3.0 %copy-start.10 = (f32[1,4,24,768]{3,2,1,0:T(8,128)S(1)}, f32[1,4,24,768]{3,2,1,0:T(8,128)}, u32[]{:S(2)}) copy-start(f32[1,4,24,768]{3,2,1,0:T(8,128)} %param.26) | copy-start | bytes 884740
  30.5 3.0 %copy-start.12 = (f32[4,24,768]{2,1,0:T(8,128)S(1)}, f32[4,24,768]{2,1,0:T(8,128)}, u32[]{:S(2)}) copy-start(f32[4,24,768]{2,1,0:T(8,128)} %param.22) | copy-start | bytes 884740
  30.5 3.0 %copy-start.14 = (f32[1,4,24,768]{3,2,1,0:T(8,128)S(1)}, f32[1,4,24,768]{3,2,1,0:T(8,128)}, u32[]{:S(2)}) copy-start(f32[1,4,24,768]{3,2,1,0:T(8,128)} %param.18) | copy-start | bytes 884740
  30.5 2.9 %copy-start.17 = (f32[4,24,64]{2,1,0:T(8,128)S(1)}, f32[4,24,64]{2,1,0:T(8,128)}, u32[]{:S(2)}) copy-start(f32[4,24,64]{2,1,0:T(8,128)} %copy-done.16) | copy-start | bytes 73732
  30.6 4.0 %copy-start.20 = (f32[4,24]{1,0:T(4,128)S(1)}, f32[4,24]{1,0:T(4,128)}, u32[]{:S(2)}) copy-start(f32[4,24]{1,0:T(4,128)} %param.25) | copy-start | bytes 1156
  30.6 4.0 %copy-start.21 = (f32[4,24]{1,0:T(4,128)S(1)}, f32[4,24]{1,0:T(4,128)}, u32[]{:S(2)}) copy-start(f32[4,24]{1,0:T(4,128)} %param.32) | copy-start | bytes 1156
  33.5 28.2 %copy-start.15 = (f32[12,24,768]{2,1,0:T(8,128)S(1)}, f32[12,24,768]{2,1,0:T(8,128)}, u32[]{:S(2)}) copy-start(f32[12,24,768]{2,1,0:T(8,128)} %get-tuple-element.24) | copy-start | bytes 2654212
Sparse Core Ops, SparseCore 0:
  30.6 68.2 all-gather.2

commit v8 on v6

--- a/solution.py
+++ b/solution.py
@@ -100,18 +100,21 @@
     factor_sq = jnp.einsum("mrd,mdk->mrk", delta_sq, basis_sq, precision=highest)
     new_resid_sq = delta_sq - jnp.einsum("mrk,mdk->mrd", factor_sq, basis_sq, precision=highest)
     delta_up = start_up - trained_up[0] + resid_up[0]
-    factor_up = jnp.dot(delta_up, basis_up, precision=highest, preferred_element_type=jnp.float32)
+    blocks_up = start_up.shape[1] // width
+    basis_up_blocks = basis_up.reshape(blocks_up, width, rank)
+    factor_up = jnp.einsum(
+        "krd,kdc->krc", split_cols(delta_up, width), basis_up_blocks, precision=highest
+    ).sum(0)
     new_resid_up = delta_up - jnp.einsum("rk,fk->rf", factor_up, basis_up, precision=highest)
     delta_down = start_down - trained_down[0] + resid_down[0]
-    factor_down = jnp.dot(
-        delta_down, basis_down, precision=highest, preferred_element_type=jnp.float32
-    )
+    blocks_down = start_down.shape[0] // rows
+    factor_down = jnp.einsum(
+        "qrd,dc->qrc", delta_down.reshape(blocks_down, rows, width), basis_down, precision=highest
+    ).reshape(-1, rank)
     new_resid_down = delta_down - jnp.einsum(
         "rk,dk->rd", factor_down, basis_down, precision=highest
     )
     norm_delta = start_ln - trained_ln[0]
-    blocks_up = start_up.shape[1] // width
-    blocks_down = start_down.shape[0] // rows
     norm_cols = norm_delta.shape[0]
     norm_block = jnp.pad(norm_delta.T, ((0, 0), (0, rank - norm_cols)))
     stacked = jnp.concatenate(

time: 117 us -> 119 us (1.017)
  other arithmetic: 2.78 us -> 5.68 us
  matrix products: 13.2 us -> 10.6 us
  waiting for transfers between devices: 39.8 us -> 41 us
    add x0 -> x2, other arithmetic: none -> 2.35 us  [the longest x1 1.18 us: on_device(): delta_up = start_up - trained_up[0] + resid_up[0]]
    dot_general x2, matrix products: 3.93 us -> 2.3 us  [the longest x1 1.92 us: on_device(): jnp.einsum('krd,kdc->krc', split_cols(delta_up, width), basis_up_blocks,...]
  transfers between devices with their start and end apart: 4 -> 4, of which waited for: 3 -> 3; matrix products, arithmetic and copies ran while one was open for 8% -> 7% of each run, Pallas kernels for 0% -> 0%
where the time goes in v8:
time: 119 us
  waiting for transfers between devices  41 us (34%)
  blocking collectives  25.8 us (22%)
  between operations  14.2 us (12%)
  matrix products  10.6 us (9%)
  Pallas kernels  10.1 us (8%)
  starting transfers between devices  6.53 us (5%)
  other arithmetic  5.68 us (5%)
  local copies, waits for them, and re-layouts  5 us (4%)
    all_gather x1, waiting for transfers between devices, on_device(): gathered = lax.all_gather(owned_all, 'shard', axis=1, tiled=True)  36.2 us
    all_gather x1, blocking collectives, on_device(): weights_ln = lax.all_gather(norm_weights, 'shard', axis=1, tiled=True)  25.8 us
    pallas_call x1, Pallas kernels, unpack(): pl.pallas_call(functools.partial(unpack_kernel, rows), grid=(total // ste...  10.1 us
    ppermute x3, starting transfers between devices, rep_sum(): lax.ppermute(parts, 'rep', [(i, (i + d) % n) for i in range(n)])  6.5 us
    ppermute x3, waiting for transfers between devices, rep_sum(): lax.ppermute(parts, 'rep', [(i, (i + d) % n) for i in range(n)])  4.72 us
    dot_general x1, matrix products, on_device(): jnp.einsum('brk,bdk->brd', mean_all, basis_all, precision=highest)  3.97 us
  transfers between devices with their start and end apart: 4, of which 3 were waited for; matrix products, arithmetic and copies ran while one was open for 7% of the time, Pallas kernels for 0%

profile of v8, /device:TPU:1, one launch (start us, length us, event | category | flops | bytes accessed | tf_op | source)
XLA Modules:
  0.0 118.9 jit_solution(5880953614339737596)
XLA Ops:
  7.2 0.0 copy-start.8
  7.2 0.0 copy-start.2
  7.2 0.0 copy-start.6
  7.2 0.0 copy-start.5
  7.2 0.0 copy-start.4
  7.2 0.0 copy-start.1
  7.2 0.0 all-gather.3.cloned.1.call-start
  7.3 0.8 fusion.14
  8.1 0.7 copy.56
  8.8 1.2 bitcast_add_fusion.1
  10.0 0.0 copy-start.10
  10.0 0.0 copy-start.3
  10.0 0.0 copy-start.9
  10.0 1.9 %convolution_bitcast_fusion = f32[24,64]{1,0:T(8,128)S(1)} fusion(f32[3,4,8,768]{3,2,1,0:T(8,128)S(1)} %bitcast.109, f32[8,4,8,768]{3,2,1,0:T(8,128)} %bitcast.106), kind=kOutput, calls=%fused_computation.12 | convolution fusion | flops 56623104 | bytes 1087488 | tf_op jit(solution)/shard_map/krd,kdc->krc/dot_general | solution.py:105
  11.9 0.0 copy-done.8
  12.0 0.0 copy-start
  12.0 1.2 bitcast_add_fusion
  13.2 0.4 fusion.12
  13.6 0.8 fusion.17
  14.4 0.0 copy-done.10
  14.4 0.7 fusion.18
  15.1 2.5 %collective-permute-start = (f32[13,24,64]{2,1,0:T(8,128)}, f32[13,24,64]{2,1,0:T(8,128)}, u32[]{:S(2)}, u32[]{:S(2)}) collective-permute-start(f32[13,24,64]{2,1,0:T(8,128)} %get-tuple-element.29), channel_id=1, source_target_pairs={{0,32},{32,64},{64,96},{96,0},{1,33},{33,65},{65,97},{97,1},{2,34}... | collective-permute-start | bytes 239624 | tf_op jit(solution)/shard_map/ppermute | solution.py:66
  17.5 3.3 %collective-permute-start.1 = (f32[13,24,64]{2,1,0:T(8,128)}, f32[13,24,64]{2,1,0:T(8,128)}, u32[]{:S(2)}, u32[]{:S(2)}) collective-permute-start(f32[13,24,64]{2,1,0:T(8,128)} %get-tuple-element.29), channel_id=1, source_target_pairs={{0,64},{32,96},{64,0},{96,32},{1,65},{33,97},{65,1},{97,33},{2,66}... | collective-permute-start | bytes 239624 | tf_op jit(solution)/shard_map/ppermute | solution.py:66
  20.8 0.7 collective-permute-start.2
  21.6 0.0 copy-done.3
  21.6 0.8 bitcast_bitcast_fusion
  22.4 0.9 copy.75
  23.4 0.4 collective-permute-done
  23.8 4.3 %collective-permute-done.1 = f32[13,24,64]{2,1,0:T(8,128)} collective-permute-done((f32[13,24,64]{2,1,0:T(8,128)}, f32[13,24,64]{2,1,0:T(8,128)}, u32[]{:S(2)}, u32[]{:S(2)}) %collective-permute-start.1) | collective-permute-done | bytes 79904 | tf_op jit(solution)/shard_map/ppermute | solution.py:66
  28.1 0.0 collective-permute-done.2
  28.1 1.1 pad_maximum_fusion
  29.2 0.1 add_multiply_fusion
  29.3 0.1 fusion.28
  29.3 0.1 copy.60
  29.4 0.1 broadcast_in_dim.29
  29.5 4.0 %fusion.10 = (bf16[12,24,768]{2,1,0:T(8,128)(2,1)}, f32[12,24,768]{2,1,0:T(8,128)}) fusion(f32[4,24,768]{2,1,0:T(8,128)} %bitcast.116, f32[4,24,768]{2,1,0:T(8,128)} %get-tuple-element.30, f32[4,24,768]{2,1,0:T(8,128)S(1)} %copy-done.5, f32[4,24,768]{2,1,0:T(8,128)} %bitcast.119, f32[4,24,768]{2,1,0:T(8,128)} %get-tuple-element.31, ...), kind=kOutput, calls=%fused_computation.16 | convolution fusion | flops 173481984 | bytes 5603328 | tf_op jit(solution)/shard_map/brk,bdk->brd/dot_general | solution.py:144
  33.4 0.0 all-gather.3.cloned.1.call-update
  33.5 1.1 fusion.7
  34.6 1.2 %fusion = f32[1,24,3072]{2,1,0:T(8,128)} fusion(f32[24,3072]{1,0:T(8,128)S(1)} %bitcast_add_fusion.1, f32[24,64]{1,0:T(8,128)S(1)} %convolution_bitcast_fusion, f32[3072,64]{0,1:T(8,128)S(1)} %copy-done), kind=kOutput, calls=%fused_computation.1 | convolution fusion | flops 56696832 | bytes 1382400 | tf_op jit(solution)/shard_map/rk,fk->rf/dot_general | solution.py:108
  35.8 1.2 %fusion.8 = f32[1,4,24,768]{3,2,1,0:T(8,128)} fusion(f32[4,24,64]{2,1,0:T(8,128)S(1)} %fusion.17, f32[4,768,64]{1,2,0:T(8,128)S(1)} %copy-done.1, f32[1,4,24,768]{3,2,1,0:T(8,128)S(1)} %copy-done.4, f32[4,24,768]{2,1,0:T(8,128)S(1)} %copy-done.5, f32[1,4,24,768]{3,2,1,0:T(8,128)S(1)} %copy-done.6), kind=kOutput, calls=%fused_computation.11 | convolution fusion | flops 56844288 | bytes 1990656 | tf_op jit(solution)/shard_map/mrk,mdk->mrd/dot_general | solution.py:101
  37.0 0.0 copy-done.11
  37.0 0.6 fusion.15
  37.6 25.8 %all-gather = bf16[32,24,4]{1,2,0:T(4,128)(2,1)S(1)} all-gather(bf16[1,24,4]{1,2,0:T(4,128)(2,1)S(1)} %get-tuple-element.21), channel_id=1, replica_groups=mesh['rep'=4,'shard'=32] {'shard'}, dimensions={0}, use_global_device_ids=true | all-gather | bytes 6336 | tf_op jit(solution)/shard_map/all_gather | solution.py:153
  63.4 0.7 reshape.76
  64.1 0.9 fusion.19
  65.0 0.7 copy.66
  65.7 36.2 %all-gather.3.cloned.1.call-done = bf16[12,768,768]{2,1,0:T(8,128)(2,1)} async-done(((bf16[12,24,768]{2,1,0:T(8,128)(2,1)}), bf16[12,768,768]{2,1,0:T(8,128)(2,1)}) %all-gather.3.cloned.1.call-update) | async-done | bytes 14155792 | tf_op jit(solution)/shard_map/all_gather | solution.py:151
  101.9 10.1 %shard_map.257 = (bf16[4,768,768]{2,1,0:T(8,128)(2,1)}, bf16[768,3072]{1,0:T(8,128)(2,1)}, bf16[3072,768]{1,0:T(8,128)(2,1)}) custom-call(bf16[3,4,768,768]{3,2,1,0:T(8,128)(2,1)} %bitcast.105), custom_call_target="tpu_custom_call" | custom-call | bytes 28311552 | tf_op jit(solution)/shard_map/pallas_call | solution.py:44
  (16 shorter events, 0.0 us)
Async XLA Ops:
  7.2 4.8 %copy-start.8 = (f32[1,96,768]{2,1,0:T(8,128)S(1)}, f32[1,96,768]{2,1,0:T(8,128)}, u32[]{:S(2)}) copy-start(f32[1,96,768]{2,1,0:T(8,128)} %param.28) | copy-start | bytes 884740
  7.2 6.0 %copy-start.2 = (f32[768,64]{0,1:T(8,128)S(1)}, f32[768,64]{0,1:T(8,128)}, u32[]{:S(2)}) copy-start(f32[768,64]{0,1:T(8,128)} %param.35) | copy-start | bytes 589828
  7.2 6.4 %copy-start.6 = (f32[1,4,24,768]{3,2,1,0:T(8,128)S(1)}, f32[1,4,24,768]{3,2,1,0:T(8,128)}, u32[]{:S(2)}) copy-start(f32[1,4,24,768]{3,2,1,0:T(8,128)} %param.18) | copy-start | bytes 884740
  7.2 6.4 %copy-start.5 = (f32[4,24,768]{2,1,0:T(8,128)S(1)}, f32[4,24,768]{2,1,0:T(8,128)}, u32[]{:S(2)}) copy-start(f32[4,24,768]{2,1,0:T(8,128)} %param.22) | copy-start | bytes 884740
  7.2 6.4 %copy-start.4 = (f32[1,4,24,768]{3,2,1,0:T(8,128)S(1)}, f32[1,4,24,768]{3,2,1,0:T(8,128)}, u32[]{:S(2)}) copy-start(f32[1,4,24,768]{3,2,1,0:T(8,128)} %param.26) | copy-start | bytes 884740
  7.2 6.4 %copy-start.1 = (f32[4,768,64]{1,2,0:T(8,128)S(1)}, f32[4,768,64]{1,2,0:T(8,128)}, u32[]{:S(2)}) copy-start(f32[4,768,64]{1,2,0:T(8,128)} %param.33) | copy-start | bytes 2359300
  7.2 94.7 %all-gather.3.cloned.1.call-start = ((), (), s32[]{:S(2)}) async-start(), calls=%async_computation | async-start | bytes 14598144 | tf_op jit(solution)/shard_map/all_gather | solution.py:151
  10.0 4.4 %copy-start.10 = (f32[1,24,64]{2,1,0:T(8,128)S(1)}, f32[1,24,64]{2,1,0:T(8,128)}, u32[]{:S(2)}) copy-start(f32[1,24,64]{2,1,0:T(8,128)} %copy.56) | copy-start | bytes 18436
  10.0 11.6 %copy-start.3 = (f32[24,3072]{1,0:T(8,128)S(1)}, f32[24,3072]{1,0:T(8,128)}, u32[]{:S(2)}) copy-start(f32[24,3072]{1,0:T(8,128)} %param.23) | copy-start | bytes 884740
  10.0 11.6 %copy-start.9 = (f32[24,3072]{1,0:T(8,128)S(1)}, f32[24,3072]{1,0:T(8,128)}, u32[]{:S(2)}) copy-start(f32[24,3072]{1,0:T(8,128)} %param.30) | copy-start | bytes 884740
  12.0 10.5 %copy-start = (f32[3072,64]{0,1:T(8,128)S(1)}, f32[3072,64]{0,1:T(8,128)}, u32[]{:S(2)}) copy-start(f32[3072,64]{0,1:T(8,128)} %param.34) | copy-start | bytes 2359300
  15.1 8.7 %collective-permute-start = (f32[13,24,64]{2,1,0:T(8,128)}, f32[13,24,64]{2,1,0:T(8,128)}, u32[]{:S(2)}, u32[]{:S(2)}) collective-permute-start(f32[13,24,64]{2,1,0:T(8,128)} %get-tuple-element.29), channel_id=1, source_target_pairs={{0,32},{32,64},{64,96},{96,0},{1,33},{33,65},{65,97},{97,1},{2,34}... | collective-permute-start | bytes 239624 | tf_op jit(solution)/shard_map/ppermute | solution.py:66
  17.5 10.5 %collective-permute-start.1 = (f32[13,24,64]{2,1,0:T(8,128)}, f32[13,24,64]{2,1,0:T(8,128)}, u32[]{:S(2)}, u32[]{:S(2)}) collective-permute-start(f32[13,24,64]{2,1,0:T(8,128)} %get-tuple-element.29), channel_id=1, source_target_pairs={{0,64},{32,96},{64,0},{96,32},{1,65},{33,97},{65,1},{97,33},{2,66}... | collective-permute-start | bytes 239624 | tf_op jit(solution)/shard_map/ppermute | solution.py:66
  20.8 7.2 %collective-permute-start.2 = (f32[13,24,64]{2,1,0:T(8,128)}, f32[13,24,64]{2,1,0:T(8,128)}, u32[]{:S(2)}, u32[]{:S(2)}) collective-permute-start(f32[13,24,64]{2,1,0:T(8,128)} %get-tuple-element.29), channel_id=1, source_target_pairs={{0,96},{32,0},{64,32},{96,64},{1,97},{33,1},{65,33},{97,65},{2,98}... | collective-permute-start | bytes 239624 | tf_op jit(solution)/shard_map/ppermute | solution.py:66
  33.4 3.6 %copy-start.11 = (f32[4,24]{1,0:T(4,128)S(1)}, f32[4,24]{1,0:T(4,128)}, u32[]{:S(2)}) copy-start(f32[4,24]{1,0:T(4,128)} %param.25) | copy-start | bytes 1156
  33.4 3.6 %copy-start.12 = (f32[4,24]{1,0:T(4,128)S(1)}, f32[4,24]{1,0:T(4,128)}, u32[]{:S(2)}) copy-start(f32[4,24]{1,0:T(4,128)} %param.32) | copy-start | bytes 1156
  35.8 28.3 %copy-start.7 = (f32[12,24,768]{2,1,0:T(8,128)S(1)}, f32[12,24,768]{2,1,0:T(8,128)}, u32[]{:S(2)}) copy-start(f32[12,24,768]{2,1,0:T(8,128)} %get-tuple-element.24) | copy-start | bytes 2654212
Sparse Core Ops, SparseCore 0:
  33.6 68.3 all-gather.2

commit v9 on v6

--- a/solution.py
+++ b/solution.py
@@ -57,6 +57,37 @@
         ],
         cost_estimate=pl.CostEstimate(flops=0, transcendentals=0, bytes_accessed=nbytes),
     )(g)
+
+
+def factor_kernel(t_sq, s_sq, r_sq, b_sq, t_up, s_up, r_up, b_up, t_dn, s_dn, r_dn, b_dn, out):
+    highest = lax.Precision.HIGHEST
+    square, rows = s_sq.shape[0], s_sq.shape[1]
+    for m in range(square):
+        delta = s_sq[m] - t_sq[0, m] + r_sq[0, m]
+        out[m] = jnp.dot(delta, b_sq[m], precision=highest, preferred_element_type=jnp.float32)
+    delta = s_up[...] - t_up[0] + r_up[0]
+    up = jnp.dot(delta, b_up[...], precision=highest, preferred_element_type=jnp.float32)
+    blocks = (out.shape[0] - square) // 2
+    for k in range(blocks):
+        out[square + k] = up
+    delta = s_dn[...] - t_dn[0] + r_dn[0]
+    down = jnp.dot(delta, b_dn[...], precision=highest, preferred_element_type=jnp.float32)
+    for q in range(blocks):
+        out[square + blocks + q] = down[q * rows : (q + 1) * rows]
+
+
+def factors(*operands):
+    s_sq, b_sq, b_up, s_dn = operands[1], operands[3], operands[7], operands[9]
+    square, rows, _ = s_sq.shape
+    blocks = s_dn.shape[0] // rows
+    rank = b_sq.shape[-1]
+    nbytes = sum(o.size * o.dtype.itemsize for o in operands)
+    flops = 2 * rank * sum(o.size for o in operands[1:12:4])
+    return pl.pallas_call(
+        factor_kernel,
+        out_shape=jax.ShapeDtypeStruct((square + 2 * blocks, rows, rank), jnp.float32),
+        cost_estimate=pl.CostEstimate(flops=flops, transcendentals=0, bytes_accessed=nbytes),
+    )(*operands)
 
 
 def rep_sum(parts):
@@ -96,32 +127,28 @@
     groups = lax.axis_size("rep")
     square, rows, width = start_sq.shape
     rank = basis_sq.shape[-1]
+    stack = factors(
+        trained_sq, start_sq, resid_sq, basis_sq,
+        trained_up, start_up, resid_up, basis_up,
+        trained_down, start_down, resid_down, basis_down,
+    )
+    blocks_up = start_up.shape[1] // width
+    blocks_down = start_down.shape[0] // rows
+    factor_sq = stack[:square]
+    factor_up = stack[square]
+    factor_down = stack[square + blocks_up :].reshape(-1, rank)
     delta_sq = start_sq - trained_sq[0] + resid_sq[0]
-    factor_sq = jnp.einsum("mrd,mdk->mrk", delta_sq, basis_sq, precision=highest)
     new_resid_sq = delta_sq - jnp.einsum("mrk,mdk->mrd", factor_sq, basis_sq, precision=highest)
     delta_up = start_up - trained_up[0] + resid_up[0]
-    factor_up = jnp.dot(delta_up, basis_up, precision=highest, preferred_element_type=jnp.float32)
     new_resid_up = delta_up - jnp.einsum("rk,fk->rf", factor_up, basis_up, precision=highest)
     delta_down = start_down - trained_down[0] + resid_down[0]
-    factor_down = jnp.dot(
-        delta_down, basis_down, precision=highest, preferred_element_type=jnp.float32
-    )
     new_resid_down = delta_down - jnp.einsum(
         "rk,dk->rd", factor_down, basis_down, precision=highest
     )
     norm_delta = start_ln - trained_ln[0]
-    blocks_up = start_up.shape[1] // width
-    blocks_down = start_down.shape[0] // rows
     norm_cols = norm_delta.shape[0]
     norm_block = jnp.pad(norm_delta.T, ((0, 0), (0, rank - norm_cols)))
-    stacked = jnp.concatenate(
-        [
-            factor_sq,
-            jnp.broadcast_to(factor_up[None], (blocks_up, rows, rank)),
-            factor_down.reshape(blocks_down, rows, rank),
-            norm_block[None],
-        ]
-    )
+    stacked = jnp.concatenate([stack, norm_block[None]])
     summed = rep_sum(stacked) / groups
     mean_all = summed[:-1]
     mean_ln = summed[-1, :, :norm_cols].T

time: 117 us -> 122 us (1.043)
  local copies, waits for them, and re-layouts: 4.54 us -> 10.4 us
  Pallas kernels: 10.1 us -> 15.2 us
  matrix products: 13.2 us -> 8.7 us
    unnamed x45 -> x38, local copies, waits for them, and re-layouts: 0.83 us -> 6.14 us
    pallas_call x0 -> x1, Pallas kernels: none -> 5.07 us  [factors(): pl.pallas_call(factor_kernel, out_shape=jax.ShapeDtypeStruct((square + 2...]
    dot_general x3 -> x0, matrix products: 4.68 us -> none  [the longest x1 2.22 us: on_device(): jnp.dot(delta_up, basis_up, precision=highest, preferred_element_type=jnp...]
    reshape x0 -> x2, local copies, waits for them, and re-layouts: none -> 1.47 us  [split_cols(): return a.reshape(a.shape[0], -1, width).transpose(1, 0, 2)]
  transfers between devices with their start and end apart: 4 -> 4, of which waited for: 3 -> 2; matrix products, arithmetic and copies ran while one was open for 8% -> 8% of each run, Pallas kernels for 0% -> 0%
where the time goes in v9:
time: 122 us
  waiting for transfers between devices  38.8 us (32%)
  blocking collectives  25.8 us (21%)
  Pallas kernels  15.2 us (12%)
  between operations  14.2 us (12%)
  local copies, waits for them, and re-layouts  10.4 us (9%)
  matrix products  8.7 us (7%)
  starting transfers between devices  6.6 us (5%)
  other arithmetic  2.39 us (2%)
    all_gather x1, waiting for transfers between devices, on_device(): gathered = lax.all_gather(owned_all, 'shard', axis=1, tiled=True)  35 us
    all_gather x1, blocking collectives, on_device(): weights_ln = lax.all_gather(norm_weights, 'shard', axis=1, tiled=True)  25.8 us
    pallas_call x1, Pallas kernels, unpack(): pl.pallas_call(functools.partial(unpack_kernel, rows), grid=(total // ste...  10.1 us
    ppermute x3, starting transfers between devices, rep_sum(): lax.ppermute(parts, 'rep', [(i, (i + d) % n) for i in range(n)])  6.57 us
    unnamed x38, local copies, waits for them, and re-layouts  6.14 us
    pallas_call x1, Pallas kernels, factors(): pl.pallas_call(factor_kernel, out_shape=jax.ShapeDtypeStruct((square + 2...  5.07 us
    dot_general x1, matrix products, on_device(): jnp.einsum('brk,bdk->brd', mean_all, basis_all, precision=highest)  4.12 us
    ppermute x3, waiting for transfers between devices, rep_sum(): lax.ppermute(parts, 'rep', [(i, (i + d) % n) for i in range(n)])  3.79 us
  transfers between devices with their start and end apart: 4, of which 2 were waited for; matrix products, arithmetic and copies ran while one was open for 8% of the time, Pallas kernels for 0%

profile of v9, /device:TPU:1, one launch (start us, length us, event | category | flops | bytes accessed | tf_op | source)
XLA Modules:
  0.0 122.1 jit_solution(3489386951728907707)
XLA Ops:
  7.2 0.0 copy-start
  7.2 0.0 copy-start.3
  7.2 0.0 copy-start.15
  7.2 0.0 all-gather.3.cloned.1.call-start
  7.3 2.8 %copy.57.b_sq = f32[4,768,64]{2,1,0:T(8,128)} copy(f32[4,768,64]{1,2,0:T(8,128)} %param.33) | data formatting | bytes 1572864 | tf_op args[15]
  10.1 1.6 %copy.58.b_up = f32[3072,64]{1,0:T(8,128)} copy(f32[3072,64]{0,1:T(8,128)S(1)} %copy-done) | data formatting | bytes 1572864 | tf_op args[16]
  11.7 0.0 copy-done.3
  11.7 0.9 copy.59.b_dn
  12.6 0.1 copy.61
  12.7 5.1 %shard_map.257 = f32[12,24,64]{2,1,0:T(8,128)} custom-call(f32[1,4,24,768]{3,2,1,0:T(8,128)} %t_sq.1, f32[4,24,768]{2,1,0:T(8,128)} %s_sq.1, f32[1,4,24,768]{3,2,1,0:T(8,128)} %r_sq.1, f32[4,768,64]{2,1,0:T(8,128)} %copy.57.b_sq, f32[1,24,3072]{2,1,0:T(8,128)} %t_up.1, f32[24,3072]{1,0:T(8,128)} %s_up.1, f32[1,24,3072]{2,1,0:T(8,128)} %r_up.1, ...), custom_call_target="tpu_custom_call" | custom-call | flops 28311552 | bytes 4423680 | tf_op jit(solution)/shard_map/pallas_call | solution.py:86
  17.8 1.0 fusion.13
  18.8 2.5 %collective-permute-start = (f32[13,24,64]{2,1,0:T(8,128)S(1)}, f32[13,24,64]{2,1,0:T(8,128)S(1)}, u32[]{:S(2)}, u32[]{:S(2)}) collective-permute-start(f32[13,24,64]{2,1,0:T(8,128)S(1)} %get-tuple-element.29), channel_id=1, source_target_pairs={{0,32},{32,64},{64,96},{96,0},{1,33},{33,65},{65,97},{97,1},{2,34}... | collective-permute-start | bytes 239624 | tf_op jit(solution)/shard_map/ppermute | solution.py:97
  21.3 3.3 %collective-permute-start.1 = (f32[13,24,64]{2,1,0:T(8,128)S(1)}, f32[13,24,64]{2,1,0:T(8,128)S(1)}, u32[]{:S(2)}, u32[]{:S(2)}) collective-permute-start(f32[13,24,64]{2,1,0:T(8,128)S(1)} %get-tuple-element.29), channel_id=1, source_target_pairs={{0,64},{32,96},{64,0},{96,32},{1,65},{33,97},{65,1},{97,33},{2,66}... | collective-permute-start | bytes 239624 | tf_op jit(solution)/shard_map/ppermute | solution.py:97
  24.6 0.7 collective-permute-start.2
  25.4 0.9 copy.74
  26.3 0.7 copy.75
  27.1 0.7 copy.76
  27.8 0.0 collective-permute-done
  27.8 3.8 %collective-permute-done.1 = f32[13,24,64]{2,1,0:T(8,128)S(1)} collective-permute-done((f32[13,24,64]{2,1,0:T(8,128)S(1)}, f32[13,24,64]{2,1,0:T(8,128)S(1)}, u32[]{:S(2)}, u32[]{:S(2)}) %collective-permute-start.1) | collective-permute-done | bytes 79904 | tf_op jit(solution)/shard_map/ppermute | solution.py:97
  31.6 0.0 collective-permute-done.2
  31.6 0.7 add_multiply_fusion
  32.4 0.1 copy.65
  32.5 0.1 broadcast_in_dim.22
  32.6 0.0 slice-start
  32.6 0.0 copy-start.5
  32.6 0.0 copy-start.7
  32.6 0.0 copy-start.4
  32.6 0.0 copy-start.8
  32.6 4.1 %fusion.10 = (bf16[12,24,768]{2,1,0:T(8,128)(2,1)}, f32[12,24,768]{2,1,0:T(8,128)}) fusion(f32[4,24,768]{2,1,0:T(8,128)S(1)} %bitcast.96, f32[4,24,768]{2,1,0:T(8,128)} %bitcast.100, f32[4,24,768]{2,1,0:T(8,128)} %s_sq.1, f32[4,24,768]{2,1,0:T(8,128)} %bitcast.109, f32[4,24,768]{2,1,0:T(8,128)} %bitcast.101, f32[4,24,768]{2,1,0:T(8,128)} %param.29, ...), kind=kOutput, calls=%fused_computation.15 | convolution fusion | flops 173481984 | bytes 5603328 | tf_op jit(solution)/shard_map/brk,bdk->brd/dot_general | solution.py:168
  36.7 0.0 all-gather.3.cloned.1.call-update
  36.8 0.0 copy-start.9
  36.8 0.0 copy-start.10
  36.8 0.0 copy-start.11
  36.8 1.1 fusion.7
  37.9 0.0 copy-done.4
  38.0 2.3 %fusion = f32[1,24,3072]{2,1,0:T(8,128)} fusion(f32[3072,64]{0,1:T(8,128)S(1)} %copy-done, f32[1,24,3072]{2,1,0:T(8,128)} %r_up.1, f32[24,3072]{1,0:T(8,128)S(1)} %copy-done.2, f32[1,24,3072]{2,1,0:T(8,128)S(1)} %copy-done.8, f32[12,24,64]{2,1,0:T(8,128)S(1)} %copy-done.4), kind=kOutput, calls=%fused_computation.1 | convolution fusion | flops 56844288 | bytes 1978368 | tf_op jit(solution)/shard_map/rk,fk->rf/dot_general | solution.py:143
  40.2 0.0 copy-done.9
  40.2 0.0 copy-done.11
  40.2 1.2 fusion.8
  41.4 0.0 copy-done.16
  41.4 0.6 fusion.11
  42.0 25.8 %all-gather = bf16[32,24,4]{1,2,0:T(4,128)(2,1)S(1)} all-gather(bf16[1,24,4]{1,2,0:T(4,128)(2,1)S(1)} %get-tuple-element.21), channel_id=1, replica_groups=mesh['rep'=4,'shard'=32] {'shard'}, dimensions={0}, use_global_device_ids=true | all-gather | bytes 6336 | tf_op jit(solution)/shard_map/all_gather | solution.py:177
  67.8 0.7 reshape.66
  68.6 0.0 copy-done.12
  68.6 0.9 fusion.14
  69.4 0.7 copy.70
  70.2 35.0 %all-gather.3.cloned.1.call-done = bf16[12,768,768]{2,1,0:T(8,128)(2,1)} async-done(((bf16[12,24,768]{2,1,0:T(8,128)(2,1)}), bf16[12,768,768]{2,1,0:T(8,128)(2,1)}) %all-gather.3.cloned.1.call-update) | async-done | bytes 14155792 | tf_op jit(solution)/shard_map/all_gather | solution.py:175
  105.2 10.1 %shard_map.258 = (bf16[4,768,768]{2,1,0:T(8,128)(2,1)}, bf16[768,3072]{1,0:T(8,128)(2,1)}, bf16[3072,768]{1,0:T(8,128)(2,1)}) custom-call(bf16[3,4,768,768]{3,2,1,0:T(8,128)(2,1)} %bitcast.92), custom_call_target="tpu_custom_call" | custom-call | bytes 28311552 | tf_op jit(solution)/shard_map/pallas_call | solution.py:44
  (25 shorter events, 0.1 us)
Async XLA Ops:
  7.2 2.9 %copy-start = (f32[3072,64]{0,1:T(8,128)S(1)}, f32[3072,64]{0,1:T(8,128)}, u32[]{:S(2)}) copy-start(f32[3072,64]{0,1:T(8,128)} %param.34) | copy-start | bytes 2359300
  7.2 4.5 %copy-start.3 = (f32[768,64]{0,1:T(8,128)S(1)}, f32[768,64]{0,1:T(8,128)}, u32[]{:S(2)}) copy-start(f32[768,64]{0,1:T(8,128)} %param.35) | copy-start | bytes 589828
  7.2 5.4 %copy-start.15 = (f32[1,4,24]{2,1,0:T(4,128)S(1)}, f32[1,4,24]{2,1,0:T(4,128)}, u32[]{:S(2)}) copy-start(f32[1,4,24]{2,1,0:T(4,128)} %param.21) | copy-start | bytes 1156
  7.2 5.4 %copy-start.14 = (f32[4,24]{1,0:T(4,128)S(1)}, f32[4,24]{1,0:T(4,128)}, u32[]{:S(2)}) copy-start(f32[4,24]{1,0:T(4,128)} %param.25) | copy-start | bytes 1156
  7.2 98.0 %all-gather.3.cloned.1.call-start = ((), (), s32[]{:S(2)}) async-start(), calls=%async_computation | async-start | bytes 14598144 | tf_op jit(solution)/shard_map/all_gather | solution.py:175
  17.8 8.5 %copy-start.2 = (f32[24,3072]{1,0:T(8,128)S(1)}, f32[24,3072]{1,0:T(8,128)}, u32[]{:S(2)}) copy-start(f32[24,3072]{1,0:T(8,128)} %s_up.1) | copy-start | bytes 884740
  17.8 9.3 %copy-start.13 = (f32[24,3072]{1,0:T(8,128)S(1)}, f32[24,3072]{1,0:T(8,128)}, u32[]{:S(2)}) copy-start(f32[24,3072]{1,0:T(8,128)} %param.30) | copy-start | bytes 884740
  18.8 9.0 %collective-permute-start = (f32[13,24,64]{2,1,0:T(8,128)S(1)}, f32[13,24,64]{2,1,0:T(8,128)S(1)}, u32[]{:S(2)}, u32[]{:S(2)}) collective-permute-start(f32[13,24,64]{2,1,0:T(8,128)S(1)} %get-tuple-element.29), channel_id=1, source_target_pairs={{0,32},{32,64},{64,96},{96,0},{1,33},{33,65},{65,97},{97,1},{2,34}... | collective-permute-start | bytes 239624 | tf_op jit(solution)/shard_map/ppermute | solution.py:97
  21.3 10.2 %collective-permute-start.1 = (f32[13,24,64]{2,1,0:T(8,128)S(1)}, f32[13,24,64]{2,1,0:T(8,128)S(1)}, u32[]{:S(2)}, u32[]{:S(2)}) collective-permute-start(f32[13,24,64]{2,1,0:T(8,128)S(1)} %get-tuple-element.29), channel_id=1, source_target_pairs={{0,64},{32,96},{64,0},{96,32},{1,65},{33,97},{65,1},{97,33},{2,66}... | collective-permute-start | bytes 239624 | tf_op jit(solution)/shard_map/ppermute | solution.py:97
  24.6 6.9 %collective-permute-start.2 = (f32[13,24,64]{2,1,0:T(8,128)S(1)}, f32[13,24,64]{2,1,0:T(8,128)S(1)}, u32[]{:S(2)}, u32[]{:S(2)}) collective-permute-start(f32[13,24,64]{2,1,0:T(8,128)S(1)} %get-tuple-element.29), channel_id=1, source_target_pairs={{0,96},{32,0},{64,32},{96,64},{1,97},{33,1},{65,33},{97,65},{2,98}... | collective-permute-start | bytes 239624 | tf_op jit(solution)/shard_map/ppermute | solution.py:97
  27.0 5.5 %copy-start.1 = (f32[4,768,64]{1,2,0:T(8,128)S(1)}, f32[4,768,64]{1,2,0:T(8,128)}, u32[]{:S(2)}) copy-start(f32[4,768,64]{1,2,0:T(8,128)} %param.33) | copy-start | bytes 2359300
  27.1 5.5 %copy-start.6 = (f32[96,768]{1,0:T(8,128)S(1)}, f32[96,768]{1,0:T(8,128)}, u32[]{:S(2)}) copy-start(f32[96,768]{1,0:T(8,128)} %s_dn.1) | copy-start | bytes 884740
  32.6 4.2 %slice-start = ((f32[12,24,64]{2,1,0:T(8,128)}), f32[4,24,64]{2,1,0:T(8,128)S(1)}, s32[]{:S(2)}) async-start(f32[12,24,64]{2,1,0:T(8,128)} %shard_map.257), calls=%async_computation.1 | async-start | bytes 98304 | tf_op jit(solution)/shard_map/slice | solution.py:139
  32.6 4.2 %copy-start.5 = (f32[1,96,768]{2,1,0:T(8,128)S(1)}, f32[1,96,768]{2,1,0:T(8,128)}, u32[]{:S(2)}) copy-start(f32[1,96,768]{2,1,0:T(8,128)} %t_dn.1) | copy-start | bytes 884740
  32.6 4.2 %copy-start.7 = (f32[1,96,768]{2,1,0:T(8,128)S(1)}, f32[1,96,768]{2,1,0:T(8,128)}, u32[]{:S(2)}) copy-start(f32[1,96,768]{2,1,0:T(8,128)} %r_dn.1) | copy-start | bytes 884740
  32.6 5.3 %copy-start.4 = (f32[12,24,64]{2,1,0:T(8,128)S(1)}, f32[12,24,64]{2,1,0:T(8,128)}, u32[]{:S(2)}) copy-start(f32[12,24,64]{2,1,0:T(8,128)} %shard_map.257) | copy-start | bytes 221188
  32.6 5.3 %copy-start.8 = (f32[1,24,3072]{2,1,0:T(8,128)S(1)}, f32[1,24,3072]{2,1,0:T(8,128)}, u32[]{:S(2)}) copy-start(f32[1,24,3072]{2,1,0:T(8,128)} %t_up.1) | copy-start | bytes 884740
  36.8 3.4 %copy-start.9 = (f32[1,4,24,768]{3,2,1,0:T(8,128)S(1)}, f32[1,4,24,768]{3,2,1,0:T(8,128)}, u32[]{:S(2)}) copy-start(f32[1,4,24,768]{3,2,1,0:T(8,128)} %t_sq.1) | copy-start | bytes 884740
  36.8 3.4 %copy-start.10 = (f32[4,24,768]{2,1,0:T(8,128)S(1)}, f32[4,24,768]{2,1,0:T(8,128)}, u32[]{:S(2)}) copy-start(f32[4,24,768]{2,1,0:T(8,128)} %s_sq.1) | copy-start | bytes 884740
  36.8 3.4 %copy-start.11 = (f32[1,4,24,768]{3,2,1,0:T(8,128)S(1)}, f32[1,4,24,768]{3,2,1,0:T(8,128)}, u32[]{:S(2)}) copy-start(f32[1,4,24,768]{3,2,1,0:T(8,128)} %r_sq.1) | copy-start | bytes 884740
  37.9 3.5 %copy-start.16 = (f32[4,24]{1,0:T(4,128)S(1)}, f32[4,24]{1,0:T(4,128)}, u32[]{:S(2)}) copy-start(f32[4,24]{1,0:T(4,128)} %param.32) | copy-start | bytes 1156
  38.0 30.6 %copy-start.12 = (f32[12,24,768]{2,1,0:T(8,128)S(1)}, f32[12,24,768]{2,1,0:T(8,128)}, u32[]{:S(2)}) copy-start(f32[12,24,768]{2,1,0:T(8,128)} %get-tuple-element.24) | copy-start | bytes 2654212
Sparse Core Ops, SparseCore 0:
  36.9 68.2 all-gather.2

commit v10 on v5

--- a/solution.py
+++ b/solution.py
@@ -143,7 +143,9 @@
             jnp.broadcast_to(basis_down[None], (blocks_down, width, rank)),
         ]
     )
-    outer_all = jnp.einsum("brk,bdk->brd", mean_all, basis_all, precision=highest)
+    outer_all = jnp.einsum(
+        "brk,bdk->brd", mean_all, basis_all, precision=lax.Precision.HIGH
+    )
     new_mom_all, owned_all = advance(start_all, mom_all, outer_all)
     new_mom_sq = new_mom_all[:square]
     new_mom_up = join_cols(new_mom_all[square : square + blocks_up])

time: 117 us -> 116 us (level)
  no operation moved by 1% of the time
where the time goes in v10:
time: 116 us
  waiting for transfers between devices  35.3 us (30%)
  blocking collectives  26.5 us (23%)
  between operations  14.4 us (12%)
  matrix products  12.9 us (11%)
  Pallas kernels  10.1 us (9%)
  local copies, waits for them, and re-layouts  8.49 us (7%)
  starting transfers between devices  6.6 us (6%)
  other arithmetic  1.69 us (1%)
    all_gather x1, waiting for transfers between devices, on_device(): gathered = lax.all_gather(owned_all, 'shard', axis=1, tiled=True)  35.2 us
    all_gather x1, blocking collectives, on_device(): weights_ln = lax.all_gather(norm_weights, 'shard', axis=1, tiled=True)  26.5 us
    pallas_call x1, Pallas kernels, unpack(): pl.pallas_call(functools.partial(unpack_kernel, rows), grid=(total // ste...  10.1 us
    ppermute x3, starting transfers between devices, rep_sum(): lax.ppermute(parts, 'rep', [(i, (i + d) % n) for i in range(n)])  6.57 us
    dot_general x1, matrix products, on_device(): jnp.einsum('brk,bdk->brd', mean_all, basis_all, precision=lax.Precision.H...  3.58 us
  transfers between devices with their start and end apart: 4, of which 1 were waited for; matrix products, arithmetic and copies ran while one was open for 8% of the time, Pallas kernels for 0%

profile of v10, /device:TPU:1, one launch (start us, length us, event | category | flops | bytes accessed | tf_op | source)
XLA Modules:
  0.0 115.9 jit_solution(7757493398576490046)
XLA Ops:
  7.2 0.0 copy-start
  7.3 0.0 all-gather.3.cloned.1.call-start
  7.3 2.3 %fusion.18 = f32[4,24,64]{2,1,0:T(8,128)S(1)} fusion(f32[4,768,64]{1,2,0:T(8,128)} %param.33, f32[1,4,24,768]{3,2,1,0:T(8,128)} %param.26, f32[4,24,768]{2,1,0:T(8,128)} %param.22, f32[1,4,24,768]{3,2,1,0:T(8,128)} %param.18), kind=kOutput, calls=%fused_computation.40 | convolution fusion | flops 56770560 | bytes 1695744 | tf_op jit(solution)/shard_map/mrd,mdk->mrk/dot_general | solution.py:100
  9.6 0.0 copy-start.14
  9.6 0.6 copy-done.14
  10.2 0.1 copy.49
  10.3 0.0 copy-start.2
  10.3 2.2 %fusion.19 = f32[24,64]{1,0:T(8,128)S(1)} fusion(f32[3072,64]{0,1:T(8,128)} %param.34, f32[1,24,3072]{2,1,0:T(8,128)} %param.27, f32[24,3072]{1,0:T(8,128)} %param.23, f32[1,24,3072]{2,1,0:T(8,128)} %param.19), kind=kOutput, calls=%fused_computation.41 | convolution fusion | flops 56770560 | bytes 1677312 | tf_op jit(solution)/shard_map/dot_general | solution.py:103
  12.5 0.0 copy-start.16
  12.5 0.1 copy.50
  12.6 0.1 reshape.84
  12.7 0.1 reshape.85
  12.8 0.1 copy.51
  12.9 0.4 fusion.20
  13.3 0.1 pad_maximum_fusion.1
  13.4 2.5 %collective-permute-start = (f32[218,64]{0,1:T(8,128)S(1)}, f32[218,64]{0,1:T(8,128)S(1)}, u32[]{:S(2)}, u32[]{:S(2)}) collective-permute-start(f32[218,64]{0,1:T(8,128)S(1)} %pad_maximum_fusion.1), channel_id=1, source_target_pairs={{0,32},{32,64},{64,96},{96,0},{1,33},{33,65},{65,97},{97,1},{2,34}... | collective-permute-start | bytes 167432 | tf_op jit(solution)/shard_map/ppermute | solution.py:66
  16.0 3.3 %collective-permute-start.1 = (f32[218,64]{0,1:T(8,128)S(1)}, f32[218,64]{0,1:T(8,128)S(1)}, u32[]{:S(2)}, u32[]{:S(2)}) collective-permute-start(f32[218,64]{0,1:T(8,128)S(1)} %pad_maximum_fusion.1), channel_id=1, source_target_pairs={{0,64},{32,96},{64,0},{96,32},{1,65},{33,97},{65,1},{97,33},{2,66}... | collective-permute-start | bytes 167432 | tf_op jit(solution)/shard_map/ppermute | solution.py:66
  19.3 0.7 collective-permute-start.2
  20.0 0.1 fusion.32
  20.2 0.0 copy-start.1
  20.2 0.9 copy.67
  21.2 0.7 copy.68
  21.9 0.7 copy.69
  22.6 0.1 collective-permute-done.2
  22.7 0.9 pad_maximum_fusion
  23.6 0.1 fusion.22
  23.6 0.1 slice_bitcast_fusion.1
  23.7 0.1 slice.45
  23.8 0.7 copy.52
  24.5 0.7 copy.54
  25.2 0.1 copy.53
  25.3 0.1 copy.58
  25.4 0.1 reshape.93
  25.4 0.7 reshape.94
  26.1 0.1 broadcast_in_dim.25
  26.2 0.0 copy-start.5
  26.2 3.6 %fusion.10 = (bf16[12,24,768]{2,1,0:T(8,128)(2,1)}, f32[12,24,768]{2,1,0:T(8,128)}) fusion(f32[4,24,768]{2,1,0:T(8,128)S(1)} %bitcast.100, f32[4,24,768]{2,1,0:T(8,128)} %bitcast.105, f32[4,24,768]{2,1,0:T(8,128)} %param.22, f32[4,24,768]{2,1,0:T(8,128)} %bitcast.114, f32[4,24,768]{2,1,0:T(8,128)} %bitcast.106, f32[4,24,768]{2,1,0:T(8,128)} %param.29, ...), kind=kOutput, calls=%fused_computation.15 | convolution fusion | flops 88584192 | bytes 5529600 | tf_op jit(solution)/shard_map/brk,bdk->brd/dot_general | solution.py:146
  29.8 0.0 all-gather.3.cloned.1.call-update
  29.9 2.0 %fusion.7 = f32[1,96,768]{2,1,0:T(8,128)} fusion(f32[96,64]{0,1:T(8,128)} %copy-done.13, f32[768,64]{0,1:T(8,128)S(1)} %copy-done.3, f32[1,96,768]{2,1,0:T(8,128)S(1)} %copy-done.6, f32[96,768]{1,0:T(8,128)S(1)} %copy-done.7, f32[1,96,768]{2,1,0:T(8,128)S(1)} %copy-done.8), kind=kOutput, calls=%fused_computation.9 | convolution fusion | flops 56844288 | bytes 1400832 | tf_op jit(solution)/shard_map/rk,dk->rd/dot_general | solution.py:109
  31.9 1.2 %fusion = f32[1,24,3072]{2,1,0:T(8,128)} fusion(f32[24,64]{1,0:T(8,128)S(1)} %fusion.19, f32[3072,64]{0,1:T(8,128)S(1)} %copy-done, f32[1,24,3072]{2,1,0:T(8,128)S(1)} %copy-done.4, f32[24,3072]{1,0:T(8,128)S(1)} %copy-done.2, f32[1,24,3072]{2,1,0:T(8,128)S(1)} %copy-done.5), kind=kOutput, calls=%fused_computation.1 | convolution fusion | flops 56844288 | bytes 1972224 | tf_op jit(solution)/shard_map/rk,fk->rf/dot_general | solution.py:104
  33.1 1.2 %fusion.8 = f32[1,4,24,768]{3,2,1,0:T(8,128)} fusion(f32[4,24,64]{2,1,0:T(8,128)S(1)} %copy-done.15, f32[4,768,64]{1,2,0:T(8,128)S(1)} %copy-done.1, f32[1,4,24,768]{3,2,1,0:T(8,128)S(1)} %copy-done.9, f32[4,24,768]{2,1,0:T(8,128)S(1)} %copy-done.10, f32[1,4,24,768]{3,2,1,0:T(8,128)S(1)} %copy-done.11), kind=kOutput, calls=%fused_computation.11 | convolution fusion | flops 56844288 | bytes 1990656 | tf_op jit(solution)/shard_map/mrk,mdk->mrd/dot_general | solution.py:101
  34.4 0.6 fusion.16
  35.0 26.5 %all-gather = bf16[32,24,4]{1,2,0:T(4,128)(2,1)S(1)} all-gather(bf16[1,24,4]{1,2,0:T(4,128)(2,1)S(1)} %get-tuple-element.21), channel_id=1, replica_groups=mesh['rep'=4,'shard'=32] {'shard'}, dimensions={0}, use_global_device_ids=true | all-gather | bytes 6336 | tf_op jit(solution)/shard_map/all_gather | solution.py:157
  61.4 0.7 reshape.97
  62.1 0.9 fusion.21
  63.0 0.7 copy.63
  63.7 35.2 %all-gather.3.cloned.1.call-done = bf16[12,768,768]{2,1,0:T(8,128)(2,1)} async-done(((bf16[12,24,768]{2,1,0:T(8,128)(2,1)}), bf16[12,768,768]{2,1,0:T(8,128)(2,1)}) %all-gather.3.cloned.1.call-update) | async-done | bytes 14155792 | tf_op jit(solution)/shard_map/all_gather | solution.py:155
  98.9 10.1 %shard_map.257 = (bf16[4,768,768]{2,1,0:T(8,128)(2,1)}, bf16[768,3072]{1,0:T(8,128)(2,1)}, bf16[3072,768]{1,0:T(8,128)(2,1)}) custom-call(bf16[3,4,768,768]{3,2,1,0:T(8,128)(2,1)} %bitcast.97), custom_call_target="tpu_custom_call" | custom-call | bytes 28311552 | tf_op jit(solution)/shard_map/pallas_call | solution.py:44
  (42 shorter events, 0.1 us)
Async XLA Ops:
  7.2 13.0 %copy-start = (f32[3072,64]{0,1:T(8,128)S(1)}, f32[3072,64]{0,1:T(8,128)}, u32[]{:S(2)}) copy-start(f32[3072,64]{0,1:T(8,128)} %param.34) | copy-start | bytes 2359300
  7.2 5.4 %copy-start.19 = (f32[1,4,24]{2,1,0:T(4,128)S(1)}, f32[1,4,24]{2,1,0:T(4,128)}, u32[]{:S(2)}) copy-start(f32[1,4,24]{2,1,0:T(4,128)} %param.21) | copy-start | bytes 1156
  7.2 5.4 %copy-start.17 = (f32[4,24]{1,0:T(4,128)S(1)}, f32[4,24]{1,0:T(4,128)}, u32[]{:S(2)}) copy-start(f32[4,24]{1,0:T(4,128)} %param.25) | copy-start | bytes 1156
  7.2 5.7 %copy-start.8 = (f32[1,96,768]{2,1,0:T(8,128)S(1)}, f32[1,96,768]{2,1,0:T(8,128)}, u32[]{:S(2)}) copy-start(f32[1,96,768]{2,1,0:T(8,128)} %param.20) | copy-start | bytes 884740
  7.2 5.7 %copy-start.7 = (f32[96,768]{1,0:T(8,128)S(1)}, f32[96,768]{1,0:T(8,128)}, u32[]{:S(2)}) copy-start(f32[96,768]{1,0:T(8,128)} %param.24) | copy-start | bytes 884740
  7.2 5.7 %copy-start.6 = (f32[1,96,768]{2,1,0:T(8,128)S(1)}, f32[1,96,768]{2,1,0:T(8,128)}, u32[]{:S(2)}) copy-start(f32[1,96,768]{2,1,0:T(8,128)} %param.28) | copy-start | bytes 884740
  7.2 5.7 %copy-start.3 = (f32[768,64]{0,1:T(8,128)S(1)}, f32[768,64]{0,1:T(8,128)}, u32[]{:S(2)}) copy-start(f32[768,64]{0,1:T(8,128)} %param.35) | copy-start | bytes 589828
  7.3 91.7 %all-gather.3.cloned.1.call-start = ((), (), s32[]{:S(2)}) async-start(), calls=%async_computation | async-start | bytes 14598144 | tf_op jit(solution)/shard_map/all_gather | solution.py:155
  9.6 0.6 copy-start.14
  10.3 10.9 %copy-start.2 = (f32[24,3072]{1,0:T(8,128)S(1)}, f32[24,3072]{1,0:T(8,128)}, u32[]{:S(2)}) copy-start(f32[24,3072]{1,0:T(8,128)} %param.23) | copy-start | bytes 884740
  12.5 9.4 %copy-start.16 = (f32[24,3072]{1,0:T(8,128)S(1)}, f32[24,3072]{1,0:T(8,128)}, u32[]{:S(2)}) copy-start(f32[24,3072]{1,0:T(8,128)} %param.30) | copy-start | bytes 884740
  13.3 6.7 %copy-start.13 = (f32[96,64]{0,1:T(8,128)}, f32[96,64]{0,1:T(8,128)S(1)}, u32[]{:S(2)}) copy-start(f32[96,64]{0,1:T(8,128)S(1)} %fusion.20) | copy-start | bytes 73732
  13.4 9.2 %collective-permute-start = (f32[218,64]{0,1:T(8,128)S(1)}, f32[218,64]{0,1:T(8,128)S(1)}, u32[]{:S(2)}, u32[]{:S(2)}) collective-permute-start(f32[218,64]{0,1:T(8,128)S(1)} %pad_maximum_fusion.1), channel_id=1, source_target_pairs={{0,32},{32,64},{64,96},{96,0},{1,33},{33,65},{65,97},{97,1},{2,34}... | collective-permute-start | bytes 167432 | tf_op jit(solution)/shard_map/ppermute | solution.py:66
  16.0 6.7 %collective-permute-start.1 = (f32[218,64]{0,1:T(8,128)S(1)}, f32[218,64]{0,1:T(8,128)S(1)}, u32[]{:S(2)}, u32[]{:S(2)}) collective-permute-start(f32[218,64]{0,1:T(8,128)S(1)} %pad_maximum_fusion.1), channel_id=1, source_target_pairs={{0,64},{32,96},{64,0},{96,32},{1,65},{33,97},{65,1},{97,33},{2,66}... | collective-permute-start | bytes 167432 | tf_op jit(solution)/shard_map/ppermute | solution.py:66
  19.3 3.4 %collective-permute-start.2 = (f32[218,64]{0,1:T(8,128)S(1)}, f32[218,64]{0,1:T(8,128)}, u32[]{:S(2)}, u32[]{:S(2)}) collective-permute-start(f32[218,64]{0,1:T(8,128)S(1)} %pad_maximum_fusion.1), channel_id=1, source_target_pairs={{0,96},{32,0},{64,32},{96,64},{1,97},{33,1},{65,33},{97,65},{2,98}... | collective-permute-start | bytes 167432 | tf_op jit(solution)/shard_map/ppermute | solution.py:66
  20.2 6.0 %copy-start.1 = (f32[4,768,64]{1,2,0:T(8,128)S(1)}, f32[4,768,64]{1,2,0:T(8,128)}, u32[]{:S(2)}) copy-start(f32[4,768,64]{1,2,0:T(8,128)} %param.33) | copy-start | bytes 2359300
  26.2 5.7 %copy-start.4 = (f32[1,24,3072]{2,1,0:T(8,128)S(1)}, f32[1,24,3072]{2,1,0:T(8,128)}, u32[]{:S(2)}) copy-start(f32[1,24,3072]{2,1,0:T(8,128)} %param.27) | copy-start | bytes 884740
  26.2 5.7 %copy-start.5 = (f32[1,24,3072]{2,1,0:T(8,128)S(1)}, f32[1,24,3072]{2,1,0:T(8,128)}, u32[]{:S(2)}) copy-start(f32[1,24,3072]{2,1,0:T(8,128)} %param.19) | copy-start | bytes 884740
  29.8 3.3 %copy-start.9 = (f32[1,4,24,768]{3,2,1,0:T(8,128)S(1)}, f32[1,4,24,768]{3,2,1,0:T(8,128)}, u32[]{:S(2)}) copy-start(f32[1,4,24,768]{3,2,1,0:T(8,128)} %param.26) | copy-start | bytes 884740
  29.9 3.3 %copy-start.10 = (f32[4,24,768]{2,1,0:T(8,128)S(1)}, f32[4,24,768]{2,1,0:T(8,128)}, u32[]{:S(2)}) copy-start(f32[4,24,768]{2,1,0:T(8,128)} %param.22) | copy-start | bytes 884740
  29.9 3.3 %copy-start.11 = (f32[1,4,24,768]{3,2,1,0:T(8,128)S(1)}, f32[1,4,24,768]{3,2,1,0:T(8,128)}, u32[]{:S(2)}) copy-start(f32[1,4,24,768]{3,2,1,0:T(8,128)} %param.18) | copy-start | bytes 884740
  29.9 3.3 %copy-start.15 = (f32[4,24,64]{2,1,0:T(8,128)S(1)}, f32[4,24,64]{2,1,0:T(8,128)}, u32[]{:S(2)}) copy-start(f32[4,24,64]{2,1,0:T(8,128)} %copy-done.14) | copy-start | bytes 73732
  29.9 4.5 %copy-start.18 = (f32[4,24]{1,0:T(4,128)S(1)}, f32[4,24]{1,0:T(4,128)}, u32[]{:S(2)}) copy-start(f32[4,24]{1,0:T(4,128)} %reshape.94) | copy-start | bytes 1156
  29.9 4.5 %copy-start.20 = (f32[4,24]{1,0:T(4,128)S(1)}, f32[4,24]{1,0:T(4,128)}, u32[]{:S(2)}) copy-start(f32[4,24]{1,0:T(4,128)} %param.32) | copy-start | bytes 1156
  31.9 30.2 %copy-start.12 = (f32[12,24,768]{2,1,0:T(8,128)S(1)}, f32[12,24,768]{2,1,0:T(8,128)}, u32[]{:S(2)}) copy-start(f32[12,24,768]{2,1,0:T(8,128)} %get-tuple-element.24) | copy-start | bytes 2654212
Sparse Core Ops, SparseCore 0:
  30.0 68.9 all-gather.2

commit v11 on v5

--- a/solution.py
+++ b/solution.py
@@ -61,12 +61,9 @@
 
 def rep_sum(parts):
     n = lax.axis_size("rep")
-    me = lax.axis_index("rep")
-    held = [parts] + [
-        lax.ppermute(parts, "rep", [(i, (i + d) % n) for i in range(n)]) for d in range(1, n)
-    ]
-    stack = jnp.stack(held)
-    by_index = [lax.dynamic_index_in_dim(stack, (me - k) % n, keepdims=False) for k in range(n)]
+    copies = jnp.broadcast_to(parts[None], (n,) + parts.shape)
+    held = lax.all_to_all(copies, "rep", 0, 0, tiled=True)
+    by_index = [held[k] for k in range(n)]
     while len(by_index) > 1:
         by_index = [a + b for a, b in zip(by_index[::2], by_index[1::2])]
     return by_index[0]

time: 117 us -> 117 us (level)
  waiting for transfers between devices: 35.3 us -> 37.9 us
    ppermute x3 -> x0, starting transfers between devices: 6.57 us -> none  [rep_sum(): lax.ppermute(parts, 'rep', [(i, (i + d) % n) for i in range(n)])]
    all_to_all x0 -> x1, starting transfers between devices: none -> 5.85 us  [rep_sum(): held = lax.all_to_all(copies, 'rep', 0, 0, tiled=True)]
    all_to_all x0 -> x1, waiting for transfers between devices: none -> 3.75 us  [rep_sum(): held = lax.all_to_all(copies, 'rep', 0, 0, tiled=True)]
    reshape x2 -> x0, local copies, waits for them, and re-layouts: 1.47 us -> none  [split_cols(): return a.reshape(a.shape[0], -1, width).transpose(1, 0, 2)]
  transfers between devices with their start and end apart: 4 -> 2, of which waited for: 1 -> 2; matrix products, arithmetic and copies ran while one was open for 8% -> 8% of each run, Pallas kernels for 0% -> 0%
where the time goes in v11:
time: 117 us
  waiting for transfers between devices  37.9 us (32%)
  blocking collectives  26.3 us (22%)
  between operations  14.3 us (12%)
  matrix products  13.3 us (11%)
  Pallas kernels  10.1 us (9%)
  local copies, waits for them, and re-layouts  8.58 us (7%)
  starting transfers between devices  5.86 us (5%)
    all_gather x1, waiting for transfers between devices, on_device(): gathered = lax.all_gather(owned_all, 'shard', axis=1, tiled=True)  34.1 us
    all_gather x1, blocking collectives, on_device(): weights_ln = lax.all_gather(norm_weights, 'shard', axis=1, tiled=True)  26.3 us
    pallas_call x1, Pallas kernels, unpack(): pl.pallas_call(functools.partial(unpack_kernel, rows), grid=(total // ste...  10.1 us
    all_to_all x1, starting transfers between devices, rep_sum(): held = lax.all_to_all(copies, 'rep', 0, 0, tiled=True)  5.85 us
    dot_general x1, matrix products, on_device(): jnp.einsum('brk,bdk->brd', mean_all, basis_all, precision=highest)  4.09 us
    all_to_all x1, waiting for transfers between devices, rep_sum(): held = lax.all_to_all(copies, 'rep', 0, 0, tiled=True)  3.75 us
  transfers between devices with their start and end apart: 2, of which 2 were waited for; matrix products, arithmetic and copies ran while one was open for 8% of the time, Pallas kernels for 0%

profile of v11, /device:TPU:1, one launch (start us, length us, event | category | flops | bytes accessed | tf_op | source)
XLA Modules:
  0.0 117.1 jit_solution(10792621047274938290)
XLA Ops:
  7.2 2.2 %fusion.20 = f32[4,24,64]{2,1,0:T(8,128)S(1)} fusion(f32[4,768,64]{1,2,0:T(8,128)} %param.33, f32[1,4,24,768]{3,2,1,0:T(8,128)} %param.26, f32[4,24,768]{2,1,0:T(8,128)} %param.22, f32[1,4,24,768]{3,2,1,0:T(8,128)} %param.18), kind=kOutput, calls=%fused_computation.42 | convolution fusion | flops 56770560 | bytes 1695744 | tf_op jit(solution)/shard_map/mrd,mdk->mrk/dot_general | solution.py:97
  9.5 0.0 copy-start.13
  9.5 0.0 copy-start
  9.5 0.6 copy-done.13
  10.1 0.1 copy.43
  10.2 0.0 copy-start.2
  10.2 0.0 copy-start.16
  10.2 2.2 %fusion.21 = f32[24,64]{1,0:T(8,128)S(1)} fusion(f32[3072,64]{0,1:T(8,128)} %param.34, f32[1,24,3072]{2,1,0:T(8,128)} %param.27, f32[24,3072]{1,0:T(8,128)} %param.23, f32[1,24,3072]{2,1,0:T(8,128)} %param.19), kind=kOutput, calls=%fused_computation.43 | convolution fusion | flops 56770560 | bytes 1677312 | tf_op jit(solution)/shard_map/dot_general | solution.py:100
  12.4 0.1 copy.44
  12.5 0.1 reshape.85
  12.6 0.1 reshape.86
  12.7 0.1 copy.45
  12.8 0.4 fusion.22
  13.2 0.0 copy-start.15
  13.2 0.1 pad_maximum_fusion
  13.3 0.7 broadcast_in_dim.30
  14.1 5.9 %all-to-all-start = ((f32[4,218,64]{1,2,0:T(8,128)}), f32[4,218,64]{1,2,0:T(8,128)S(1)}, u32[]{:S(2)}, u32[]{:S(2)}) async-start(f32[4,218,64]{1,2,0:T(8,128)} %broadcast_in_dim.30), calls=%async_computation | async-start | bytes 524288 | tf_op jit(solution)/shard_map/all_to_all | solution.py:65
  19.9 0.9 copy.61
  20.9 0.8 bitcast_bitcast_fusion
  21.7 3.7 %all-to-all-done = f32[4,218,64]{1,2,0:T(8,128)S(1)} async-done(((f32[4,218,64]{1,2,0:T(8,128)}), f32[4,218,64]{1,2,0:T(8,128)S(1)}, u32[]{:S(2)}, u32[]{:S(2)}) %all-to-all-start) | async-done | bytes 223264 | tf_op jit(solution)/shard_map/all_to_all | solution.py:65
  25.5 0.1 fusion.24
  25.6 0.1 slice_bitcast_fusion.1
  25.7 0.1 slice.65
  25.7 0.7 copy.46
  26.5 0.7 copy.48
  27.2 0.1 copy.47
  27.2 0.1 copy.52
  27.3 0.1 reshape.94
  27.4 0.7 reshape.95
  28.1 0.1 broadcast_in_dim.32
  28.1 0.0 copy-start.4
  28.2 0.0 copy-start.5
  28.2 4.1 %fusion.10 = (bf16[12,24,768]{2,1,0:T(8,128)(2,1)}, f32[12,24,768]{2,1,0:T(8,128)}) fusion(f32[4,24,768]{2,1,0:T(8,128)S(1)} %bitcast.91, f32[4,24,768]{2,1,0:T(8,128)} %get-tuple-element.30, f32[4,24,768]{2,1,0:T(8,128)} %param.22, f32[4,24,768]{2,1,0:T(8,128)} %bitcast.101, f32[4,24,768]{2,1,0:T(8,128)} %get-tuple-element.31, f32[4,24,768]{2,1,0:T(8,128)} %param.29, ...), kind=kOutput, calls=%fused_computation.15 | convolution fusion | flops 173518848 | bytes 5529600 | tf_op jit(solution)/shard_map/brk,bdk->brd/dot_general | solution.py:143
  32.3 0.0 all-gather.3.cloned.1.call-update
  32.3 0.0 copy-start.10
  32.3 0.0 copy-start.11
  32.3 0.0 copy-start.20
  32.4 2.0 %fusion.7 = f32[1,96,768]{2,1,0:T(8,128)} fusion(f32[96,64]{0,1:T(8,128)} %copy-done.15, f32[768,64]{0,1:T(8,128)S(1)} %copy-done.3, f32[1,96,768]{2,1,0:T(8,128)S(1)} %copy-done.6, f32[96,768]{1,0:T(8,128)S(1)} %copy-done.7, f32[1,96,768]{2,1,0:T(8,128)S(1)} %copy-done.8), kind=kOutput, calls=%fused_computation.9 | convolution fusion | flops 56844288 | bytes 1400832 | tf_op jit(solution)/shard_map/rk,dk->rd/dot_general | solution.py:106
  34.3 1.2 %fusion = f32[1,24,3072]{2,1,0:T(8,128)} fusion(f32[24,64]{1,0:T(8,128)S(1)} %fusion.21, f32[3072,64]{0,1:T(8,128)S(1)} %copy-done, f32[1,24,3072]{2,1,0:T(8,128)S(1)} %copy-done.4, f32[24,3072]{1,0:T(8,128)S(1)} %copy-done.2, f32[1,24,3072]{2,1,0:T(8,128)S(1)} %copy-done.5), kind=kOutput, calls=%fused_computation.1 | convolution fusion | flops 56844288 | bytes 1972224 | tf_op jit(solution)/shard_map/rk,fk->rf/dot_general | solution.py:101
  35.6 0.0 copy-start.12
  35.6 1.2 %fusion.8 = f32[1,4,24,768]{3,2,1,0:T(8,128)} fusion(f32[4,24,64]{2,1,0:T(8,128)S(1)} %copy-done.14, f32[4,768,64]{1,2,0:T(8,128)S(1)} %copy-done.1, f32[1,4,24,768]{3,2,1,0:T(8,128)S(1)} %copy-done.9, f32[4,24,768]{2,1,0:T(8,128)S(1)} %copy-done.10, f32[1,4,24,768]{3,2,1,0:T(8,128)S(1)} %copy-done.11), kind=kOutput, calls=%fused_computation.11 | convolution fusion | flops 56844288 | bytes 1990656 | tf_op jit(solution)/shard_map/mrk,mdk->mrd/dot_general | solution.py:98
  36.8 0.6 fusion.18
  37.4 26.3 %all-gather = bf16[32,24,4]{1,2,0:T(4,128)(2,1)S(1)} all-gather(bf16[1,24,4]{1,2,0:T(4,128)(2,1)S(1)} %get-tuple-element.21), channel_id=1, replica_groups=mesh['rep'=4,'shard'=32] {'shard'}, dimensions={0}, use_global_device_ids=true | all-gather | bytes 6336 | tf_op jit(solution)/shard_map/all_gather | solution.py:152
  63.7 0.7 reshape.98
  64.5 0.9 fusion.23
  65.3 0.7 copy.57
  66.1 34.1 %all-gather.3.cloned.1.call-done = bf16[12,768,768]{2,1,0:T(8,128)(2,1)} async-done(((bf16[12,24,768]{2,1,0:T(8,128)(2,1)}), bf16[12,768,768]{2,1,0:T(8,128)(2,1)}) %all-gather.3.cloned.1.call-update) | async-done | bytes 14155792 | tf_op jit(solution)/shard_map/all_gather | solution.py:150
  100.2 10.1 %shard_map.257 = (bf16[4,768,768]{2,1,0:T(8,128)(2,1)}, bf16[768,3072]{1,0:T(8,128)(2,1)}, bf16[3072,768]{1,0:T(8,128)(2,1)}) custom-call(bf16[3,4,768,768]{3,2,1,0:T(8,128)(2,1)} %bitcast.88), custom_call_target="tpu_custom_call" | custom-call | bytes 28311552 | tf_op jit(solution)/shard_map/pallas_call | solution.py:44
  (36 shorter events, 0.1 us)
Async XLA Ops:
  7.2 5.3 %copy-start.19 = (f32[1,4,24]{2,1,0:T(4,128)S(1)}, f32[1,4,24]{2,1,0:T(4,128)}, u32[]{:S(2)}) copy-start(f32[1,4,24]{2,1,0:T(4,128)} %param.21) | copy-start | bytes 1156
  7.2 5.3 %copy-start.17 = (f32[4,24]{1,0:T(4,128)S(1)}, f32[4,24]{1,0:T(4,128)}, u32[]{:S(2)}) copy-start(f32[4,24]{1,0:T(4,128)} %param.25) | copy-start | bytes 1156
  7.2 5.6 %copy-start.8 = (f32[1,96,768]{2,1,0:T(8,128)S(1)}, f32[1,96,768]{2,1,0:T(8,128)}, u32[]{:S(2)}) copy-start(f32[1,96,768]{2,1,0:T(8,128)} %param.20) | copy-start | bytes 884740
  7.2 5.6 %copy-start.7 = (f32[96,768]{1,0:T(8,128)S(1)}, f32[96,768]{1,0:T(8,128)}, u32[]{:S(2)}) copy-start(f32[96,768]{1,0:T(8,128)} %param.24) | copy-start | bytes 884740
  7.2 5.6 %copy-start.6 = (f32[1,96,768]{2,1,0:T(8,128)S(1)}, f32[1,96,768]{2,1,0:T(8,128)}, u32[]{:S(2)}) copy-start(f32[1,96,768]{2,1,0:T(8,128)} %param.28) | copy-start | bytes 884740
  7.2 5.6 %copy-start.3 = (f32[768,64]{0,1:T(8,128)S(1)}, f32[768,64]{0,1:T(8,128)}, u32[]{:S(2)}) copy-start(f32[768,64]{0,1:T(8,128)} %param.35) | copy-start | bytes 589828
  9.5 0.6 copy-start.13
  9.5 10.4 %copy-start = (f32[3072,64]{0,1:T(8,128)S(1)}, f32[3072,64]{0,1:T(8,128)}, u32[]{:S(2)}) copy-start(f32[3072,64]{0,1:T(8,128)} %param.34) | copy-start | bytes 2359300
  10.2 10.7 %copy-start.2 = (f32[24,3072]{1,0:T(8,128)S(1)}, f32[24,3072]{1,0:T(8,128)}, u32[]{:S(2)}) copy-start(f32[24,3072]{1,0:T(8,128)} %param.23) | copy-start | bytes 884740
  10.2 10.7 %copy-start.16 = (f32[24,3072]{1,0:T(8,128)S(1)}, f32[24,3072]{1,0:T(8,128)}, u32[]{:S(2)}) copy-start(f32[24,3072]{1,0:T(8,128)} %param.30) | copy-start | bytes 884740
  13.2 0.9 copy-start.15
  14.1 11.4 %all-to-all-start = ((f32[4,218,64]{1,2,0:T(8,128)}), f32[4,218,64]{1,2,0:T(8,128)S(1)}, u32[]{:S(2)}, u32[]{:S(2)}) async-start(f32[4,218,64]{1,2,0:T(8,128)} %broadcast_in_dim.30), calls=%async_computation | async-start | bytes 524288 | tf_op jit(solution)/shard_map/all_to_all | solution.py:65
  19.9 8.2 %copy-start.1 = (f32[4,768,64]{1,2,0:T(8,128)S(1)}, f32[4,768,64]{1,2,0:T(8,128)}, u32[]{:S(2)}) copy-start(f32[4,768,64]{1,2,0:T(8,128)} %param.33) | copy-start | bytes 2359300
  19.9 80.3 %all-gather.3.cloned.1.call-start = ((), (), s32[]{:S(2)}) async-start(), calls=%async_computation.1 | async-start | bytes 14598144 | tf_op jit(solution)/shard_map/all_gather | solution.py:150
  28.1 6.2 %copy-start.4 = (f32[1,24,3072]{2,1,0:T(8,128)S(1)}, f32[1,24,3072]{2,1,0:T(8,128)}, u32[]{:S(2)}) copy-start(f32[1,24,3072]{2,1,0:T(8,128)} %param.27) | copy-start | bytes 884740
  28.2 6.2 %copy-start.5 = (f32[1,24,3072]{2,1,0:T(8,128)S(1)}, f32[1,24,3072]{2,1,0:T(8,128)}, u32[]{:S(2)}) copy-start(f32[1,24,3072]{2,1,0:T(8,128)} %param.19) | copy-start | bytes 884740
  32.3 3.3 %copy-start.9 = (f32[1,4,24,768]{3,2,1,0:T(8,128)S(1)}, f32[1,4,24,768]{3,2,1,0:T(8,128)}, u32[]{:S(2)}) copy-start(f32[1,4,24,768]{3,2,1,0:T(8,128)} %param.26) | copy-start | bytes 884740
  32.3 3.3 %copy-start.10 = (f32[4,24,768]{2,1,0:T(8,128)S(1)}, f32[4,24,768]{2,1,0:T(8,128)}, u32[]{:S(2)}) copy-start(f32[4,24,768]{2,1,0:T(8,128)} %param.22) | copy-start | bytes 884740
  32.3 3.3 %copy-start.11 = (f32[1,4,24,768]{3,2,1,0:T(8,128)S(1)}, f32[1,4,24,768]{3,2,1,0:T(8,128)}, u32[]{:S(2)}) copy-start(f32[1,4,24,768]{3,2,1,0:T(8,128)} %param.18) | copy-start | bytes 884740
  32.3 3.3 %copy-start.14 = (f32[4,24,64]{2,1,0:T(8,128)S(1)}, f32[4,24,64]{2,1,0:T(8,128)}, u32[]{:S(2)}) copy-start(f32[4,24,64]{2,1,0:T(8,128)} %copy-done.13) | copy-start | bytes 73732
  32.3 4.5 %copy-start.18 = (f32[4,24]{1,0:T(4,128)S(1)}, f32[4,24]{1,0:T(4,128)}, u32[]{:S(2)}) copy-start(f32[4,24]{1,0:T(4,128)} %reshape.95) | copy-start | bytes 1156
  32.3 4.5 %copy-start.20 = (f32[4,24]{1,0:T(4,128)S(1)}, f32[4,24]{1,0:T(4,128)}, u32[]{:S(2)}) copy-start(f32[4,24]{1,0:T(4,128)} %param.32) | copy-start | bytes 1156
  35.6 28.9 %copy-start.12 = (f32[12,24,768]{2,1,0:T(8,128)S(1)}, f32[12,24,768]{2,1,0:T(8,128)}, u32[]{:S(2)}) copy-start(f32[12,24,768]{2,1,0:T(8,128)} %get-tuple-element.24) | copy-start | bytes 2654212
Sparse Core Ops, SparseCore 0:
  32.4 67.7 all-gather.2

commit v12 on v5

--- a/solution.py
+++ b/solution.py
@@ -38,7 +38,7 @@
     kinds_blocks, total, width = gathered.shape
     blocks = kinds_blocks // 3
     g = gathered.reshape(3, blocks, total, width)
-    step = 8 * rows
+    step = 16 * rows
     dt = gathered.dtype
     nbytes = 2 * gathered.size * dt.itemsize
     return pl.pallas_call(

time: 117 us -> 116 us (level)
  no operation moved by 1% of the time
where the time goes in v12:
time: 116 us
  waiting for transfers between devices  35.3 us (30%)
  blocking collectives  26.5 us (23%)
  between operations  14.4 us (12%)
  matrix products  13.4 us (12%)
  Pallas kernels  9.81 us (8%)
  local copies, waits for them, and re-layouts  8.49 us (7%)
  starting transfers between devices  6.6 us (6%)
  other arithmetic  1.69 us (1%)
    all_gather x1, waiting for transfers between devices, on_device(): gathered = lax.all_gather(owned_all, 'shard', axis=1, tiled=True)  35.2 us
    all_gather x1, blocking collectives, on_device(): weights_ln = lax.all_gather(norm_weights, 'shard', axis=1, tiled=True)  26.5 us
    pallas_call x1, Pallas kernels, unpack(): pl.pallas_call(functools.partial(unpack_kernel, rows), grid=(total // ste...  9.81 us
    ppermute x3, starting transfers between devices, rep_sum(): lax.ppermute(parts, 'rep', [(i, (i + d) % n) for i in range(n)])  6.57 us
    dot_general x1, matrix products, on_device(): jnp.einsum('brk,bdk->brd', mean_all, basis_all, precision=highest)  4.09 us
  transfers between devices with their start and end apart: 4, of which 1 were waited for; matrix products, arithmetic and copies ran while one was open for 8% of the time, Pallas kernels for 0%

profile of v12, /device:TPU:1, one launch (start us, length us, event | category | flops | bytes accessed | tf_op | source)
XLA Modules:
  0.0 116.1 jit_solution(2851063228327772217)
XLA Ops:
  7.2 0.0 copy-start
  7.3 0.0 all-gather.3.cloned.1.call-start
  7.3 2.3 %fusion.18 = f32[4,24,64]{2,1,0:T(8,128)S(1)} fusion(f32[4,768,64]{1,2,0:T(8,128)} %param.33, f32[1,4,24,768]{3,2,1,0:T(8,128)} %param.26, f32[4,24,768]{2,1,0:T(8,128)} %param.22, f32[1,4,24,768]{3,2,1,0:T(8,128)} %param.18), kind=kOutput, calls=%fused_computation.40 | convolution fusion | flops 56770560 | bytes 1695744 | tf_op jit(solution)/shard_map/mrd,mdk->mrk/dot_general | solution.py:100
  9.6 0.0 copy-start.14
  9.6 0.6 copy-done.14
  10.2 0.1 copy.49
  10.3 0.0 copy-start.2
  10.3 2.2 %fusion.19 = f32[24,64]{1,0:T(8,128)S(1)} fusion(f32[3072,64]{0,1:T(8,128)} %param.34, f32[1,24,3072]{2,1,0:T(8,128)} %param.27, f32[24,3072]{1,0:T(8,128)} %param.23, f32[1,24,3072]{2,1,0:T(8,128)} %param.19), kind=kOutput, calls=%fused_computation.41 | convolution fusion | flops 56770560 | bytes 1677312 | tf_op jit(solution)/shard_map/dot_general | solution.py:103
  12.5 0.0 copy-start.16
  12.5 0.1 copy.50
  12.6 0.1 reshape.84
  12.7 0.1 reshape.85
  12.8 0.1 copy.51
  12.9 0.4 fusion.20
  13.3 0.1 pad_maximum_fusion.1
  13.4 2.5 %collective-permute-start = (f32[218,64]{0,1:T(8,128)S(1)}, f32[218,64]{0,1:T(8,128)S(1)}, u32[]{:S(2)}, u32[]{:S(2)}) collective-permute-start(f32[218,64]{0,1:T(8,128)S(1)} %pad_maximum_fusion.1), channel_id=1, source_target_pairs={{0,32},{32,64},{64,96},{96,0},{1,33},{33,65},{65,97},{97,1},{2,34}... | collective-permute-start | bytes 167432 | tf_op jit(solution)/shard_map/ppermute | solution.py:66
  16.0 3.3 %collective-permute-start.1 = (f32[218,64]{0,1:T(8,128)S(1)}, f32[218,64]{0,1:T(8,128)S(1)}, u32[]{:S(2)}, u32[]{:S(2)}) collective-permute-start(f32[218,64]{0,1:T(8,128)S(1)} %pad_maximum_fusion.1), channel_id=1, source_target_pairs={{0,64},{32,96},{64,0},{96,32},{1,65},{33,97},{65,1},{97,33},{2,66}... | collective-permute-start | bytes 167432 | tf_op jit(solution)/shard_map/ppermute | solution.py:66
  19.3 0.7 collective-permute-start.2
  20.0 0.1 fusion.32
  20.2 0.0 copy-start.1
  20.2 0.9 copy.67
  21.2 0.7 copy.68
  21.9 0.7 copy.69
  22.6 0.1 collective-permute-done.2
  22.7 0.9 pad_maximum_fusion
  23.6 0.1 fusion.22
  23.6 0.1 slice_bitcast_fusion.1
  23.7 0.1 slice.45
  23.8 0.7 copy.52
  24.5 0.7 copy.54
  25.2 0.1 copy.53
  25.3 0.1 copy.58
  25.4 0.1 reshape.93
  25.4 0.7 reshape.94
  26.1 0.1 broadcast_in_dim.25
  26.2 0.0 copy-start.5
  26.2 4.1 %fusion.10 = (bf16[12,24,768]{2,1,0:T(8,128)(2,1)}, f32[12,24,768]{2,1,0:T(8,128)}) fusion(f32[4,24,768]{2,1,0:T(8,128)S(1)} %bitcast.100, f32[4,24,768]{2,1,0:T(8,128)} %bitcast.105, f32[4,24,768]{2,1,0:T(8,128)} %param.22, f32[4,24,768]{2,1,0:T(8,128)} %bitcast.114, f32[4,24,768]{2,1,0:T(8,128)} %bitcast.106, f32[4,24,768]{2,1,0:T(8,128)} %param.29, ...), kind=kOutput, calls=%fused_computation.15 | convolution fusion | flops 173518848 | bytes 5529600 | tf_op jit(solution)/shard_map/brk,bdk->brd/dot_general | solution.py:146
  30.3 0.0 all-gather.3.cloned.1.call-update
  30.4 2.0 %fusion.7 = f32[1,96,768]{2,1,0:T(8,128)} fusion(f32[96,64]{0,1:T(8,128)} %copy-done.13, f32[768,64]{0,1:T(8,128)S(1)} %copy-done.3, f32[1,96,768]{2,1,0:T(8,128)S(1)} %copy-done.6, f32[96,768]{1,0:T(8,128)S(1)} %copy-done.7, f32[1,96,768]{2,1,0:T(8,128)S(1)} %copy-done.8), kind=kOutput, calls=%fused_computation.9 | convolution fusion | flops 56844288 | bytes 1400832 | tf_op jit(solution)/shard_map/rk,dk->rd/dot_general | solution.py:109
  32.4 1.2 %fusion = f32[1,24,3072]{2,1,0:T(8,128)} fusion(f32[24,64]{1,0:T(8,128)S(1)} %fusion.19, f32[3072,64]{0,1:T(8,128)S(1)} %copy-done, f32[1,24,3072]{2,1,0:T(8,128)S(1)} %copy-done.4, f32[24,3072]{1,0:T(8,128)S(1)} %copy-done.2, f32[1,24,3072]{2,1,0:T(8,128)S(1)} %copy-done.5), kind=kOutput, calls=%fused_computation.1 | convolution fusion | flops 56844288 | bytes 1972224 | tf_op jit(solution)/shard_map/rk,fk->rf/dot_general | solution.py:104
  33.6 1.2 %fusion.8 = f32[1,4,24,768]{3,2,1,0:T(8,128)} fusion(f32[4,24,64]{2,1,0:T(8,128)S(1)} %copy-done.15, f32[4,768,64]{1,2,0:T(8,128)S(1)} %copy-done.1, f32[1,4,24,768]{3,2,1,0:T(8,128)S(1)} %copy-done.9, f32[4,24,768]{2,1,0:T(8,128)S(1)} %copy-done.10, f32[1,4,24,768]{3,2,1,0:T(8,128)S(1)} %copy-done.11), kind=kOutput, calls=%fused_computation.11 | convolution fusion | flops 56844288 | bytes 1990656 | tf_op jit(solution)/shard_map/mrk,mdk->mrd/dot_general | solution.py:101
  34.9 0.6 fusion.16
  35.5 26.5 %all-gather = bf16[32,24,4]{1,2,0:T(4,128)(2,1)S(1)} all-gather(bf16[1,24,4]{1,2,0:T(4,128)(2,1)S(1)} %get-tuple-element.21), channel_id=1, replica_groups=mesh['rep'=4,'shard'=32] {'shard'}, dimensions={0}, use_global_device_ids=true | all-gather | bytes 6336 | tf_op jit(solution)/shard_map/all_gather | solution.py:155
  61.9 0.7 reshape.97
  62.6 0.9 fusion.21
  63.5 0.7 copy.63
  64.2 35.2 %all-gather.3.cloned.1.call-done = bf16[12,768,768]{2,1,0:T(8,128)(2,1)} async-done(((bf16[12,24,768]{2,1,0:T(8,128)(2,1)}), bf16[12,768,768]{2,1,0:T(8,128)(2,1)}) %all-gather.3.cloned.1.call-update) | async-done | bytes 14155792 | tf_op jit(solution)/shard_map/all_gather | solution.py:153
  99.4 9.8 %shard_map.257 = (bf16[4,768,768]{2,1,0:T(8,128)(2,1)}, bf16[768,3072]{1,0:T(8,128)(2,1)}, bf16[3072,768]{1,0:T(8,128)(2,1)}) custom-call(bf16[3,4,768,768]{3,2,1,0:T(8,128)(2,1)} %bitcast.97), custom_call_target="tpu_custom_call" | custom-call | bytes 28311552 | tf_op jit(solution)/shard_map/pallas_call | solution.py:44
  (42 shorter events, 0.1 us)
Async XLA Ops:
  7.2 13.0 %copy-start = (f32[3072,64]{0,1:T(8,128)S(1)}, f32[3072,64]{0,1:T(8,128)}, u32[]{:S(2)}) copy-start(f32[3072,64]{0,1:T(8,128)} %param.34) | copy-start | bytes 2359300
  7.2 5.4 %copy-start.19 = (f32[1,4,24]{2,1,0:T(4,128)S(1)}, f32[1,4,24]{2,1,0:T(4,128)}, u32[]{:S(2)}) copy-start(f32[1,4,24]{2,1,0:T(4,128)} %param.21) | copy-start | bytes 1156
  7.2 5.4 %copy-start.17 = (f32[4,24]{1,0:T(4,128)S(1)}, f32[4,24]{1,0:T(4,128)}, u32[]{:S(2)}) copy-start(f32[4,24]{1,0:T(4,128)} %param.25) | copy-start | bytes 1156
  7.2 5.7 %copy-start.8 = (f32[1,96,768]{2,1,0:T(8,128)S(1)}, f32[1,96,768]{2,1,0:T(8,128)}, u32[]{:S(2)}) copy-start(f32[1,96,768]{2,1,0:T(8,128)} %param.20) | copy-start | bytes 884740
  7.2 5.7 %copy-start.7 = (f32[96,768]{1,0:T(8,128)S(1)}, f32[96,768]{1,0:T(8,128)}, u32[]{:S(2)}) copy-start(f32[96,768]{1,0:T(8,128)} %param.24) | copy-start | bytes 884740
  7.2 5.7 %copy-start.6 = (f32[1,96,768]{2,1,0:T(8,128)S(1)}, f32[1,96,768]{2,1,0:T(8,128)}, u32[]{:S(2)}) copy-start(f32[1,96,768]{2,1,0:T(8,128)} %param.28) | copy-start | bytes 884740
  7.2 5.7 %copy-start.3 = (f32[768,64]{0,1:T(8,128)S(1)}, f32[768,64]{0,1:T(8,128)}, u32[]{:S(2)}) copy-start(f32[768,64]{0,1:T(8,128)} %param.35) | copy-start | bytes 589828
  7.3 92.2 %all-gather.3.cloned.1.call-start = ((), (), s32[]{:S(2)}) async-start(), calls=%async_computation | async-start | bytes 14598144 | tf_op jit(solution)/shard_map/all_gather | solution.py:153
  9.6 0.6 copy-start.14
  10.3 10.9 %copy-start.2 = (f32[24,3072]{1,0:T(8,128)S(1)}, f32[24,3072]{1,0:T(8,128)}, u32[]{:S(2)}) copy-start(f32[24,3072]{1,0:T(8,128)} %param.23) | copy-start | bytes 884740
  12.5 9.4 %copy-start.16 = (f32[24,3072]{1,0:T(8,128)S(1)}, f32[24,3072]{1,0:T(8,128)}, u32[]{:S(2)}) copy-start(f32[24,3072]{1,0:T(8,128)} %param.30) | copy-start | bytes 884740
  13.3 6.7 %copy-start.13 = (f32[96,64]{0,1:T(8,128)}, f32[96,64]{0,1:T(8,128)S(1)}, u32[]{:S(2)}) copy-start(f32[96,64]{0,1:T(8,128)S(1)} %fusion.20) | copy-start | bytes 73732
  13.4 9.2 %collective-permute-start = (f32[218,64]{0,1:T(8,128)S(1)}, f32[218,64]{0,1:T(8,128)S(1)}, u32[]{:S(2)}, u32[]{:S(2)}) collective-permute-start(f32[218,64]{0,1:T(8,128)S(1)} %pad_maximum_fusion.1), channel_id=1, source_target_pairs={{0,32},{32,64},{64,96},{96,0},{1,33},{33,65},{65,97},{97,1},{2,34}... | collective-permute-start | bytes 167432 | tf_op jit(solution)/shard_map/ppermute | solution.py:66
  16.0 6.7 %collective-permute-start.1 = (f32[218,64]{0,1:T(8,128)S(1)}, f32[218,64]{0,1:T(8,128)S(1)}, u32[]{:S(2)}, u32[]{:S(2)}) collective-permute-start(f32[218,64]{0,1:T(8,128)S(1)} %pad_maximum_fusion.1), channel_id=1, source_target_pairs={{0,64},{32,96},{64,0},{96,32},{1,65},{33,97},{65,1},{97,33},{2,66}... | collective-permute-start | bytes 167432 | tf_op jit(solution)/shard_map/ppermute | solution.py:66
  19.3 3.4 %collective-permute-start.2 = (f32[218,64]{0,1:T(8,128)S(1)}, f32[218,64]{0,1:T(8,128)}, u32[]{:S(2)}, u32[]{:S(2)}) collective-permute-start(f32[218,64]{0,1:T(8,128)S(1)} %pad_maximum_fusion.1), channel_id=1, source_target_pairs={{0,96},{32,0},{64,32},{96,64},{1,97},{33,1},{65,33},{97,65},{2,98}... | collective-permute-start | bytes 167432 | tf_op jit(solution)/shard_map/ppermute | solution.py:66
  20.2 6.0 %copy-start.1 = (f32[4,768,64]{1,2,0:T(8,128)S(1)}, f32[4,768,64]{1,2,0:T(8,128)}, u32[]{:S(2)}) copy-start(f32[4,768,64]{1,2,0:T(8,128)} %param.33) | copy-start | bytes 2359300
  26.2 6.2 %copy-start.4 = (f32[1,24,3072]{2,1,0:T(8,128)S(1)}, f32[1,24,3072]{2,1,0:T(8,128)}, u32[]{:S(2)}) copy-start(f32[1,24,3072]{2,1,0:T(8,128)} %param.27) | copy-start | bytes 884740
  26.2 6.2 %copy-start.5 = (f32[1,24,3072]{2,1,0:T(8,128)S(1)}, f32[1,24,3072]{2,1,0:T(8,128)}, u32[]{:S(2)}) copy-start(f32[1,24,3072]{2,1,0:T(8,128)} %param.19) | copy-start | bytes 884740
  30.3 3.3 %copy-start.9 = (f32[1,4,24,768]{3,2,1,0:T(8,128)S(1)}, f32[1,4,24,768]{3,2,1,0:T(8,128)}, u32[]{:S(2)}) copy-start(f32[1,4,24,768]{3,2,1,0:T(8,128)} %param.26) | copy-start | bytes 884740
  30.4 3.3 %copy-start.10 = (f32[4,24,768]{2,1,0:T(8,128)S(1)}, f32[4,24,768]{2,1,0:T(8,128)}, u32[]{:S(2)}) copy-start(f32[4,24,768]{2,1,0:T(8,128)} %param.22) | copy-start | bytes 884740
  30.4 3.3 %copy-start.11 = (f32[1,4,24,768]{3,2,1,0:T(8,128)S(1)}, f32[1,4,24,768]{3,2,1,0:T(8,128)}, u32[]{:S(2)}) copy-start(f32[1,4,24,768]{3,2,1,0:T(8,128)} %param.18) | copy-start | bytes 884740
  30.4 3.3 %copy-start.15 = (f32[4,24,64]{2,1,0:T(8,128)S(1)}, f32[4,24,64]{2,1,0:T(8,128)}, u32[]{:S(2)}) copy-start(f32[4,24,64]{2,1,0:T(8,128)} %copy-done.14) | copy-start | bytes 73732
  30.4 4.5 %copy-start.18 = (f32[4,24]{1,0:T(4,128)S(1)}, f32[4,24]{1,0:T(4,128)}, u32[]{:S(2)}) copy-start(f32[4,24]{1,0:T(4,128)} %reshape.94) | copy-start | bytes 1156
  30.4 4.5 %copy-start.20 = (f32[4,24]{1,0:T(4,128)S(1)}, f32[4,24]{1,0:T(4,128)}, u32[]{:S(2)}) copy-start(f32[4,24]{1,0:T(4,128)} %param.32) | copy-start | bytes 1156
  32.4 30.2 %copy-start.12 = (f32[12,24,768]{2,1,0:T(8,128)S(1)}, f32[12,24,768]{2,1,0:T(8,128)}, u32[]{:S(2)}) copy-start(f32[12,24,768]{2,1,0:T(8,128)} %get-tuple-element.24) | copy-start | bytes 2654212
Sparse Core Ops, SparseCore 0:
  30.5 68.9 all-gather.2

commit v13 on v5

--- a/solution.py
+++ b/solution.py
@@ -65,8 +65,7 @@
     held = [parts] + [
         lax.ppermute(parts, "rep", [(i, (i + d) % n) for i in range(n)]) for d in range(1, n)
     ]
-    stack = jnp.stack(held)
-    by_index = [lax.dynamic_index_in_dim(stack, (me - k) % n, keepdims=False) for k in range(n)]
+    by_index = [lax.select_n((me - k) % n, *held) for k in range(n)]
     while len(by_index) > 1:
         by_index = [a + b for a, b in zip(by_index[::2], by_index[1::2])]
     return by_index[0]

time: 117 us -> 118 us (level)
  transfers between devices with their start and end apart: 4 -> 4, of which waited for: 1 -> 2; matrix products, arithmetic and copies ran while one was open for 8% -> 8% of each run, Pallas kernels for 0% -> 0%
where the time goes in v13:
time: 118 us; the launch traced here: 117 us
  waiting for transfers between devices  35.7 us (30%)
  blocking collectives  26.5 us (22%)
  between operations  14.3 us (12%)
  matrix products  13.4 us (11%)
  Pallas kernels  10.1 us (9%)
  local copies, waits for them, and re-layouts  8.49 us (7%)
  starting transfers between devices  6.53 us (6%)
  other arithmetic  2.3 us (2%)
    all_gather x1, waiting for transfers between devices, on_device(): gathered = lax.all_gather(owned_all, 'shard', axis=1, tiled=True)  35.2 us
    all_gather x1, blocking collectives, on_device(): weights_ln = lax.all_gather(norm_weights, 'shard', axis=1, tiled=True)  26.5 us
    pallas_call x1, Pallas kernels, unpack(): pl.pallas_call(functools.partial(unpack_kernel, rows), grid=(total // ste...  10.1 us
    ppermute x3, starting transfers between devices, rep_sum(): lax.ppermute(parts, 'rep', [(i, (i + d) % n) for i in range(n)])  6.5 us
    dot_general x1, matrix products, on_device(): jnp.einsum('brk,bdk->brd', mean_all, basis_all, precision=highest)  4.09 us
  transfers between devices with their start and end apart: 4, of which 2 were waited for; matrix products, arithmetic and copies ran while one was open for 8% of the time, Pallas kernels for 0%

profile of v13, /device:TPU:1, one launch (start us, length us, event | category | flops | bytes accessed | tf_op | source)
XLA Modules:
  0.0 117.2 jit_solution(7405188972794914498)
XLA Ops:
  7.2 0.0 copy-start
  7.3 0.0 all-gather.3.cloned.1.call-start
  7.3 2.3 %fusion.18 = f32[4,24,64]{2,1,0:T(8,128)S(1)} fusion(f32[4,768,64]{1,2,0:T(8,128)} %param.33, f32[1,4,24,768]{3,2,1,0:T(8,128)} %param.26, f32[4,24,768]{2,1,0:T(8,128)} %param.22, f32[1,4,24,768]{3,2,1,0:T(8,128)} %param.18), kind=kOutput, calls=%fused_computation.38 | convolution fusion | flops 56770560 | bytes 1695744 | tf_op jit(solution)/shard_map/mrd,mdk->mrk/dot_general | solution.py:99
  9.6 0.0 copy-start.14
  9.6 0.6 copy-done.14
  10.2 0.1 copy.49
  10.3 0.0 copy-start.2
  10.3 0.0 copy-start.16
  10.3 2.2 %fusion.19 = f32[24,64]{1,0:T(8,128)S(1)} fusion(f32[3072,64]{0,1:T(8,128)} %param.34, f32[1,24,3072]{2,1,0:T(8,128)} %param.27, f32[24,3072]{1,0:T(8,128)} %param.23, f32[1,24,3072]{2,1,0:T(8,128)} %param.19), kind=kOutput, calls=%fused_computation.39 | convolution fusion | flops 56770560 | bytes 1677312 | tf_op jit(solution)/shard_map/dot_general | solution.py:102
  12.5 0.1 copy.50
  12.6 0.1 reshape.72
  12.7 0.1 reshape.73
  12.8 0.1 copy.51
  12.9 0.4 fusion.20
  13.3 0.7 pad_maximum_fusion
  14.1 2.5 %collective-permute-start = (f32[218,64]{0,1:T(8,128)}, f32[218,64]{0,1:T(8,128)S(1)}, u32[]{:S(2)}, u32[]{:S(2)}) collective-permute-start(f32[218,64]{0,1:T(8,128)} %pad_maximum_fusion), channel_id=1, source_target_pairs={{0,32},{32,64},{64,96},{96,0},{1,33},{33,65},{65,97},{97,1},{2,34}... | collective-permute-start | bytes 167432 | tf_op jit(solution)/shard_map/ppermute | solution.py:66
  16.5 3.3 %collective-permute-start.1 = (f32[218,64]{0,1:T(8,128)}, f32[218,64]{0,1:T(8,128)S(1)}, u32[]{:S(2)}, u32[]{:S(2)}) collective-permute-start(f32[218,64]{0,1:T(8,128)} %pad_maximum_fusion), channel_id=1, source_target_pairs={{0,64},{32,96},{64,0},{96,32},{1,65},{33,97},{65,1},{97,33},{2,66}... | collective-permute-start | bytes 167432 | tf_op jit(solution)/shard_map/ppermute | solution.py:66
  19.8 0.7 collective-permute-start.2
  20.6 0.9 copy.67
  21.5 0.7 copy.68
  22.3 0.7 copy.69
  23.0 0.5 collective-permute-done.2
  23.5 1.0 add_multiply_fusion
  24.4 0.1 fusion.22
  24.5 0.1 slice.33
  24.6 0.1 slice.38
  24.7 0.7 copy.52
  25.4 0.7 copy.54
  26.1 0.1 copy.53
  26.2 0.1 copy.58
  26.2 0.1 reshape.81
  26.3 0.7 reshape.82
  27.0 0.1 broadcast_in_dim.25
  27.1 4.1 %fusion.10 = (bf16[12,24,768]{2,1,0:T(8,128)(2,1)}, f32[12,24,768]{2,1,0:T(8,128)}) fusion(f32[4,24,768]{2,1,0:T(8,128)S(1)} %bitcast.93, f32[4,24,768]{2,1,0:T(8,128)} %bitcast.98, f32[4,24,768]{2,1,0:T(8,128)} %param.22, f32[4,24,768]{2,1,0:T(8,128)} %bitcast.105, f32[4,24,768]{2,1,0:T(8,128)} %bitcast.99, f32[4,24,768]{2,1,0:T(8,128)} %param.29, ...), kind=kOutput, calls=%fused_computation.15 | convolution fusion | flops 173518848 | bytes 5529600 | tf_op jit(solution)/shard_map/brk,bdk->brd/dot_general | solution.py:145
  31.2 0.0 all-gather.3.cloned.1.call-update
  31.2 0.0 copy-start.10
  31.2 0.0 copy-start.11
  31.3 0.0 copy-start.20
  31.3 2.0 %fusion.7 = f32[1,96,768]{2,1,0:T(8,128)} fusion(f32[96,64]{0,1:T(8,128)} %copy-done.13, f32[768,64]{0,1:T(8,128)S(1)} %copy-done.3, f32[1,96,768]{2,1,0:T(8,128)S(1)} %copy-done.6, f32[96,768]{1,0:T(8,128)S(1)} %copy-done.7, f32[1,96,768]{2,1,0:T(8,128)S(1)} %copy-done.8), kind=kOutput, calls=%fused_computation.9 | convolution fusion | flops 56844288 | bytes 1400832 | tf_op jit(solution)/shard_map/rk,dk->rd/dot_general | solution.py:108
  33.3 1.2 %fusion = f32[1,24,3072]{2,1,0:T(8,128)} fusion(f32[24,64]{1,0:T(8,128)S(1)} %fusion.19, f32[3072,64]{0,1:T(8,128)S(1)} %copy-done, f32[1,24,3072]{2,1,0:T(8,128)S(1)} %copy-done.4, f32[24,3072]{1,0:T(8,128)S(1)} %copy-done.2, f32[1,24,3072]{2,1,0:T(8,128)S(1)} %copy-done.5), kind=kOutput, calls=%fused_computation.1 | convolution fusion | flops 56844288 | bytes 1972224 | tf_op jit(solution)/shard_map/rk,fk->rf/dot_general | solution.py:103
  34.5 1.2 %fusion.8 = f32[1,4,24,768]{3,2,1,0:T(8,128)} fusion(f32[4,24,64]{2,1,0:T(8,128)S(1)} %copy-done.15, f32[4,768,64]{1,2,0:T(8,128)S(1)} %copy-done.1, f32[1,4,24,768]{3,2,1,0:T(8,128)S(1)} %copy-done.9, f32[4,24,768]{2,1,0:T(8,128)S(1)} %copy-done.10, f32[1,4,24,768]{3,2,1,0:T(8,128)S(1)} %copy-done.11), kind=kOutput, calls=%fused_computation.11 | convolution fusion | flops 56844288 | bytes 1990656 | tf_op jit(solution)/shard_map/mrk,mdk->mrd/dot_general | solution.py:100
  35.8 0.6 fusion.16
  36.3 26.5 %all-gather = bf16[32,24,4]{1,2,0:T(4,128)(2,1)S(1)} all-gather(bf16[1,24,4]{1,2,0:T(4,128)(2,1)S(1)} %get-tuple-element.21), channel_id=1, replica_groups=mesh['rep'=4,'shard'=32] {'shard'}, dimensions={0}, use_global_device_ids=true | all-gather | bytes 6336 | tf_op jit(solution)/shard_map/all_gather | solution.py:154
  62.8 0.7 reshape.85
  63.5 0.9 fusion.21
  64.4 0.7 copy.63
  65.1 35.2 %all-gather.3.cloned.1.call-done = bf16[12,768,768]{2,1,0:T(8,128)(2,1)} async-done(((bf16[12,24,768]{2,1,0:T(8,128)(2,1)}), bf16[12,768,768]{2,1,0:T(8,128)(2,1)}) %all-gather.3.cloned.1.call-update) | async-done | bytes 14155792 | tf_op jit(solution)/shard_map/all_gather | solution.py:152
  100.3 10.1 %shard_map.257 = (bf16[4,768,768]{2,1,0:T(8,128)(2,1)}, bf16[768,3072]{1,0:T(8,128)(2,1)}, bf16[3072,768]{1,0:T(8,128)(2,1)}) custom-call(bf16[3,4,768,768]{3,2,1,0:T(8,128)(2,1)} %bitcast.90), custom_call_target="tpu_custom_call" | custom-call | bytes 28311552 | tf_op jit(solution)/shard_map/pallas_call | solution.py:44
  (40 shorter events, 0.1 us)
Async XLA Ops:
  7.2 13.4 %copy-start = (f32[3072,64]{0,1:T(8,128)S(1)}, f32[3072,64]{0,1:T(8,128)}, u32[]{:S(2)}) copy-start(f32[3072,64]{0,1:T(8,128)} %param.34) | copy-start | bytes 2359300
  7.2 5.4 %copy-start.19 = (f32[1,4,24]{2,1,0:T(4,128)S(1)}, f32[1,4,24]{2,1,0:T(4,128)}, u32[]{:S(2)}) copy-start(f32[1,4,24]{2,1,0:T(4,128)} %param.21) | copy-start | bytes 1156
  7.2 5.4 %copy-start.17 = (f32[4,24]{1,0:T(4,128)S(1)}, f32[4,24]{1,0:T(4,128)}, u32[]{:S(2)}) copy-start(f32[4,24]{1,0:T(4,128)} %param.25) | copy-start | bytes 1156
  7.2 5.7 %copy-start.8 = (f32[1,96,768]{2,1,0:T(8,128)S(1)}, f32[1,96,768]{2,1,0:T(8,128)}, u32[]{:S(2)}) copy-start(f32[1,96,768]{2,1,0:T(8,128)} %param.20) | copy-start | bytes 884740
  7.2 5.7 %copy-start.7 = (f32[96,768]{1,0:T(8,128)S(1)}, f32[96,768]{1,0:T(8,128)}, u32[]{:S(2)}) copy-start(f32[96,768]{1,0:T(8,128)} %param.24) | copy-start | bytes 884740
  7.2 5.7 %copy-start.6 = (f32[1,96,768]{2,1,0:T(8,128)S(1)}, f32[1,96,768]{2,1,0:T(8,128)}, u32[]{:S(2)}) copy-start(f32[1,96,768]{2,1,0:T(8,128)} %param.28) | copy-start | bytes 884740
  7.2 5.7 %copy-start.3 = (f32[768,64]{0,1:T(8,128)S(1)}, f32[768,64]{0,1:T(8,128)}, u32[]{:S(2)}) copy-start(f32[768,64]{0,1:T(8,128)} %param.35) | copy-start | bytes 589828
  7.3 93.1 %all-gather.3.cloned.1.call-start = ((), (), s32[]{:S(2)}) async-start(), calls=%async_computation | async-start | bytes 14598144 | tf_op jit(solution)/shard_map/all_gather | solution.py:152
  9.6 0.6 copy-start.14
  10.3 11.2 %copy-start.2 = (f32[24,3072]{1,0:T(8,128)S(1)}, f32[24,3072]{1,0:T(8,128)}, u32[]{:S(2)}) copy-start(f32[24,3072]{1,0:T(8,128)} %param.23) | copy-start | bytes 884740
  10.3 12.0 %copy-start.16 = (f32[24,3072]{1,0:T(8,128)S(1)}, f32[24,3072]{1,0:T(8,128)}, u32[]{:S(2)}) copy-start(f32[24,3072]{1,0:T(8,128)} %param.30) | copy-start | bytes 884740
  13.3 13.8 %copy-start.13 = (f32[96,64]{0,1:T(8,128)}, f32[96,64]{0,1:T(8,128)S(1)}, u32[]{:S(2)}) copy-start(f32[96,64]{0,1:T(8,128)S(1)} %fusion.20) | copy-start | bytes 73732
  14.1 8.9 %collective-permute-start = (f32[218,64]{0,1:T(8,128)}, f32[218,64]{0,1:T(8,128)S(1)}, u32[]{:S(2)}, u32[]{:S(2)}) collective-permute-start(f32[218,64]{0,1:T(8,128)} %pad_maximum_fusion), channel_id=1, source_target_pairs={{0,32},{32,64},{64,96},{96,0},{1,33},{33,65},{65,97},{97,1},{2,34}... | collective-permute-start | bytes 167432 | tf_op jit(solution)/shard_map/ppermute | solution.py:66
  16.5 6.5 %collective-permute-start.1 = (f32[218,64]{0,1:T(8,128)}, f32[218,64]{0,1:T(8,128)S(1)}, u32[]{:S(2)}, u32[]{:S(2)}) collective-permute-start(f32[218,64]{0,1:T(8,128)} %pad_maximum_fusion), channel_id=1, source_target_pairs={{0,64},{32,96},{64,0},{96,32},{1,65},{33,97},{65,1},{97,33},{2,66}... | collective-permute-start | bytes 167432 | tf_op jit(solution)/shard_map/ppermute | solution.py:66
  19.8 3.6 %collective-permute-start.2 = (f32[218,64]{0,1:T(8,128)}, f32[218,64]{0,1:T(8,128)}, u32[]{:S(2)}, u32[]{:S(2)}) collective-permute-start(f32[218,64]{0,1:T(8,128)} %pad_maximum_fusion), channel_id=1, source_target_pairs={{0,96},{32,0},{64,32},{96,64},{1,97},{33,1},{65,33},{97,65},{2,98}... | collective-permute-start | bytes 167432 | tf_op jit(solution)/shard_map/ppermute | solution.py:66
  20.6 6.5 %copy-start.1 = (f32[4,768,64]{1,2,0:T(8,128)S(1)}, f32[4,768,64]{1,2,0:T(8,128)}, u32[]{:S(2)}) copy-start(f32[4,768,64]{1,2,0:T(8,128)} %param.33) | copy-start | bytes 2359300
  27.1 6.2 %copy-start.4 = (f32[1,24,3072]{2,1,0:T(8,128)S(1)}, f32[1,24,3072]{2,1,0:T(8,128)}, u32[]{:S(2)}) copy-start(f32[1,24,3072]{2,1,0:T(8,128)} %param.27) | copy-start | bytes 884740
  27.1 6.2 %copy-start.5 = (f32[1,24,3072]{2,1,0:T(8,128)S(1)}, f32[1,24,3072]{2,1,0:T(8,128)}, u32[]{:S(2)}) copy-start(f32[1,24,3072]{2,1,0:T(8,128)} %param.19) | copy-start | bytes 884740
  31.2 3.3 %copy-start.9 = (f32[1,4,24,768]{3,2,1,0:T(8,128)S(1)}, f32[1,4,24,768]{3,2,1,0:T(8,128)}, u32[]{:S(2)}) copy-start(f32[1,4,24,768]{3,2,1,0:T(8,128)} %param.26) | copy-start | bytes 884740
  31.2 3.3 %copy-start.10 = (f32[4,24,768]{2,1,0:T(8,128)S(1)}, f32[4,24,768]{2,1,0:T(8,128)}, u32[]{:S(2)}) copy-start(f32[4,24,768]{2,1,0:T(8,128)} %param.22) | copy-start | bytes 884740
  31.2 3.3 %copy-start.11 = (f32[1,4,24,768]{3,2,1,0:T(8,128)S(1)}, f32[1,4,24,768]{3,2,1,0:T(8,128)}, u32[]{:S(2)}) copy-start(f32[1,4,24,768]{3,2,1,0:T(8,128)} %param.18) | copy-start | bytes 884740
  31.3 3.3 %copy-start.15 = (f32[4,24,64]{2,1,0:T(8,128)S(1)}, f32[4,24,64]{2,1,0:T(8,128)}, u32[]{:S(2)}) copy-start(f32[4,24,64]{2,1,0:T(8,128)} %copy-done.14) | copy-start | bytes 73732
  31.3 4.5 %copy-start.18 = (f32[4,24]{1,0:T(4,128)S(1)}, f32[4,24]{1,0:T(4,128)}, u32[]{:S(2)}) copy-start(f32[4,24]{1,0:T(4,128)} %reshape.82) | copy-start | bytes 1156
  31.3 4.5 %copy-start.20 = (f32[4,24]{1,0:T(4,128)S(1)}, f32[4,24]{1,0:T(4,128)}, u32[]{:S(2)}) copy-start(f32[4,24]{1,0:T(4,128)} %param.32) | copy-start | bytes 1156
  33.3 30.2 %copy-start.12 = (f32[12,24,768]{2,1,0:T(8,128)S(1)}, f32[12,24,768]{2,1,0:T(8,128)}, u32[]{:S(2)}) copy-start(f32[12,24,768]{2,1,0:T(8,128)} %get-tuple-element.24) | copy-start | bytes 2654212
Sparse Core Ops, SparseCore 0:
  31.3 68.9 all-gather.2
